TPU v7x, 1024 devices: a whole 8x8x8 slice. The times are simulated.
1024 devices in a mesh: comp: 16 (over z, y_lo), tile: 64 (over y_hi, x, core).
Axes of the slice: x: 8, y: 8 (y_hi: 4, y_lo: 2; y = y_hi * 2 + y_lo), z: 8, core: 2. Of those that a mesh axis runs over, the one named last changes fastest.
Arguments:
- atm_state: float32 [72, 128, 8192], P(None, 'comp', 'tile'), may hold values from -6 to 6
- kappa: float32 [128, 8192], P('comp', 'tile'), may hold values from 0.02 to 0.2
- vert_mix: float32 [72, 72], replicated, may hold values from -0.375 to 0.375
- flux_proj: float32 [24, 72], replicated, may hold values from -0.75 to 0.75
- remap_weight: bfloat16 [32768, 4, 64, 64], P(('comp', 'tile')), may hold values from -0.375 to 0.375
- remap_cols: int32 [32768, 4], P(('comp', 'tile')), may hold values from 0 to 1023, as said below
- ocean_state: float32 [80, 2097152], P(None, ('comp', 'tile')), may hold values from -6 to 6
- ocean_mix: float32 [80, 80], replicated, may hold values from -0.3125 to 0.3125
- forcing: float32 [80, 24], replicated, may hold values from -1.25 to 1.25
- wet_mask: int32 [2097152], P(('comp', 'tile')), may hold values 0 or 1
- surface_proj: float32 [8, 80], replicated, may hold values from -0.625 to 0.625
- back_weight: bfloat16 [16384, 4, 64, 64], P(('comp', 'tile')), may hold values from -0.375 to 0.375
- back_cols: int32 [16384, 4], P(('comp', 'tile')), may hold values from 0 to 2047, as said below
- back_proj: float32 [72, 8], replicated, may hold values from -2 to 2
Outputs:
- atm_out: float32 [72, 128, 8192], P(None, 'comp', 'tile')
- ocean_out: float32 [80, 2097152], P(None, ('comp', 'tile'))
Inputs may be any that keep to these rules, and one draw needn't show every extreme that they name: Indices count the atmosphere blocks of the ocean block's own comp group; the tile of each index, remap_cols // 16, lies within 2 tiles, cyclically over 64 tiles, of the ocean block's own tile (r % 2048) // 32. Indices count the ocean blocks of the atmosphere block's own comp group; the tile of each index, back_cols // 32, lies within 2 tiles, cyclically over 64 tiles, of the atmosphere block's own tile (a % 1024) // 16.
All inputs are finite; a program needn't handle non-finite values. No bound on the sum of `wet_mask` on one device may be relied on, other than what follows from the above.
Results may differ from a plain program's by a relative error of at most 0.0029.
Values may be sent and summed in bfloat16 or wider, within the bound.
No kernel may reach another device: no remote copies, remote signals or barrier semaphores. Data moves between devices by JAX's collectives and lax.ppermute only.
A program may use at most 32 MiB of HBM per device.

v0:
```python
import jax
import jax.numpy as jnp
from jax import lax
from jax.sharding import PartitionSpec as P


def padded_2(cells, sides, width):
    for axis, dim in sides:
        count = lax.axis_size(axis)
        head = lax.slice_in_dim(cells, 0, width, axis=dim)
        tail = lax.slice_in_dim(cells, cells.shape[dim] - width, cells.shape[dim], axis=dim)
        cells = jnp.concatenate(
            [
                lax.ppermute(tail, axis, [(i, (i + 1) % count) for i in range(count)]),
                cells,
                lax.ppermute(head, axis, [((i + 1) % count, i) for i in range(count)]),
            ],
            axis=dim,
        )
    return cells


def from_behind(value, axis, steps):
    count = lax.axis_size(axis)
    pairs = [(source, (source + steps) % count) for source in range(count)]
    return lax.ppermute(value, axis, pairs)


def level_mix(matrix, field):
    flat = field.reshape(field.shape[0], -1)
    return jnp.dot(matrix, flat, precision=lax.Precision.HIGHEST).reshape(
        (matrix.shape[0],) + field.shape[1:]
    )


def inner_step(padded, coeff, vert_mix):
    center = padded[:, 1:-1, 1:-1]
    beside_all = (
        padded[:, 2:, 1:-1] + padded[:, :-2, 1:-1] + padded[:, 1:-1, 2:] + padded[:, 1:-1, :-2]
    )
    return (
        center + coeff[None, 1:-1, 1:-1] * (beside_all - 4.0 * center) + level_mix(vert_mix, center)
    )


def block_product(weights, picked):
    return jnp.einsum("okij,fokj->foi", weights, picked, preferred_element_type=jnp.float32)


def near_index(cols, per_tile, tiles, here):
    relative = (cols // per_tile - here + 2) % tiles
    return relative * per_tile + cols % per_tile


def body(
    atm_state,
    kappa,
    vert_mix,
    flux_proj,
    remap_weight,
    remap_cols,
    ocean_state,
    ocean_mix,
    forcing,
    wet_mask,
    surface_proj,
    back_weight,
    back_cols,
    back_proj,
):
    levels, rows_here, cols_here = atm_state.shape
    padded_coeff = jnp.pad(kappa, 1)
    atm_mid = atm_state
    for turn in range(2):
        padded = padded_2(atm_mid, (("comp", 1), ("tile", 2)), 1)
        atm_mid = inner_step(padded, padded_coeff, vert_mix)
    surface = level_mix(flux_proj, atm_mid).astype(jnp.bfloat16)
    fields = surface.shape[0]
    atm_blocks = rows_here * cols_here // 64
    surface_blocks = surface.reshape(fields, atm_blocks, 64)
    ocean_blocks = remap_weight.shape[0]
    tiles = lax.axis_size("tile")
    here = lax.axis_index("tile")
    pieces = []
    for offset in (-2, -1, 0, 1, 2):
        if offset == 0:
            pieces.append(surface_blocks)
        else:
            pieces.append(from_behind(surface_blocks, "tile", -offset))
    nearby = jnp.concatenate(pieces, 1)
    local = near_index(remap_cols, atm_blocks, tiles, here)
    remapped = block_product(remap_weight, nearby[:, local])
    remapped = remapped.reshape(fields, ocean_blocks * 64)
    stepped = (
        ocean_state
        + jnp.dot(ocean_mix, ocean_state, precision=lax.Precision.HIGHEST)
        + jnp.dot(forcing, remapped, precision=lax.Precision.HIGHEST)
    )
    ocean_out = jnp.where(wet_mask[None] == 1, stepped, ocean_state)
    sea = jnp.dot(surface_proj, ocean_out, precision=lax.Precision.HIGHEST).astype(jnp.bfloat16)
    sea_blocks = sea.reshape(sea.shape[0], ocean_blocks, 64)
    sea_pieces = []
    for offset in (-2, -1, 0, 1, 2):
        if offset == 0:
            sea_pieces.append(sea_blocks)
        else:
            sea_pieces.append(from_behind(sea_blocks, "tile", -offset))
    sea_nearby = jnp.concatenate(sea_pieces, 1)
    back_local = near_index(back_cols, ocean_blocks, tiles, here)
    returned = block_product(back_weight, sea_nearby[:, back_local])
    returned = returned.reshape(sea.shape[0], rows_here, cols_here)
    atm_out = atm_mid + level_mix(back_proj, returned)
    return (atm_out, ocean_out)


def solution(mesh):
    return jax.shard_map(
        body,
        mesh=mesh,
        in_specs=(
            P(None, "comp", "tile"),
            P("comp", "tile"),
            P(),
            P(),
            P(("comp", "tile"), None, None, None),
            P(("comp", "tile"), None),
            P(None, ("comp", "tile")),
            P(),
            P(),
            P(("comp", "tile")),
            P(),
            P(("comp", "tile"), None, None, None),
            P(("comp", "tile"), None),
            P(),
        ),
        out_specs=(P(None, "comp", "tile"), P(None, ("comp", "tile"))),
        check_vma=False,
    )
```

profile of v0, /device:TPU:1, one launch (start us, length us, event | category | flops | bytes accessed | tf_op | source)
XLA Modules:
  0.0 125.4 jit_solution(1168586196102954136)
XLA Ops:
  0.7 1.2 copy.34
  1.9 4.1 %collective-permute-start.1 = (f32[72,1,128]{2,0,1:T(8,128)S(1)}, f32[72,1,128]{2,0,1:T(8,128)S(1)}, u32[]{:S(2)}, u32[]{:S(2)}) collective-permute-start(f32[72,1,128]{2,0,1:T(8,128)S(1)} %get-tuple-element.13), channel_id=1, source_target_pairs={{0,64},{64,128},{128,192},{192,256},{256,320},{320,384},{384,448},... | collective-permute-start | bytes 110600 | tf_op jit(solution)/shard_map/ppermute | solution.py:14
  6.0 16.8 %collective-permute-start = (f32[72,1,128]{2,0,1:T(8,128)S(1)}, f32[72,1,128]{2,0,1:T(8,128)S(1)}, u32[]{:S(2)}, u32[]{:S(2)}) collective-permute-start(f32[72,1,128]{2,0,1:T(8,128)S(1)} %get-tuple-element.12), channel_id=1, source_target_pairs={{64,0},{128,64},{192,128},{256,192},{320,256},{384,320},{448,384},... | collective-permute-start | bytes 110600 | tf_op jit(solution)/shard_map/ppermute | solution.py:16
  22.8 0.7 broadcast_compare_fusion
  23.5 1.0 constant_dynamic-update-slice_fusion.1
  24.7 3.1 %collective-permute-start.2 = (f32[72,10,1]{2,0,1:T(8,128)S(1)}, f32[72,10,1]{2,0,1:T(8,128)S(1)}, u32[]{:S(2)}, u32[]{:S(2)}) collective-permute-start(f32[72,10,1]{2,0,1:T(8,128)S(1)} %get-tuple-element.8), channel_id=1, source_target_pairs={{1,0},{2,1},{3,2},{4,3},{5,4},{6,5},{7,6},{8,7},{9,8},{10,9},{11,1... | collective-permute-start | bytes 8648 | tf_op jit(solution)/shard_map/ppermute | solution.py:16
  27.9 2.8 %collective-permute-start.3 = (f32[72,10,1]{2,0,1:T(8,128)S(1)}, f32[72,10,1]{2,0,1:T(8,128)S(1)}, u32[]{:S(2)}, u32[]{:S(2)}) collective-permute-start(f32[72,10,1]{2,0,1:T(8,128)S(1)} %get-tuple-element.9), channel_id=1, source_target_pairs={{0,1},{1,2},{2,3},{3,4},{4,5},{5,6},{6,7},{7,8},{8,9},{9,10},{10,1... | collective-permute-start | bytes 8648 | tf_op jit(solution)/shard_map/ppermute | solution.py:14
  30.7 3.2 %collective-permute-done.2 = f32[72,10,1]{2,0,1:T(8,128)S(1)} collective-permute-done((f32[72,10,1]{2,0,1:T(8,128)S(1)}, f32[72,10,1]{2,0,1:T(8,128)S(1)}, u32[]{:S(2)}, u32[]{:S(2)}) %collective-permute-start.2) | collective-permute-done | bytes 2912 | tf_op jit(solution)/shard_map/ppermute | solution.py:16
  33.9 2.3 %collective-permute-done.3 = f32[72,10,1]{2,0,1:T(8,128)S(1)} collective-permute-done((f32[72,10,1]{2,0,1:T(8,128)S(1)}, f32[72,10,1]{2,0,1:T(8,128)S(1)}, u32[]{:S(2)}, u32[]{:S(2)}) %collective-permute-start.3) | collective-permute-done | bytes 2912 | tf_op jit(solution)/shard_map/ppermute | solution.py:14
  36.7 5.0 %collective-permute-start.4 = (f32[72,1,128]{2,0,1:T(8,128)S(1)}, f32[72,1,128]{2,0,1:T(8,128)S(1)}, u32[]{:S(2)}, u32[]{:S(2)}) collective-permute-start(f32[72,1,128]{2,0,1:T(8,128)S(1)} %get-tuple-element.11), channel_id=1, source_target_pairs={{64,0},{128,64},{192,128},{256,192},{320,256},{384,320},{448,384},... | collective-permute-start | bytes 110600 | tf_op jit(solution)/shard_map/ppermute | solution.py:16
  41.8 1.9 %collective-permute-start.5 = (f32[72,1,128]{2,0,1:T(8,128)S(1)}, f32[72,1,128]{2,0,1:T(8,128)S(1)}, u32[]{:S(2)}, u32[]{:S(2)}) collective-permute-start(f32[72,1,128]{2,0,1:T(8,128)S(1)} %get-tuple-element.10), channel_id=1, source_target_pairs={{0,64},{64,128},{128,192},{192,256},{256,320},{320,384},{384,448},... | collective-permute-start | bytes 110600 | tf_op jit(solution)/shard_map/ppermute | solution.py:14
  43.9 4.6 %collective-permute-done.5 = f32[72,1,128]{2,0,1:T(8,128)S(1)} collective-permute-done((f32[72,1,128]{2,0,1:T(8,128)S(1)}, f32[72,1,128]{2,0,1:T(8,128)S(1)}, u32[]{:S(2)}, u32[]{:S(2)}) %collective-permute-start.5) | collective-permute-done | bytes 36896 | tf_op jit(solution)/shard_map/ppermute | solution.py:14
  48.8 16.8 %collective-permute-start.6 = (f32[72,10,1]{2,0,1:T(8,128)S(1)}, f32[72,10,1]{2,0,1:T(8,128)S(1)}, u32[]{:S(2)}, u32[]{:S(2)}) collective-permute-start(f32[72,10,1]{2,0,1:T(8,128)S(1)} %get-tuple-element.6), channel_id=1, source_target_pairs={{1,0},{2,1},{3,2},{4,3},{5,4},{6,5},{7,6},{8,7},{9,8},{10,9},{11,1... | collective-permute-start | bytes 8648 | tf_op jit(solution)/shard_map/ppermute | solution.py:16
  65.5 1.9 %collective-permute-start.7 = (f32[72,10,1]{2,0,1:T(8,128)S(1)}, f32[72,10,1]{2,0,1:T(8,128)S(1)}, u32[]{:S(2)}, u32[]{:S(2)}) collective-permute-start(f32[72,10,1]{2,0,1:T(8,128)S(1)} %get-tuple-element.7), channel_id=1, source_target_pairs={{0,1},{1,2},{2,3},{3,4},{4,5},{5,6},{6,7},{7,8},{8,9},{9,10},{10,1... | collective-permute-start | bytes 8648 | tf_op jit(solution)/shard_map/ppermute | solution.py:14
  67.9 4.0 %collective-permute-done.7 = f32[72,10,1]{2,0,1:T(8,128)S(1)} collective-permute-done((f32[72,10,1]{2,0,1:T(8,128)S(1)}, f32[72,10,1]{2,0,1:T(8,128)S(1)}, u32[]{:S(2)}, u32[]{:S(2)}) %collective-permute-start.7) | collective-permute-done | bytes 2912 | tf_op jit(solution)/shard_map/ppermute | solution.py:14
  72.7 1.9 %collective-permute-start.8 = (bf16[24,16,64]{2,0,1:T(8,128)(2,1)S(1)}, bf16[24,16,64]{2,0,1:T(8,128)(2,1)S(1)}, u32[]{:S(2)}, u32[]{:S(2)}) collective-permute-start(bf16[24,16,64]{2,0,1:T(8,128)(2,1)S(1)} %copy.39), channel_id=1, source_target_pairs={{0,2},{1,3},{2,4},{3,5},{4,6},{5,7},{6,8},{7,9},{8,10},{9,11},{10,... | collective-permute-start | bytes 147464 | tf_op jit(solution)/shard_map/ppermute | solution.py:26
  74.8 4.4 %collective-permute-start.9 = (bf16[24,16,64]{2,0,1:T(8,128)(2,1)S(1)}, bf16[24,16,64]{2,0,1:T(8,128)(2,1)S(1)}, u32[]{:S(2)}, u32[]{:S(2)}) collective-permute-start(bf16[24,16,64]{2,0,1:T(8,128)(2,1)S(1)} %copy.39), channel_id=1, source_target_pairs={{0,1},{1,2},{2,3},{3,4},{4,5},{5,6},{6,7},{7,8},{8,9},{9,10},{10,1... | collective-permute-start | bytes 147464 | tf_op jit(solution)/shard_map/ppermute | solution.py:26
  79.2 8.1 %collective-permute-start.10 = (bf16[24,16,64]{2,0,1:T(8,128)(2,1)S(1)}, bf16[24,16,64]{2,0,1:T(8,128)(2,1)S(1)}, u32[]{:S(2)}, u32[]{:S(2)}) collective-permute-start(bf16[24,16,64]{2,0,1:T(8,128)(2,1)S(1)} %copy.39), channel_id=1, source_target_pairs={{0,63},{1,0},{2,1},{3,2},{4,3},{5,4},{6,5},{7,6},{8,7},{9,8},{10,9... | collective-permute-start | bytes 147464 | tf_op jit(solution)/shard_map/ppermute | solution.py:26
  87.3 7.9 %collective-permute-start.11 = (bf16[24,16,64]{2,0,1:T(8,128)(2,1)S(1)}, bf16[24,16,64]{2,0,1:T(8,128)(2,1)S(1)}, u32[]{:S(2)}, u32[]{:S(2)}) collective-permute-start(bf16[24,16,64]{2,0,1:T(8,128)(2,1)S(1)} %copy.39), channel_id=1, source_target_pairs={{0,62},{1,63},{2,0},{3,1},{4,2},{5,3},{6,4},{7,5},{8,6},{9,7},{10,... | collective-permute-start | bytes 147464 | tf_op jit(solution)/shard_map/ppermute | solution.py:26
  95.2 0.7 constant_dynamic-update-slice_fusion.7
  95.8 0.7 constant_dynamic-update-slice_fusion.6
  96.5 0.7 constant_dynamic-update-slice_fusion.5
  98.5 1.8 %gather_fusion = bf16[128,24,64]{2,1,0:T(8,128)(2,1)S(1)} fusion(bf16[24,80,64]{2,0,1:T(8,128)(2,1)} %constant_dynamic-update-slice_fusion.3, s32[1024]{0:T(1024)S(1)} %pad_clamp_fusion.1), kind=kCustom, calls=%fused_computation | custom fusion | bytes 786944 | tf_op jit(solution)/shard_map/gather | solution.py:92
  101.2 0.7 convolution_bitcast_fusion
  101.9 2.0 %fusion.1 = f32[80,2048]{1,0:T(8,128)S(1)} fusion(f32[80,2048]{1,0:T(8,128)} %param.20, f32[80,2048]{1,0:T(8,128)S(1)} %convolution_bitcast_fusion, f32[80,80]{1,0:T(8,128)S(1)} %copy-done.4, pred[2048]{0:T(1024)(128)(4,1)S(1)} %broadcast_compare_fusion), kind=kOutput, calls=%fused_computation.4 | convolution fusion | flops 157777920 | bytes 1993728 | tf_op jit(solution)/shard_map/dot_general | solution.py:96
  104.6 1.9 %collective-permute-start.12 = (bf16[8,32,64]{2,0,1:T(8,128)(2,1)S(1)}, bf16[8,32,64]{2,0,1:T(8,128)(2,1)S(1)}, u32[]{:S(2)}, u32[]{:S(2)}) collective-permute-start(bf16[8,32,64]{2,0,1:T(8,128)(2,1)S(1)} %copy.46), channel_id=1, source_target_pairs={{0,2},{1,3},{2,4},{3,5},{4,6},{5,7},{6,8},{7,9},{8,10},{9,11},{10,... | collective-permute-start | bytes 98312 | tf_op jit(solution)/shard_map/ppermute | solution.py:26
  106.5 3.5 %collective-permute-start.13 = (bf16[8,32,64]{2,0,1:T(8,128)(2,1)S(1)}, bf16[8,32,64]{2,0,1:T(8,128)(2,1)S(1)}, u32[]{:S(2)}, u32[]{:S(2)}) collective-permute-start(bf16[8,32,64]{2,0,1:T(8,128)(2,1)S(1)} %copy.46), channel_id=1, source_target_pairs={{0,1},{1,2},{2,3},{3,4},{4,5},{5,6},{6,7},{7,8},{8,9},{9,10},{10,1... | collective-permute-start | bytes 98312 | tf_op jit(solution)/shard_map/ppermute | solution.py:26
  110.1 2.3 %collective-permute-start.14 = (bf16[8,32,64]{2,0,1:T(8,128)(2,1)S(1)}, bf16[8,32,64]{2,0,1:T(8,128)(2,1)S(1)}, u32[]{:S(2)}, u32[]{:S(2)}) collective-permute-start(bf16[8,32,64]{2,0,1:T(8,128)(2,1)S(1)} %copy.46), channel_id=1, source_target_pairs={{0,63},{1,0},{2,1},{3,2},{4,3},{5,4},{6,5},{7,6},{8,7},{9,8},{10,9... | collective-permute-start | bytes 98312 | tf_op jit(solution)/shard_map/ppermute | solution.py:26
  112.4 8.1 %collective-permute-start.15 = (bf16[8,32,64]{2,0,1:T(8,128)(2,1)S(1)}, bf16[8,32,64]{2,0,1:T(8,128)(2,1)S(1)}, u32[]{:S(2)}, u32[]{:S(2)}) collective-permute-start(bf16[8,32,64]{2,0,1:T(8,128)(2,1)S(1)} %copy.46), channel_id=1, source_target_pairs={{0,62},{1,63},{2,0},{3,1},{4,2},{5,3},{6,4},{7,5},{8,6},{9,7},{10,... | collective-permute-start | bytes 98312 | tf_op jit(solution)/shard_map/ppermute | solution.py:26
  120.6 1.2 collective-permute-done.15
  122.4 1.6 %convolution_bitcast_fusion.4 = f32[8,16,64]{2,0,1:T(8,128)S(1)} fusion(bf16[8,16,4,64]{3,0,2,1:T(8,128)(2,1)S(1)} %bitcast.78, bf16[16,4,64,64]{3,2,1,0:T(8,128)(2,1)} %param.25), kind=kOutput, calls=%fused_computation.13 | convolution fusion | flops 4194304 | bytes 622592 | tf_op jit(solution)/shard_map/okij,fokj->foi/dot_general | solution.py:47
  124.6 0.8 copy.54
  (74 shorter events, 6.6 us)
Async XLA Ops:
  0.6 99.6 %copy-start = (bf16[32,4,64,64]{3,2,1,0:T(8,128)(2,1)S(1)}, bf16[32,4,64,64]{3,2,1,0:T(8,128)(2,1)}, u32[]{:S(2)}) copy-start(bf16[32,4,64,64]{3,2,1,0:T(8,128)(2,1)} %param.18) | copy-start | bytes 3145732
  0.6 35.6 %copy-start.1 = (f32[72,8,128]{2,1,0:T(8,128)S(1)}, f32[72,8,128]{2,1,0:T(8,128)}, u32[]{:S(2)}) copy-start(f32[72,8,128]{2,1,0:T(8,128)} %param.14) | copy-start | bytes 884740
  0.7 30.0 %copy-start.10 = (s32[32,4]{0,1:T(4,128)S(1)}, s32[32,4]{0,1:T(4,128)}, u32[]{:S(2)}) copy-start(s32[32,4]{0,1:T(4,128)} %param.19) | copy-start | bytes 1540
  0.7 35.5 %copy-start.5 = (f32[8,128]{1,0:T(8,128)S(1)}, f32[8,128]{1,0:T(8,128)}, u32[]{:S(2)}) copy-start(f32[8,128]{1,0:T(8,128)} %param.15) | copy-start | bytes 12292
  0.7 35.5 %copy-start.3 = (f32[72,72]{1,0:T(8,128)S(1)}, f32[72,72]{1,0:T(8,128)}, u32[]{:S(2)}) copy-start(f32[72,72]{1,0:T(8,128)} %param.16) | copy-start | bytes 62212
  1.9 21.6 %collective-permute-start.1 = (f32[72,1,128]{2,0,1:T(8,128)S(1)}, f32[72,1,128]{2,0,1:T(8,128)S(1)}, u32[]{:S(2)}, u32[]{:S(2)}) collective-permute-start(f32[72,1,128]{2,0,1:T(8,128)S(1)} %get-tuple-element.13), channel_id=1, source_target_pairs={{0,64},{64,128},{128,192},{192,256},{256,320},{320,384},{384,448},... | collective-permute-start | bytes 110600 | tf_op jit(solution)/shard_map/ppermute | solution.py:14
  6.0 18.5 %collective-permute-start = (f32[72,1,128]{2,0,1:T(8,128)S(1)}, f32[72,1,128]{2,0,1:T(8,128)S(1)}, u32[]{:S(2)}, u32[]{:S(2)}) collective-permute-start(f32[72,1,128]{2,0,1:T(8,128)S(1)} %get-tuple-element.12), channel_id=1, source_target_pairs={{64,0},{128,64},{192,128},{256,192},{320,256},{384,320},{448,384},... | collective-permute-start | bytes 110600 | tf_op jit(solution)/shard_map/ppermute | solution.py:16
  23.5 20.2 %copy-start.11 = (s32[16,4]{0,1:T(4,128)S(1)}, s32[16,4]{0,1:T(4,128)}, u32[]{:S(2)}) copy-start(s32[16,4]{0,1:T(4,128)} %param.26) | copy-start | bytes 772
  24.7 9.1 %collective-permute-start.2 = (f32[72,10,1]{2,0,1:T(8,128)S(1)}, f32[72,10,1]{2,0,1:T(8,128)S(1)}, u32[]{:S(2)}, u32[]{:S(2)}) collective-permute-start(f32[72,10,1]{2,0,1:T(8,128)S(1)} %get-tuple-element.8), channel_id=1, source_target_pairs={{1,0},{2,1},{3,2},{4,3},{5,4},{6,5},{7,6},{8,7},{9,8},{10,9},{11,1... | collective-permute-start | bytes 8648 | tf_op jit(solution)/shard_map/ppermute | solution.py:16
  27.9 8.3 %collective-permute-start.3 = (f32[72,10,1]{2,0,1:T(8,128)S(1)}, f32[72,10,1]{2,0,1:T(8,128)S(1)}, u32[]{:S(2)}, u32[]{:S(2)}) collective-permute-start(f32[72,10,1]{2,0,1:T(8,128)S(1)} %get-tuple-element.9), channel_id=1, source_target_pairs={{0,1},{1,2},{2,3},{3,4},{4,5},{5,6},{6,7},{7,8},{8,9},{9,10},{10,1... | collective-permute-start | bytes 8648 | tf_op jit(solution)/shard_map/ppermute | solution.py:14
  36.7 7.2 %collective-permute-start.4 = (f32[72,1,128]{2,0,1:T(8,128)S(1)}, f32[72,1,128]{2,0,1:T(8,128)S(1)}, u32[]{:S(2)}, u32[]{:S(2)}) collective-permute-start(f32[72,1,128]{2,0,1:T(8,128)S(1)} %get-tuple-element.11), channel_id=1, source_target_pairs={{64,0},{128,64},{192,128},{256,192},{320,256},{384,320},{448,384},... | collective-permute-start | bytes 110600 | tf_op jit(solution)/shard_map/ppermute | solution.py:16
  41.8 6.8 %collective-permute-start.5 = (f32[72,1,128]{2,0,1:T(8,128)S(1)}, f32[72,1,128]{2,0,1:T(8,128)S(1)}, u32[]{:S(2)}, u32[]{:S(2)}) collective-permute-start(f32[72,1,128]{2,0,1:T(8,128)S(1)} %get-tuple-element.10), channel_id=1, source_target_pairs={{0,64},{64,128},{128,192},{192,256},{256,320},{320,384},{384,448},... | collective-permute-start | bytes 110600 | tf_op jit(solution)/shard_map/ppermute | solution.py:14
  43.9 28.3 %copy-start.6 = (f32[24,72]{1,0:T(8,128)S(1)}, f32[24,72]{1,0:T(8,128)}, u32[]{:S(2)}) copy-start(f32[24,72]{1,0:T(8,128)} %param.17) | copy-start | bytes 20740
  48.8 19.1 %collective-permute-start.6 = (f32[72,10,1]{2,0,1:T(8,128)S(1)}, f32[72,10,1]{2,0,1:T(8,128)S(1)}, u32[]{:S(2)}, u32[]{:S(2)}) collective-permute-start(f32[72,10,1]{2,0,1:T(8,128)S(1)} %get-tuple-element.6), channel_id=1, source_target_pairs={{1,0},{2,1},{3,2},{4,3},{5,4},{6,5},{7,6},{8,7},{9,8},{10,9},{11,1... | collective-permute-start | bytes 8648 | tf_op jit(solution)/shard_map/ppermute | solution.py:16
  65.5 6.4 %collective-permute-start.7 = (f32[72,10,1]{2,0,1:T(8,128)S(1)}, f32[72,10,1]{2,0,1:T(8,128)S(1)}, u32[]{:S(2)}, u32[]{:S(2)}) collective-permute-start(f32[72,10,1]{2,0,1:T(8,128)S(1)} %get-tuple-element.7), channel_id=1, source_target_pairs={{0,1},{1,2},{2,3},{3,4},{4,5},{5,6},{6,7},{7,8},{8,9},{9,10},{10,1... | collective-permute-start | bytes 8648 | tf_op jit(solution)/shard_map/ppermute | solution.py:14
  72.7 22.5 %collective-permute-start.8 = (bf16[24,16,64]{2,0,1:T(8,128)(2,1)S(1)}, bf16[24,16,64]{2,0,1:T(8,128)(2,1)S(1)}, u32[]{:S(2)}, u32[]{:S(2)}) collective-permute-start(bf16[24,16,64]{2,0,1:T(8,128)(2,1)S(1)} %copy.39), channel_id=1, source_target_pairs={{0,2},{1,3},{2,4},{3,5},{4,6},{5,7},{6,8},{7,9},{8,10},{9,11},{10,... | collective-permute-start | bytes 147464 | tf_op jit(solution)/shard_map/ppermute | solution.py:26
  74.8 21.0 %collective-permute-start.9 = (bf16[24,16,64]{2,0,1:T(8,128)(2,1)S(1)}, bf16[24,16,64]{2,0,1:T(8,128)(2,1)S(1)}, u32[]{:S(2)}, u32[]{:S(2)}) collective-permute-start(bf16[24,16,64]{2,0,1:T(8,128)(2,1)S(1)} %copy.39), channel_id=1, source_target_pairs={{0,1},{1,2},{2,3},{3,4},{4,5},{5,6},{6,7},{7,8},{8,9},{9,10},{10,1... | collective-permute-start | bytes 147464 | tf_op jit(solution)/shard_map/ppermute | solution.py:26
  79.2 18.0 %collective-permute-start.10 = (bf16[24,16,64]{2,0,1:T(8,128)(2,1)S(1)}, bf16[24,16,64]{2,0,1:T(8,128)(2,1)S(1)}, u32[]{:S(2)}, u32[]{:S(2)}) collective-permute-start(bf16[24,16,64]{2,0,1:T(8,128)(2,1)S(1)} %copy.39), channel_id=1, source_target_pairs={{0,63},{1,0},{2,1},{3,2},{4,3},{5,4},{6,5},{7,6},{8,7},{9,8},{10,9... | collective-permute-start | bytes 147464 | tf_op jit(solution)/shard_map/ppermute | solution.py:26
  87.3 10.5 %collective-permute-start.11 = (bf16[24,16,64]{2,0,1:T(8,128)(2,1)S(1)}, bf16[24,16,64]{2,0,1:T(8,128)(2,1)S(1)}, u32[]{:S(2)}, u32[]{:S(2)}) collective-permute-start(bf16[24,16,64]{2,0,1:T(8,128)(2,1)S(1)} %copy.39), channel_id=1, source_target_pairs={{0,62},{1,63},{2,0},{3,1},{4,2},{5,3},{6,4},{7,5},{8,6},{9,7},{10,... | collective-permute-start | bytes 147464 | tf_op jit(solution)/shard_map/ppermute | solution.py:26
  100.3 0.9 copy-start.7
  100.3 1.6 %copy-start.4 = (f32[80,80]{1,0:T(8,128)S(1)}, f32[80,80]{1,0:T(8,128)}, u32[]{:S(2)}) copy-start(f32[80,80]{1,0:T(8,128)} %param.21) | copy-start | bytes 76804
  100.9 3.0 %copy-start.8 = (f32[8,80]{1,0:T(8,128)S(1)}, f32[8,80]{1,0:T(8,128)}, u32[]{:S(2)}) copy-start(f32[8,80]{1,0:T(8,128)} %param.24) | copy-start | bytes 7684
  103.9 20.7 %copy-start.2 = (f32[80,2048]{1,0:T(8,128)}, f32[80,2048]{1,0:T(8,128)S(1)}, u32[]{:S(2)}) copy-start(f32[80,2048]{1,0:T(8,128)S(1)} %fusion.1) | copy-start | bytes 1966084
  103.9 20.2 %copy-start.9 = (f32[72,8]{0,1:T(8,128)S(1)}, f32[72,8]{0,1:T(8,128)}, u32[]{:S(2)}) copy-start(f32[72,8]{0,1:T(8,128)} %param.27) | copy-start | bytes 6916
  104.6 15.9 %collective-permute-start.12 = (bf16[8,32,64]{2,0,1:T(8,128)(2,1)S(1)}, bf16[8,32,64]{2,0,1:T(8,128)(2,1)S(1)}, u32[]{:S(2)}, u32[]{:S(2)}) collective-permute-start(bf16[8,32,64]{2,0,1:T(8,128)(2,1)S(1)} %copy.46), channel_id=1, source_target_pairs={{0,2},{1,3},{2,4},{3,5},{4,6},{5,7},{6,8},{7,9},{8,10},{9,11},{10,... | collective-permute-start | bytes 98312 | tf_op jit(solution)/shard_map/ppermute | solution.py:26
  106.5 14.0 %collective-permute-start.13 = (bf16[8,32,64]{2,0,1:T(8,128)(2,1)S(1)}, bf16[8,32,64]{2,0,1:T(8,128)(2,1)S(1)}, u32[]{:S(2)}, u32[]{:S(2)}) collective-permute-start(bf16[8,32,64]{2,0,1:T(8,128)(2,1)S(1)} %copy.46), channel_id=1, source_target_pairs={{0,1},{1,2},{2,3},{3,4},{4,5},{5,6},{6,7},{7,8},{8,9},{9,10},{10,1... | collective-permute-start | bytes 98312 | tf_op jit(solution)/shard_map/ppermute | solution.py:26
  110.1 10.5 %collective-permute-start.14 = (bf16[8,32,64]{2,0,1:T(8,128)(2,1)S(1)}, bf16[8,32,64]{2,0,1:T(8,128)(2,1)S(1)}, u32[]{:S(2)}, u32[]{:S(2)}) collective-permute-start(bf16[8,32,64]{2,0,1:T(8,128)(2,1)S(1)} %copy.46), channel_id=1, source_target_pairs={{0,63},{1,0},{2,1},{3,2},{4,3},{5,4},{6,5},{7,6},{8,7},{9,8},{10,9... | collective-permute-start | bytes 98312 | tf_op jit(solution)/shard_map/ppermute | solution.py:26
  112.4 9.4 %collective-permute-start.15 = (bf16[8,32,64]{2,0,1:T(8,128)(2,1)S(1)}, bf16[8,32,64]{2,0,1:T(8,128)(2,1)S(1)}, u32[]{:S(2)}, u32[]{:S(2)}) collective-permute-start(bf16[8,32,64]{2,0,1:T(8,128)(2,1)S(1)} %copy.46), channel_id=1, source_target_pairs={{0,62},{1,63},{2,0},{3,1},{4,2},{5,3},{6,4},{7,5},{8,6},{9,7},{10,... | collective-permute-start | bytes 98312 | tf_op jit(solution)/shard_map/ppermute | solution.py:26
where the time goes:
time: 127 us; the launch traced here: 125 us
  starting transfers between devices  90.5 us (71%)
  waiting for transfers between devices  15.4 us (12%)
  local copies, waits for them, and re-layouts  10.2 us (8%)
  matrix products  6.96 us (5%)
    ppermute x4, starting transfers between devices, padded_2(): lax.ppermute(head, axis, [((i + 1) % count, i) for i in range(count)])  41.7 us
    ppermute x8, starting transfers between devices, from_behind(): return lax.ppermute(value, axis, pairs)  38.1 us
    ppermute x4, waiting for transfers between devices, padded_2(): lax.ppermute(tail, axis, [(i, (i + 1) % count) for i in range(count)])  11 us
    ppermute x4, starting transfers between devices, padded_2(): lax.ppermute(tail, axis, [(i, (i + 1) % count) for i in range(count)])  10.8 us
    unnamed x36, local copies, waits for them, and re-layouts  5.72 us
    ppermute x4, waiting for transfers between devices, padded_2(): lax.ppermute(head, axis, [((i + 1) % count, i) for i in range(count)])  3.23 us
  transfers between devices with their start and end apart: 16, of which 5 were waited for; matrix products, arithmetic and copies ran while one was open for 4% of the time, Pallas kernels for 0%

commit v1 on v0

--- a/solution.py
+++ b/solution.py
@@ -2,22 +2,6 @@
 import jax.numpy as jnp
 from jax import lax
 from jax.sharding import PartitionSpec as P
-
-
-def padded_2(cells, sides, width):
-    for axis, dim in sides:
-        count = lax.axis_size(axis)
-        head = lax.slice_in_dim(cells, 0, width, axis=dim)
-        tail = lax.slice_in_dim(cells, cells.shape[dim] - width, cells.shape[dim], axis=dim)
-        cells = jnp.concatenate(
-            [
-                lax.ppermute(tail, axis, [(i, (i + 1) % count) for i in range(count)]),
-                cells,
-                lax.ppermute(head, axis, [((i + 1) % count, i) for i in range(count)]),
-            ],
-            axis=dim,
-        )
-    return cells
 
 
 def from_behind(value, axis, steps):
@@ -26,11 +10,26 @@
     return lax.ppermute(value, axis, pairs)
 
 
+def halo_cols(cells, width):
+    levels, rows, cols = cells.shape
+    head = cells[:, :, :width].reshape(-1)
+    tail = cells[:, :, cols - width:].reshape(-1)
+    left = from_behind(tail, "tile", 1).reshape(levels, rows, width)
+    right = from_behind(head, "tile", -1).reshape(levels, rows, width)
+    return jnp.concatenate([left, cells, right], axis=2)
+
+
+def halo_rows(cells, width):
+    levels, rows, cols = cells.shape
+    head = cells[:, :width, :]
+    tail = cells[:, rows - width:, :]
+    up = from_behind(tail, "comp", 1)
+    down = from_behind(head, "comp", -1)
+    return jnp.concatenate([up, cells, down], axis=1)
+
+
 def level_mix(matrix, field):
-    flat = field.reshape(field.shape[0], -1)
-    return jnp.dot(matrix, flat, precision=lax.Precision.HIGHEST).reshape(
-        (matrix.shape[0],) + field.shape[1:]
-    )
+    return jnp.einsum("ml,l...->m...", matrix, field, precision=lax.Precision.HIGHEST)
 
 
 def inner_step(padded, coeff, vert_mix):
@@ -38,9 +37,7 @@
     beside_all = (
         padded[:, 2:, 1:-1] + padded[:, :-2, 1:-1] + padded[:, 1:-1, 2:] + padded[:, 1:-1, :-2]
     )
-    return (
-        center + coeff[None, 1:-1, 1:-1] * (beside_all - 4.0 * center) + level_mix(vert_mix, center)
-    )
+    return center + coeff[None] * (beside_all - 4.0 * center) + level_mix(vert_mix, center)
 
 
 def block_product(weights, picked):
@@ -69,11 +66,12 @@
     back_proj,
 ):
     levels, rows_here, cols_here = atm_state.shape
-    padded_coeff = jnp.pad(kappa, 1)
-    atm_mid = atm_state
-    for turn in range(2):
-        padded = padded_2(atm_mid, (("comp", 1), ("tile", 2)), 1)
-        atm_mid = inner_step(padded, padded_coeff, vert_mix)
+    joined = jnp.concatenate([atm_state, kappa[None]], axis=0)
+    padded = halo_rows(halo_cols(joined, 2), 2)
+    field = padded[:levels]
+    coeff = padded[levels]
+    first = inner_step(field, coeff[1:-1, 1:-1], vert_mix)
+    atm_mid = inner_step(first, coeff[2:-2, 2:-2], vert_mix)
     surface = level_mix(flux_proj, atm_mid).astype(jnp.bfloat16)
     fields = surface.shape[0]
     atm_blocks = rows_here * cols_here // 64

time: 127 us -> 106 us (0.83)
  the two profiles are of different devices: /device:TPU:1 before, /device:TPU:64 now
where the time goes in v1:
time: 106 us; the launch traced here: 105 us
  starting transfers between devices  57.8 us (55%)
  waiting for transfers between devices  18.1 us (17%)
  local copies, waits for them, and re-layouts  17.6 us (17%)
  matrix products  9.54 us (9%)
  other arithmetic  1.23 us (1%)
  between operations  1.08 us (1%)
    ppermute x12, starting transfers between devices, from_behind(): return lax.ppermute(value, axis, pairs)  57.8 us
    ppermute x12, waiting for transfers between devices, from_behind(): return lax.ppermute(value, axis, pairs)  18.1 us
    unnamed x32, local copies, waits for them, and re-layouts  8.47 us
    dot_general x4, matrix products, level_mix(): jnp.einsum('ml,l...->m...', matrix, field, precision=lax.Precision.HIGHEST)  4.18 us
    dot_general x2, matrix products, block_product(): jnp.einsum('okij,fokj->foi', weights, picked, preferred_element_type=jnp....  2.22 us
  transfers between devices with their start and end apart: 12, of which 5 were waited for; matrix products, arithmetic and copies ran while one was open for 6% of the time, Pallas kernels for 0%

profile of v1, /device:TPU:64, one launch (start us, length us, event | category | flops | bytes accessed | tf_op | source)
XLA Modules:
  0.0 105.4 jit_solution(6683750374738226922)
XLA Ops:
  0.7 1.3 %copy.25 = f32[72,8,128]{0,2,1:T(8,128)S(1)} copy(f32[72,8,128]{2,1,0:T(8,128)} %param.14) | data formatting | bytes 589824 | tf_op args[0]
  2.0 0.9 copy.26
  3.4 1.9 %collective-permute-start = (f32[1168]{0:T(1024)S(1)}, f32[1168]{0:T(1024)S(1)}, u32[]{:S(2)}, u32[]{:S(2)}) collective-permute-start(f32[1168]{0:T(1024)S(1)} %reshape.32), channel_id=1, source_target_pairs={{0,1},{1,2},{2,3},{3,4},{4,5},{5,6},{6,7},{7,8},{8,9},{9,10},{10,1... | collective-permute-start | bytes 14024 | tf_op jit(solution)/shard_map/ppermute | solution.py:10
  5.8 7.9 %collective-permute-start.1 = (f32[1168]{0:T(1024)S(1)}, f32[1168]{0:T(1024)S(1)}, u32[]{:S(2)}, u32[]{:S(2)}) collective-permute-start(f32[1168]{0:T(1024)S(1)} %reshape.34), channel_id=1, source_target_pairs={{0,63},{1,0},{2,1},{3,2},{4,3},{5,4},{6,5},{7,6},{8,7},{9,8},{10,9... | collective-permute-start | bytes 14024 | tf_op jit(solution)/shard_map/ppermute | solution.py:10
  14.1 0.8 collective-permute-done.1
  15.4 0.9 pad_maximum_fusion.12
  16.3 2.7 %collective-permute-start.2 = (f32[73,2,132]{0,2,1:T(8,128)}, f32[73,2,132]{0,2,1:T(8,128)S(1)}, u32[]{:S(2)}, u32[]{:S(2)}) collective-permute-start(f32[73,2,132]{0,2,1:T(8,128)} %get-tuple-element.6), channel_id=1, source_target_pairs={{0,64},{64,128},{128,192},{192,256},{256,320},{320,384},{384,448},... | collective-permute-start | bytes 231272 | tf_op jit(solution)/shard_map/ppermute | solution.py:10
  19.0 16.8 %collective-permute-start.3 = (f32[73,2,132]{0,2,1:T(8,128)}, f32[73,2,132]{0,2,1:T(8,128)S(1)}, u32[]{:S(2)}, u32[]{:S(2)}) collective-permute-start(f32[73,2,132]{0,2,1:T(8,128)} %get-tuple-element.7), channel_id=1, source_target_pairs={{0,960},{64,0},{128,64},{192,128},{256,192},{320,256},{384,320},{4... | collective-permute-start | bytes 231272 | tf_op jit(solution)/shard_map/ppermute | solution.py:10
  36.0 2.2 %collective-permute-done.2 = f32[73,2,132]{0,2,1:T(8,128)S(1)} collective-permute-done((f32[73,2,132]{0,2,1:T(8,128)}, f32[73,2,132]{0,2,1:T(8,128)S(1)}, u32[]{:S(2)}, u32[]{:S(2)}) %collective-permute-start.2) | collective-permute-done | bytes 77120 | tf_op jit(solution)/shard_map/ppermute | solution.py:10
  38.9 0.7 slice_reduce_fusion
  39.8 1.1 %fusion.9 = f32[72,10,130]{0,2,1:T(8,128)S(1)} fusion(f32[73,12,132]{0,2,1:T(8,128)S(1)} %pad_maximum_fusion, f32[73,2,132]{0,2,1:T(8,128)S(1)} %collective-permute-done.2, f32[73,8,2]{0,2,1:T(2,128)S(1)} %copy.30, f32[73,8,2]{0,2,1:T(2,128)S(1)} %copy.29, f32[1,8,128]{0,2,1:T(8,128)S(1)} %copy.26, f32[72,8,128]{0,2,1:T(8,128)S(1)} %copy.25, ...), kind=kOutput, calls=%fused_computation.23 | convolution fusion | flops 82368000 | bytes 4556416 | tf_op jit(solution)/shard_map/ml,l...->m.../dot_general | solution.py:32
  40.8 0.7 fusion.4
  42.3 1.9 %collective-permute-start.4 = (bf16[24,16,64]{2,0,1:T(8,128)(2,1)S(1)}, bf16[24,16,64]{2,0,1:T(8,128)(2,1)S(1)}, u32[]{:S(2)}, u32[]{:S(2)}) collective-permute-start(bf16[24,16,64]{2,0,1:T(8,128)(2,1)S(1)} %copy.35), channel_id=1, source_target_pairs={{0,2},{1,3},{2,4},{3,5},{4,6},{5,7},{6,8},{7,9},{8,10},{9,11},{10,... | collective-permute-start | bytes 147464 | tf_op jit(solution)/shard_map/ppermute | solution.py:10
  44.4 7.0 %collective-permute-start.6 = (bf16[24,16,64]{2,0,1:T(8,128)(2,1)S(1)}, bf16[24,16,64]{2,0,1:T(8,128)(2,1)S(1)}, u32[]{:S(2)}, u32[]{:S(2)}) collective-permute-start(bf16[24,16,64]{2,0,1:T(8,128)(2,1)S(1)} %copy.35), channel_id=1, source_target_pairs={{0,63},{1,0},{2,1},{3,2},{4,3},{5,4},{6,5},{7,6},{8,7},{9,8},{10,9... | collective-permute-start | bytes 147464 | tf_op jit(solution)/shard_map/ppermute | solution.py:10
  51.4 3.6 %collective-permute-start.7 = (bf16[24,16,64]{2,0,1:T(8,128)(2,1)S(1)}, bf16[24,16,64]{2,0,1:T(8,128)(2,1)S(1)}, u32[]{:S(2)}, u32[]{:S(2)}) collective-permute-start(bf16[24,16,64]{2,0,1:T(8,128)(2,1)S(1)} %copy.35), channel_id=1, source_target_pairs={{0,62},{1,63},{2,0},{3,1},{4,2},{5,3},{6,4},{7,5},{8,6},{9,7},{10,... | collective-permute-start | bytes 147464 | tf_op jit(solution)/shard_map/ppermute | solution.py:10
  55.1 1.9 %collective-permute-start.5 = (bf16[24,16,64]{2,0,1:T(8,128)(2,1)S(1)}, bf16[24,16,64]{2,0,1:T(8,128)(2,1)S(1)}, u32[]{:S(2)}, u32[]{:S(2)}) collective-permute-start(bf16[24,16,64]{2,0,1:T(8,128)(2,1)S(1)} %copy.35), channel_id=1, source_target_pairs={{0,1},{1,2},{2,3},{3,4},{4,5},{5,6},{6,7},{7,8},{8,9},{9,10},{10,1... | collective-permute-start | bytes 147464 | tf_op jit(solution)/shard_map/ppermute | solution.py:10
  57.0 0.7 constant_dynamic-update-slice_fusion.4
  57.7 7.6 %collective-permute-done.5 = bf16[24,16,64]{2,0,1:T(8,128)(2,1)S(1)} collective-permute-done((bf16[24,16,64]{2,0,1:T(8,128)(2,1)S(1)}, bf16[24,16,64]{2,0,1:T(8,128)(2,1)S(1)}, u32[]{:S(2)}, u32[]{:S(2)}) %collective-permute-start.5) | collective-permute-done | bytes 49184 | tf_op jit(solution)/shard_map/ppermute | solution.py:10
  65.9 0.7 constant_dynamic-update-slice_fusion.2
  66.5 0.7 constant_dynamic-update-slice_fusion.1
  67.8 1.8 %gather_fusion = bf16[128,24,64]{2,1,0:T(8,128)(2,1)S(1)} fusion(bf16[24,80,64]{2,0,1:T(8,128)(2,1)} %constant_dynamic-update-slice_fusion, s32[1024]{0:T(1024)S(1)} %pad_clamp_fusion.1), kind=kCustom, calls=%fused_computation | custom fusion | bytes 786944 | tf_op jit(solution)/shard_map/gather | solution.py:90
  70.6 0.7 convolution_bitcast_fusion
  71.3 2.0 %fusion.1 = f32[80,2048]{1,0:T(8,128)S(1)} fusion(f32[80,2048]{1,0:T(8,128)} %param.20, f32[80,2048]{1,0:T(8,128)S(1)} %convolution_bitcast_fusion, f32[80,80]{1,0:T(8,128)S(1)} %copy-done.2, pred[2048]{0:T(1024)(128)(4,1)S(1)} %broadcast_compare_fusion), kind=kOutput, calls=%fused_computation.4 | convolution fusion | flops 157777920 | bytes 1993728 | tf_op jit(solution)/shard_map/dot_general | solution.py:94
  73.9 1.9 %collective-permute-start.8 = (bf16[8,32,64]{2,0,1:T(8,128)(2,1)S(1)}, bf16[8,32,64]{2,0,1:T(8,128)(2,1)S(1)}, u32[]{:S(2)}, u32[]{:S(2)}) collective-permute-start(bf16[8,32,64]{2,0,1:T(8,128)(2,1)S(1)} %copy.42), channel_id=1, source_target_pairs={{0,2},{1,3},{2,4},{3,5},{4,6},{5,7},{6,8},{7,9},{8,10},{9,11},{10,... | collective-permute-start | bytes 98312 | tf_op jit(solution)/shard_map/ppermute | solution.py:10
  75.9 1.9 %collective-permute-start.10 = (bf16[8,32,64]{2,0,1:T(8,128)(2,1)S(1)}, bf16[8,32,64]{2,0,1:T(8,128)(2,1)S(1)}, u32[]{:S(2)}, u32[]{:S(2)}) collective-permute-start(bf16[8,32,64]{2,0,1:T(8,128)(2,1)S(1)} %copy.42), channel_id=1, source_target_pairs={{0,63},{1,0},{2,1},{3,2},{4,3},{5,4},{6,5},{7,6},{8,7},{9,8},{10,9... | collective-permute-start | bytes 98312 | tf_op jit(solution)/shard_map/ppermute | solution.py:10
  77.8 8.1 %collective-permute-start.11 = (bf16[8,32,64]{2,0,1:T(8,128)(2,1)S(1)}, bf16[8,32,64]{2,0,1:T(8,128)(2,1)S(1)}, u32[]{:S(2)}, u32[]{:S(2)}) collective-permute-start(bf16[8,32,64]{2,0,1:T(8,128)(2,1)S(1)} %copy.42), channel_id=1, source_target_pairs={{0,62},{1,63},{2,0},{3,1},{4,2},{5,3},{6,4},{7,5},{8,6},{9,7},{10,... | collective-permute-start | bytes 98312 | tf_op jit(solution)/shard_map/ppermute | solution.py:10
  86.0 2.1 %collective-permute-start.9 = (bf16[8,32,64]{2,0,1:T(8,128)(2,1)S(1)}, bf16[8,32,64]{2,0,1:T(8,128)(2,1)S(1)}, u32[]{:S(2)}, u32[]{:S(2)}) collective-permute-start(bf16[8,32,64]{2,0,1:T(8,128)(2,1)S(1)} %copy.42), channel_id=1, source_target_pairs={{0,1},{1,2},{2,3},{3,4},{4,5},{5,6},{6,7},{7,8},{8,9},{9,10},{10,1... | collective-permute-start | bytes 98312 | tf_op jit(solution)/shard_map/ppermute | solution.py:10
  88.7 7.0 %collective-permute-done.9 = bf16[8,32,64]{2,0,1:T(8,128)(2,1)S(1)} collective-permute-done((bf16[8,32,64]{2,0,1:T(8,128)(2,1)S(1)}, bf16[8,32,64]{2,0,1:T(8,128)(2,1)S(1)}, u32[]{:S(2)}, u32[]{:S(2)}) %collective-permute-start.9) | collective-permute-done | bytes 32800 | tf_op jit(solution)/shard_map/ppermute | solution.py:10
  98.3 1.6 %gather_fusion.1 = bf16[64,8,64]{2,1,0:T(8,128)(2,1)S(1)} fusion(bf16[8,160,64]{2,0,1:T(8,128)(2,1)} %constant_dynamic-update-slice_fusion.5, s32[1024]{0:T(1024)S(1)} %pad_clamp_fusion), kind=kCustom, calls=%fused_computation.1 | custom fusion | bytes 131328 | tf_op jit(solution)/shard_map/gather | solution.py:108
  99.9 1.6 %convolution_bitcast_fusion.5 = f32[8,16,64]{2,0,1:T(8,128)S(1)} fusion(bf16[8,16,4,64]{3,0,2,1:T(8,128)(2,1)S(1)} %bitcast.58, bf16[16,4,64,64]{3,2,1,0:T(8,128)(2,1)} %param.25), kind=kOutput, calls=%fused_computation.15 | convolution fusion | flops 4194304 | bytes 622592 | tf_op jit(solution)/shard_map/okij,fokj->foi/dot_general | solution.py:44
  101.6 1.8 %fusion.3 = f32[72,8,128]{0,2,1:T(8,128)} fusion(f32[72,8,128]{0,2,1:T(8,128)S(1)} %fusion.4, f32[8,8,128]{2,1,0:T(8,128)S(1)} %reshape.39, f32[72,8]{0,1:T(8,128)S(1)} %copy-done.7), kind=kOutput, calls=%fused_computation.10 | convolution fusion | flops 7151616 | bytes 624896 | tf_op jit(solution)/shard_map/ml,l...->m.../dot_general | solution.py:32
  103.4 1.9 %copy.51 = f32[72,8,128]{2,1,0:T(8,128)} copy(f32[72,8,128]{0,2,1:T(8,128)} %fusion.3) | data formatting | bytes 589824
  (70 shorter events, 9.8 us)
Async XLA Ops:
  0.6 69.0 %copy-start = (bf16[32,4,64,64]{3,2,1,0:T(8,128)(2,1)S(1)}, bf16[32,4,64,64]{3,2,1,0:T(8,128)(2,1)}, u32[]{:S(2)}) copy-start(bf16[32,4,64,64]{3,2,1,0:T(8,128)(2,1)} %param.18) | copy-start | bytes 3145732
  0.6 13.0 %copy-start.5 = (s32[2048]{0:T(1024)S(1)}, s32[2048]{0:T(1024)}, u32[]{:S(2)}) copy-start(s32[2048]{0:T(1024)} %param.23) | copy-start | bytes 24580
  0.7 13.0 %copy-start.8 = (s32[32,4]{0,1:T(4,128)S(1)}, s32[32,4]{0,1:T(4,128)}, u32[]{:S(2)}) copy-start(s32[32,4]{0,1:T(4,128)} %param.19) | copy-start | bytes 1540
  3.0 32.8 %copy-start.9 = (s32[16,4]{0,1:T(4,128)S(1)}, s32[16,4]{0,1:T(4,128)}, u32[]{:S(2)}) copy-start(s32[16,4]{0,1:T(4,128)} %param.26) | copy-start | bytes 772
  3.4 10.3 %collective-permute-start = (f32[1168]{0:T(1024)S(1)}, f32[1168]{0:T(1024)S(1)}, u32[]{:S(2)}, u32[]{:S(2)}) collective-permute-start(f32[1168]{0:T(1024)S(1)} %reshape.32), channel_id=1, source_target_pairs={{0,1},{1,2},{2,3},{3,4},{4,5},{5,6},{6,7},{7,8},{8,9},{9,10},{10,1... | collective-permute-start | bytes 14024 | tf_op jit(solution)/shard_map/ppermute | solution.py:10
  5.8 9.2 %collective-permute-start.1 = (f32[1168]{0:T(1024)S(1)}, f32[1168]{0:T(1024)S(1)}, u32[]{:S(2)}, u32[]{:S(2)}) collective-permute-start(f32[1168]{0:T(1024)S(1)} %reshape.34), channel_id=1, source_target_pairs={{0,63},{1,0},{2,1},{3,2},{4,3},{5,4},{6,5},{7,6},{8,7},{9,8},{10,9... | collective-permute-start | bytes 14024 | tf_op jit(solution)/shard_map/ppermute | solution.py:10
  15.4 24.3 %copy-start.10 = (f32[72,72]{1,0:T(8,128)S(1)}, f32[72,72]{1,0:T(8,128)}, u32[]{:S(2)}) copy-start(f32[72,72]{1,0:T(8,128)} %param.16) | copy-start | bytes 62212
  16.3 21.9 %collective-permute-start.2 = (f32[73,2,132]{0,2,1:T(8,128)}, f32[73,2,132]{0,2,1:T(8,128)S(1)}, u32[]{:S(2)}, u32[]{:S(2)}) collective-permute-start(f32[73,2,132]{0,2,1:T(8,128)} %get-tuple-element.6), channel_id=1, source_target_pairs={{0,64},{64,128},{128,192},{192,256},{256,320},{320,384},{384,448},... | collective-permute-start | bytes 231272 | tf_op jit(solution)/shard_map/ppermute | solution.py:10
  19.0 19.7 %collective-permute-start.3 = (f32[73,2,132]{0,2,1:T(8,128)}, f32[73,2,132]{0,2,1:T(8,128)S(1)}, u32[]{:S(2)}, u32[]{:S(2)}) collective-permute-start(f32[73,2,132]{0,2,1:T(8,128)} %get-tuple-element.7), channel_id=1, source_target_pairs={{0,960},{64,0},{128,64},{192,128},{256,192},{320,256},{384,320},{4... | collective-permute-start | bytes 231272 | tf_op jit(solution)/shard_map/ppermute | solution.py:10
  39.8 1.8 %copy-start.3 = (f32[24,72]{1,0:T(8,128)S(1)}, f32[24,72]{1,0:T(8,128)}, u32[]{:S(2)}) copy-start(f32[24,72]{1,0:T(8,128)} %param.17) | copy-start | bytes 20740
  42.3 14.7 %collective-permute-start.4 = (bf16[24,16,64]{2,0,1:T(8,128)(2,1)S(1)}, bf16[24,16,64]{2,0,1:T(8,128)(2,1)S(1)}, u32[]{:S(2)}, u32[]{:S(2)}) collective-permute-start(bf16[24,16,64]{2,0,1:T(8,128)(2,1)S(1)} %copy.35), channel_id=1, source_target_pairs={{0,2},{1,3},{2,4},{3,5},{4,6},{5,7},{6,8},{7,9},{8,10},{9,11},{10,... | collective-permute-start | bytes 147464 | tf_op jit(solution)/shard_map/ppermute | solution.py:10
  44.4 22.1 %collective-permute-start.6 = (bf16[24,16,64]{2,0,1:T(8,128)(2,1)S(1)}, bf16[24,16,64]{2,0,1:T(8,128)(2,1)S(1)}, u32[]{:S(2)}, u32[]{:S(2)}) collective-permute-start(bf16[24,16,64]{2,0,1:T(8,128)(2,1)S(1)} %copy.35), channel_id=1, source_target_pairs={{0,63},{1,0},{2,1},{3,2},{4,3},{5,4},{6,5},{7,6},{8,7},{9,8},{10,9... | collective-permute-start | bytes 147464 | tf_op jit(solution)/shard_map/ppermute | solution.py:10
  51.4 15.8 %collective-permute-start.7 = (bf16[24,16,64]{2,0,1:T(8,128)(2,1)S(1)}, bf16[24,16,64]{2,0,1:T(8,128)(2,1)S(1)}, u32[]{:S(2)}, u32[]{:S(2)}) collective-permute-start(bf16[24,16,64]{2,0,1:T(8,128)(2,1)S(1)} %copy.35), channel_id=1, source_target_pairs={{0,62},{1,63},{2,0},{3,1},{4,2},{5,3},{6,4},{7,5},{8,6},{9,7},{10,... | collective-permute-start | bytes 147464 | tf_op jit(solution)/shard_map/ppermute | solution.py:10
  55.1 10.2 %collective-permute-start.5 = (bf16[24,16,64]{2,0,1:T(8,128)(2,1)S(1)}, bf16[24,16,64]{2,0,1:T(8,128)(2,1)S(1)}, u32[]{:S(2)}, u32[]{:S(2)}) collective-permute-start(bf16[24,16,64]{2,0,1:T(8,128)(2,1)S(1)} %copy.35), channel_id=1, source_target_pairs={{0,1},{1,2},{2,3},{3,4},{4,5},{5,6},{6,7},{7,8},{8,9},{9,10},{10,1... | collective-permute-start | bytes 147464 | tf_op jit(solution)/shard_map/ppermute | solution.py:10
  69.6 0.9 copy-start.4
  69.7 1.6 %copy-start.2 = (f32[80,80]{1,0:T(8,128)S(1)}, f32[80,80]{1,0:T(8,128)}, u32[]{:S(2)}) copy-start(f32[80,80]{1,0:T(8,128)} %param.21) | copy-start | bytes 76804
  70.3 3.0 %copy-start.6 = (f32[8,80]{1,0:T(8,128)S(1)}, f32[8,80]{1,0:T(8,128)}, u32[]{:S(2)}) copy-start(f32[8,80]{1,0:T(8,128)} %param.24) | copy-start | bytes 7684
  73.3 30.2 %copy-start.1 = (f32[80,2048]{1,0:T(8,128)}, f32[80,2048]{1,0:T(8,128)S(1)}, u32[]{:S(2)}) copy-start(f32[80,2048]{1,0:T(8,128)S(1)} %fusion.1) | copy-start | bytes 1966084
  73.3 28.3 %copy-start.7 = (f32[72,8]{0,1:T(8,128)S(1)}, f32[72,8]{0,1:T(8,128)}, u32[]{:S(2)}) copy-start(f32[72,8]{0,1:T(8,128)} %param.27) | copy-start | bytes 6916
  73.9 14.2 %collective-permute-start.8 = (bf16[8,32,64]{2,0,1:T(8,128)(2,1)S(1)}, bf16[8,32,64]{2,0,1:T(8,128)(2,1)S(1)}, u32[]{:S(2)}, u32[]{:S(2)}) collective-permute-start(bf16[8,32,64]{2,0,1:T(8,128)(2,1)S(1)} %copy.42), channel_id=1, source_target_pairs={{0,2},{1,3},{2,4},{3,5},{4,6},{5,7},{6,8},{7,9},{8,10},{9,11},{10,... | collective-permute-start | bytes 98312 | tf_op jit(solution)/shard_map/ppermute | solution.py:10
  75.9 21.2 %collective-permute-start.10 = (bf16[8,32,64]{2,0,1:T(8,128)(2,1)S(1)}, bf16[8,32,64]{2,0,1:T(8,128)(2,1)S(1)}, u32[]{:S(2)}, u32[]{:S(2)}) collective-permute-start(bf16[8,32,64]{2,0,1:T(8,128)(2,1)S(1)} %copy.42), channel_id=1, source_target_pairs={{0,63},{1,0},{2,1},{3,2},{4,3},{5,4},{6,5},{7,6},{8,7},{9,8},{10,9... | collective-permute-start | bytes 98312 | tf_op jit(solution)/shard_map/ppermute | solution.py:10
  77.8 19.9 %collective-permute-start.11 = (bf16[8,32,64]{2,0,1:T(8,128)(2,1)S(1)}, bf16[8,32,64]{2,0,1:T(8,128)(2,1)S(1)}, u32[]{:S(2)}, u32[]{:S(2)}) collective-permute-start(bf16[8,32,64]{2,0,1:T(8,128)(2,1)S(1)} %copy.42), channel_id=1, source_target_pairs={{0,62},{1,63},{2,0},{3,1},{4,2},{5,3},{6,4},{7,5},{8,6},{9,7},{10,... | collective-permute-start | bytes 98312 | tf_op jit(solution)/shard_map/ppermute | solution.py:10
  86.0 9.8 %collective-permute-start.9 = (bf16[8,32,64]{2,0,1:T(8,128)(2,1)S(1)}, bf16[8,32,64]{2,0,1:T(8,128)(2,1)S(1)}, u32[]{:S(2)}, u32[]{:S(2)}) collective-permute-start(bf16[8,32,64]{2,0,1:T(8,128)(2,1)S(1)} %copy.42), channel_id=1, source_target_pairs={{0,1},{1,2},{2,3},{3,4},{4,5},{5,6},{6,7},{7,8},{8,9},{9,10},{10,1... | collective-permute-start | bytes 98312 | tf_op jit(solution)/shard_map/ppermute | solution.py:10

commit v2 on v1

--- a/solution.py
+++ b/solution.py
@@ -49,6 +49,20 @@
     return relative * per_tile + cols % per_tile
 
 
+def exchange_and_pick(blocks, cols, here):
+    fields, per_tile, cells = blocks.shape
+    tiles = lax.axis_size("tile")
+    local = near_index(cols, per_tile, tiles, here).reshape(-1)
+    picked = None
+    for slot, offset in enumerate((-2, -1, 0, 1, 2)):
+        piece = blocks if offset == 0 else from_behind(blocks, "tile", -offset)
+        ids = slot * per_tile + jnp.arange(per_tile, dtype=local.dtype)
+        onehot = (local[:, None] == ids[None, :]).astype(blocks.dtype)
+        part = jnp.einsum("qb,fbj->fqj", onehot, piece, preferred_element_type=jnp.float32)
+        picked = part if picked is None else picked + part
+    return picked.astype(blocks.dtype).reshape((fields,) + cols.shape + (cells,))
+
+
 def body(
     atm_state,
     kappa,
@@ -77,35 +91,17 @@
     atm_blocks = rows_here * cols_here // 64
     surface_blocks = surface.reshape(fields, atm_blocks, 64)
     ocean_blocks = remap_weight.shape[0]
-    tiles = lax.axis_size("tile")
     here = lax.axis_index("tile")
-    pieces = []
-    for offset in (-2, -1, 0, 1, 2):
-        if offset == 0:
-            pieces.append(surface_blocks)
-        else:
-            pieces.append(from_behind(surface_blocks, "tile", -offset))
-    nearby = jnp.concatenate(pieces, 1)
-    local = near_index(remap_cols, atm_blocks, tiles, here)
-    remapped = block_product(remap_weight, nearby[:, local])
+    mixed = lax.optimization_barrier(
+        ocean_state + jnp.dot(ocean_mix, ocean_state, precision=lax.Precision.HIGHEST)
+    )
+    remapped = block_product(remap_weight, exchange_and_pick(surface_blocks, remap_cols, here))
     remapped = remapped.reshape(fields, ocean_blocks * 64)
-    stepped = (
-        ocean_state
-        + jnp.dot(ocean_mix, ocean_state, precision=lax.Precision.HIGHEST)
-        + jnp.dot(forcing, remapped, precision=lax.Precision.HIGHEST)
-    )
+    stepped = mixed + jnp.dot(forcing, remapped, precision=lax.Precision.HIGHEST)
     ocean_out = jnp.where(wet_mask[None] == 1, stepped, ocean_state)
     sea = jnp.dot(surface_proj, ocean_out, precision=lax.Precision.HIGHEST).astype(jnp.bfloat16)
     sea_blocks = sea.reshape(sea.shape[0], ocean_blocks, 64)
-    sea_pieces = []
-    for offset in (-2, -1, 0, 1, 2):
-        if offset == 0:
-            sea_pieces.append(sea_blocks)
-        else:
-            sea_pieces.append(from_behind(sea_blocks, "tile", -offset))
-    sea_nearby = jnp.concatenate(sea_pieces, 1)
-    back_local = near_index(back_cols, ocean_blocks, tiles, here)
-    returned = block_product(back_weight, sea_nearby[:, back_local])
+    returned = block_product(back_weight, exchange_and_pick(sea_blocks, back_cols, here))
     returned = returned.reshape(sea.shape[0], rows_here, cols_here)
     atm_out = atm_mid + level_mix(back_proj, returned)
     return (atm_out, ocean_out)

time: 106 us -> 94.9 us (0.90)
  the two profiles are of different devices: /device:TPU:64 before, /device:TPU:47 now
where the time goes in v2:
time: 94.9 us; the launch traced here: 94.3 us
  starting transfers between devices  52.1 us (55%)
  waiting for transfers between devices  15.5 us (16%)
  matrix products  13.4 us (14%)
  local copies, waits for them, and re-layouts  8.75 us (9%)
  other arithmetic  3.34 us (4%)
  between operations  1.2 us (1%)
    ppermute x12, starting transfers between devices, from_behind(): return lax.ppermute(value, axis, pairs)  52.1 us
    ppermute x12, waiting for transfers between devices, from_behind(): return lax.ppermute(value, axis, pairs)  15.5 us
    dot_general x4, matrix products, level_mix(): jnp.einsum('ml,l...->m...', matrix, field, precision=lax.Precision.HIGHEST)  3.38 us
    unnamed x38, local copies, waits for them, and re-layouts  3.09 us
    dot_general x1, matrix products, body(): jnp.dot(ocean_mix, ocean_state, precision=lax.Precision.HIGHEST)  2.79 us
    dot_general x10, matrix products, exchange_and_pick(): jnp.einsum('qb,fbj->fqj', onehot, piece, preferred_element_type=jnp.float32)  2.73 us
    add x8, other arithmetic, exchange_and_pick(): ids = slot * per_tile + jnp.arange(per_tile, dtype=local.dtype)  2.25 us
    dot_general x2, matrix products, block_product(): jnp.einsum('okij,fokj->foi', weights, picked, preferred_element_type=jnp....  2.22 us
  transfers between devices with their start and end apart: 12, of which 6 were waited for; matrix products, arithmetic and copies ran while one was open for 10% of the time, Pallas kernels for 0%

profile of v2, /device:TPU:47, one launch (start us, length us, event | category | flops | bytes accessed | tf_op | source)
XLA Modules:
  0.0 94.3 jit_solution(7873842096047229113)
XLA Ops:
  0.7 1.3 %copy.26 = f32[72,8,128]{0,2,1:T(8,128)S(1)} copy(f32[72,8,128]{2,1,0:T(8,128)} %param.14) | data formatting | bytes 589824 | tf_op args[0]
  2.0 0.9 copy.27
  3.4 6.0 %collective-permute-start = (f32[1168]{0:T(1024)S(1)}, f32[1168]{0:T(1024)S(1)}, u32[]{:S(2)}, u32[]{:S(2)}) collective-permute-start(f32[1168]{0:T(1024)S(1)} %reshape.72), channel_id=1, source_target_pairs={{0,1},{1,2},{2,3},{3,4},{4,5},{5,6},{6,7},{7,8},{8,9},{9,10},{10,1... | collective-permute-start | bytes 14024 | tf_op jit(solution)/shard_map/ppermute | solution.py:10
  9.9 1.9 %collective-permute-start.1 = (f32[1168]{0:T(1024)S(1)}, f32[1168]{0:T(1024)S(1)}, u32[]{:S(2)}, u32[]{:S(2)}) collective-permute-start(f32[1168]{0:T(1024)S(1)} %reshape.74), channel_id=1, source_target_pairs={{0,63},{1,0},{2,1},{3,2},{4,3},{5,4},{6,5},{7,6},{8,7},{9,8},{10,9... | collective-permute-start | bytes 14024 | tf_op jit(solution)/shard_map/ppermute | solution.py:10
  11.8 0.6 iota_add_fusion.3
  13.6 2.8 %convolution_add_fusion = f32[80,2048]{1,0:T(8,128)} fusion(f32[80,2048]{1,0:T(8,128)} %param.20, f32[80,80]{1,0:T(8,128)S(1)} %copy-done.5), kind=kOutput, calls=%fused_computation | convolution fusion | flops 157450240 | bytes 1336320 | tf_op jit(solution)/shard_map/dot_general | solution.py:96
  17.8 1.3 %collective-permute-done.1 = f32[1168]{0:T(1024)S(1)} collective-permute-done((f32[1168]{0:T(1024)S(1)}, f32[1168]{0:T(1024)S(1)}, u32[]{:S(2)}, u32[]{:S(2)}) %collective-permute-start.1) | collective-permute-done | bytes 4704 | tf_op jit(solution)/shard_map/ppermute | solution.py:10
  19.7 2.4 %collective-permute-start.2 = (f32[73,2,132]{0,2,1:T(8,128)S(1)}, f32[73,2,132]{0,2,1:T(8,128)S(1)}, u32[]{:S(2)}, u32[]{:S(2)}) collective-permute-start(f32[73,2,132]{0,2,1:T(8,128)S(1)} %get-tuple-element.6), channel_id=1, source_target_pairs={{0,64},{64,128},{128,192},{192,256},{256,320},{320,384},{384,448},... | collective-permute-start | bytes 231272 | tf_op jit(solution)/shard_map/ppermute | solution.py:10
  22.1 16.8 %collective-permute-start.3 = (f32[73,2,132]{0,2,1:T(8,128)S(1)}, f32[73,2,132]{0,2,1:T(8,128)S(1)}, u32[]{:S(2)}, u32[]{:S(2)}) collective-permute-start(f32[73,2,132]{0,2,1:T(8,128)S(1)} %get-tuple-element.7), channel_id=1, source_target_pairs={{0,960},{64,0},{128,64},{192,128},{256,192},{320,256},{384,320},{4... | collective-permute-start | bytes 231272 | tf_op jit(solution)/shard_map/ppermute | solution.py:10
  39.4 1.5 %collective-permute-done.3 = f32[73,2,132]{0,2,1:T(8,128)S(1)} collective-permute-done((f32[73,2,132]{0,2,1:T(8,128)S(1)}, f32[73,2,132]{0,2,1:T(8,128)S(1)}, u32[]{:S(2)}, u32[]{:S(2)}) %collective-permute-start.3) | collective-permute-done | bytes 77120 | tf_op jit(solution)/shard_map/ppermute | solution.py:10
  41.1 0.7 slice_reduce_fusion
  42.0 1.1 %fusion.17 = f32[72,10,130]{0,2,1:T(8,128)S(1)} fusion(f32[73,12,132]{0,2,1:T(8,128)S(1)} %pad_maximum_fusion, f32[73,2,132]{0,2,1:T(8,128)S(1)} %collective-permute-done.2, f32[73,8,2]{0,2,1:T(2,128)S(1)} %copy.31, f32[73,8,2]{0,2,1:T(2,128)S(1)} %copy.30, f32[1,8,128]{0,2,1:T(8,128)S(1)} %copy.27, f32[72,8,128]{0,2,1:T(8,128)S(1)} %copy.26, ...), kind=kOutput, calls=%fused_computation.33 | convolution fusion | flops 82368000 | bytes 4556416 | tf_op jit(solution)/shard_map/ml,l...->m.../dot_general | solution.py:32
  43.1 0.7 fusion.7
  43.8 0.8 copy-done.3
  45.3 7.5 %collective-permute-start.5 = (bf16[24,16,64]{2,1,0:T(8,128)(2,1)S(1)}, bf16[24,16,64]{2,1,0:T(8,128)(2,1)S(1)}, u32[]{:S(2)}, u32[]{:S(2)}) collective-permute-start(bf16[24,16,64]{2,1,0:T(8,128)(2,1)S(1)} %reshape.76), channel_id=1, source_target_pairs={{0,1},{1,2},{2,3},{3,4},{4,5},{5,6},{6,7},{7,8},{8,9},{9,10},{10,1... | collective-permute-start | bytes 147464 | tf_op jit(solution)/shard_map/ppermute | solution.py:10
  52.8 1.9 %collective-permute-start.4 = (bf16[24,16,64]{2,1,0:T(8,128)(2,1)S(1)}, bf16[24,16,64]{2,1,0:T(8,128)(2,1)S(1)}, u32[]{:S(2)}, u32[]{:S(2)}) collective-permute-start(bf16[24,16,64]{2,1,0:T(8,128)(2,1)S(1)} %reshape.76), channel_id=1, source_target_pairs={{0,2},{1,3},{2,4},{3,5},{4,6},{5,7},{6,8},{7,9},{8,10},{9,11},{10,... | collective-permute-start | bytes 147464 | tf_op jit(solution)/shard_map/ppermute | solution.py:10
  54.7 3.4 %collective-permute-start.7 = (bf16[24,16,64]{2,1,0:T(8,128)(2,1)S(1)}, bf16[24,16,64]{2,1,0:T(8,128)(2,1)S(1)}, u32[]{:S(2)}, u32[]{:S(2)}) collective-permute-start(bf16[24,16,64]{2,1,0:T(8,128)(2,1)S(1)} %reshape.76), channel_id=1, source_target_pairs={{0,62},{1,63},{2,0},{3,1},{4,2},{5,3},{6,4},{7,5},{8,6},{9,7},{10,... | collective-permute-start | bytes 147464 | tf_op jit(solution)/shard_map/ppermute | solution.py:10
  58.1 1.9 %collective-permute-start.6 = (bf16[24,16,64]{2,1,0:T(8,128)(2,1)S(1)}, bf16[24,16,64]{2,1,0:T(8,128)(2,1)S(1)}, u32[]{:S(2)}, u32[]{:S(2)}) collective-permute-start(bf16[24,16,64]{2,1,0:T(8,128)(2,1)S(1)} %reshape.76), channel_id=1, source_target_pairs={{0,63},{1,0},{2,1},{3,2},{4,3},{5,4},{6,5},{7,6},{8,7},{9,8},{10,9... | collective-permute-start | bytes 147464 | tf_op jit(solution)/shard_map/ppermute | solution.py:10
  61.0 3.8 %collective-permute-done.7 = bf16[24,16,64]{2,1,0:T(8,128)(2,1)S(1)} collective-permute-done((bf16[24,16,64]{2,1,0:T(8,128)(2,1)S(1)}, bf16[24,16,64]{2,1,0:T(8,128)(2,1)S(1)}, u32[]{:S(2)}, u32[]{:S(2)}) %collective-permute-start.7) | collective-permute-done | bytes 49184 | tf_op jit(solution)/shard_map/ppermute | solution.py:10
  65.1 3.1 %collective-permute-done.6 = bf16[24,16,64]{2,1,0:T(8,128)(2,1)S(1)} collective-permute-done((bf16[24,16,64]{2,1,0:T(8,128)(2,1)S(1)}, bf16[24,16,64]{2,1,0:T(8,128)(2,1)S(1)}, u32[]{:S(2)}, u32[]{:S(2)}) %collective-permute-start.6) | collective-permute-done | bytes 49184 | tf_op jit(solution)/shard_map/ppermute | solution.py:10
  69.0 0.6 convolution_bitcast_fusion.4
  69.8 0.8 reshape.78
  70.6 1.8 %fusion.1 = f32[80,2048]{1,0:T(8,128)S(1)} fusion(f32[80,2048]{1,0:T(8,128)S(1)} %copy-done.1, f32[80,2048]{1,0:T(8,128)} %convolution_add_fusion, f32[24,2048]{1,0:T(8,128)} %reshape.78, f32[80,24]{0,1:T(8,128)S(1)} %copy-done.6, pred[2048]{0:T(1024)(128)(4,1)} %broadcast_compare_fusion), kind=kOutput, calls=%fused_computation.3 | convolution fusion | flops 47513600 | bytes 2172416 | tf_op jit(solution)/shard_map/dot_general | solution.py:100
  73.1 2.1 %collective-permute-start.9 = (bf16[8,32,64]{2,1,0:T(8,128)(2,1)S(1)}, bf16[8,32,64]{2,1,0:T(8,128)(2,1)S(1)}, u32[]{:S(2)}, u32[]{:S(2)}) collective-permute-start(bf16[8,32,64]{2,1,0:T(8,128)(2,1)S(1)} %reshape.79), channel_id=1, source_target_pairs={{0,1},{1,2},{2,3},{3,4},{4,5},{5,6},{6,7},{7,8},{8,9},{9,10},{10,1... | collective-permute-start | bytes 98312 | tf_op jit(solution)/shard_map/ppermute | solution.py:10
  75.2 1.9 %collective-permute-start.8 = (bf16[8,32,64]{2,1,0:T(8,128)(2,1)S(1)}, bf16[8,32,64]{2,1,0:T(8,128)(2,1)S(1)}, u32[]{:S(2)}, u32[]{:S(2)}) collective-permute-start(bf16[8,32,64]{2,1,0:T(8,128)(2,1)S(1)} %reshape.79), channel_id=1, source_target_pairs={{0,2},{1,3},{2,4},{3,5},{4,6},{5,7},{6,8},{7,9},{8,10},{9,11},{10,... | collective-permute-start | bytes 98312 | tf_op jit(solution)/shard_map/ppermute | solution.py:10
  77.1 3.4 %collective-permute-start.11 = (bf16[8,32,64]{2,1,0:T(8,128)(2,1)S(1)}, bf16[8,32,64]{2,1,0:T(8,128)(2,1)S(1)}, u32[]{:S(2)}, u32[]{:S(2)}) collective-permute-start(bf16[8,32,64]{2,1,0:T(8,128)(2,1)S(1)} %reshape.79), channel_id=1, source_target_pairs={{0,62},{1,63},{2,0},{3,1},{4,2},{5,3},{6,4},{7,5},{8,6},{9,7},{10,... | collective-permute-start | bytes 98312 | tf_op jit(solution)/shard_map/ppermute | solution.py:10
  80.5 3.0 %collective-permute-start.10 = (bf16[8,32,64]{2,1,0:T(8,128)(2,1)S(1)}, bf16[8,32,64]{2,1,0:T(8,128)(2,1)S(1)}, u32[]{:S(2)}, u32[]{:S(2)}) collective-permute-start(bf16[8,32,64]{2,1,0:T(8,128)(2,1)S(1)} %reshape.79), channel_id=1, source_target_pairs={{0,63},{1,0},{2,1},{3,2},{4,3},{5,4},{6,5},{7,6},{8,7},{9,8},{10,9... | collective-permute-start | bytes 98312 | tf_op jit(solution)/shard_map/ppermute | solution.py:10
  84.2 2.2 %collective-permute-done.11 = bf16[8,32,64]{2,1,0:T(8,128)(2,1)S(1)} collective-permute-done((bf16[8,32,64]{2,1,0:T(8,128)(2,1)S(1)}, bf16[8,32,64]{2,1,0:T(8,128)(2,1)S(1)}, u32[]{:S(2)}, u32[]{:S(2)}) %collective-permute-start.11) | collective-permute-done | bytes 32800 | tf_op jit(solution)/shard_map/ppermute | solution.py:10
  86.6 3.7 %collective-permute-done.10 = bf16[8,32,64]{2,1,0:T(8,128)(2,1)S(1)} collective-permute-done((bf16[8,32,64]{2,1,0:T(8,128)(2,1)S(1)}, bf16[8,32,64]{2,1,0:T(8,128)(2,1)S(1)}, u32[]{:S(2)}, u32[]{:S(2)}) %collective-permute-start.10) | collective-permute-done | bytes 32800 | tf_op jit(solution)/shard_map/ppermute | solution.py:10
  90.7 1.6 %convolution_bitcast_fusion.5 = f32[8,16,64]{2,0,1:T(8,128)S(1)} fusion(bf16[8,16,4,64]{3,0,2,1:T(8,128)(2,1)S(1)} %bitcast.102, bf16[16,4,64,64]{3,2,1,0:T(8,128)(2,1)} %param.25), kind=kOutput, calls=%fused_computation.25 | convolution fusion | flops 4194304 | bytes 622592 | tf_op jit(solution)/shard_map/okij,fokj->foi/dot_general | solution.py:44
  92.4 1.0 %fusion.6 = f32[72,8,128]{0,2,1:T(8,128)S(1)} fusion(f32[72,8,128]{0,2,1:T(8,128)S(1)} %copy-done.4, f32[8,8,128]{2,1,0:T(8,128)S(1)} %reshape.81, f32[72,8]{0,1:T(8,128)S(1)} %copy-done.10), kind=kOutput, calls=%fused_computation.13 | convolution fusion | flops 7151616 | bytes 624896 | tf_op jit(solution)/shard_map/ml,l...->m.../dot_general | solution.py:32
  93.4 0.9 copy.44
  (88 shorter events, 9.8 us)
Async XLA Ops:
  0.6 68.4 %copy-start = (bf16[32,4,64,64]{3,2,1,0:T(8,128)(2,1)S(1)}, bf16[32,4,64,64]{3,2,1,0:T(8,128)(2,1)}, u32[]{:S(2)}) copy-start(bf16[32,4,64,64]{3,2,1,0:T(8,128)(2,1)} %param.18) | copy-start | bytes 3145732
  0.6 12.3 %copy-start.8 = (s32[2048]{0:T(1024)S(1)}, s32[2048]{0:T(1024)}, u32[]{:S(2)}) copy-start(s32[2048]{0:T(1024)} %param.23) | copy-start | bytes 24580
  0.7 12.9 %copy-start.11 = (s32[32,4]{0,1:T(4,128)S(1)}, s32[32,4]{0,1:T(4,128)}, u32[]{:S(2)}) copy-start(s32[32,4]{0,1:T(4,128)} %param.19) | copy-start | bytes 1540
  0.7 12.9 %copy-start.12 = (s32[16,4]{0,1:T(4,128)S(1)}, s32[16,4]{0,1:T(4,128)}, u32[]{:S(2)}) copy-start(s32[16,4]{0,1:T(4,128)} %param.26) | copy-start | bytes 772
  0.7 12.9 %copy-start.5 = (f32[80,80]{1,0:T(8,128)S(1)}, f32[80,80]{1,0:T(8,128)}, u32[]{:S(2)}) copy-start(f32[80,80]{1,0:T(8,128)} %param.21) | copy-start | bytes 76804
  3.4 13.9 %collective-permute-start = (f32[1168]{0:T(1024)S(1)}, f32[1168]{0:T(1024)S(1)}, u32[]{:S(2)}, u32[]{:S(2)}) collective-permute-start(f32[1168]{0:T(1024)S(1)} %reshape.72), channel_id=1, source_target_pairs={{0,1},{1,2},{2,3},{3,4},{4,5},{5,6},{6,7},{7,8},{8,9},{9,10},{10,1... | collective-permute-start | bytes 14024 | tf_op jit(solution)/shard_map/ppermute | solution.py:10
  9.9 9.2 %collective-permute-start.1 = (f32[1168]{0:T(1024)S(1)}, f32[1168]{0:T(1024)S(1)}, u32[]{:S(2)}, u32[]{:S(2)}) collective-permute-start(f32[1168]{0:T(1024)S(1)} %reshape.74), channel_id=1, source_target_pairs={{0,63},{1,0},{2,1},{3,2},{4,3},{5,4},{6,5},{7,6},{8,7},{9,8},{10,9... | collective-permute-start | bytes 14024 | tf_op jit(solution)/shard_map/ppermute | solution.py:10
  19.5 22.5 %copy-start.17 = (f32[72,72]{1,0:T(8,128)S(1)}, f32[72,72]{1,0:T(8,128)}, u32[]{:S(2)}) copy-start(f32[72,72]{1,0:T(8,128)} %param.16) | copy-start | bytes 62212
  19.7 19.7 %collective-permute-start.2 = (f32[73,2,132]{0,2,1:T(8,128)S(1)}, f32[73,2,132]{0,2,1:T(8,128)S(1)}, u32[]{:S(2)}, u32[]{:S(2)}) collective-permute-start(f32[73,2,132]{0,2,1:T(8,128)S(1)} %get-tuple-element.6), channel_id=1, source_target_pairs={{0,64},{64,128},{128,192},{192,256},{256,320},{320,384},{384,448},... | collective-permute-start | bytes 231272 | tf_op jit(solution)/shard_map/ppermute | solution.py:10
  22.1 18.8 %collective-permute-start.3 = (f32[73,2,132]{0,2,1:T(8,128)S(1)}, f32[73,2,132]{0,2,1:T(8,128)S(1)}, u32[]{:S(2)}, u32[]{:S(2)}) collective-permute-start(f32[73,2,132]{0,2,1:T(8,128)S(1)} %get-tuple-element.7), channel_id=1, source_target_pairs={{0,960},{64,0},{128,64},{192,128},{256,192},{320,256},{384,320},{4... | collective-permute-start | bytes 231272 | tf_op jit(solution)/shard_map/ppermute | solution.py:10
  42.0 2.6 %copy-start.7 = (f32[24,72]{1,0:T(8,128)S(1)}, f32[24,72]{1,0:T(8,128)}, u32[]{:S(2)}) copy-start(f32[24,72]{1,0:T(8,128)} %param.17) | copy-start | bytes 20740
  43.8 0.8 copy-start.3
  45.3 15.0 %collective-permute-start.5 = (bf16[24,16,64]{2,1,0:T(8,128)(2,1)S(1)}, bf16[24,16,64]{2,1,0:T(8,128)(2,1)S(1)}, u32[]{:S(2)}, u32[]{:S(2)}) collective-permute-start(bf16[24,16,64]{2,1,0:T(8,128)(2,1)S(1)} %reshape.76), channel_id=1, source_target_pairs={{0,1},{1,2},{2,3},{3,4},{4,5},{5,6},{6,7},{7,8},{8,9},{9,10},{10,1... | collective-permute-start | bytes 147464 | tf_op jit(solution)/shard_map/ppermute | solution.py:10
  52.8 7.9 %collective-permute-start.4 = (bf16[24,16,64]{2,1,0:T(8,128)(2,1)S(1)}, bf16[24,16,64]{2,1,0:T(8,128)(2,1)S(1)}, u32[]{:S(2)}, u32[]{:S(2)}) collective-permute-start(bf16[24,16,64]{2,1,0:T(8,128)(2,1)S(1)} %reshape.76), channel_id=1, source_target_pairs={{0,2},{1,3},{2,4},{3,5},{4,6},{5,7},{6,8},{7,9},{8,10},{9,11},{10,... | collective-permute-start | bytes 147464 | tf_op jit(solution)/shard_map/ppermute | solution.py:10
  54.7 10.1 %collective-permute-start.7 = (bf16[24,16,64]{2,1,0:T(8,128)(2,1)S(1)}, bf16[24,16,64]{2,1,0:T(8,128)(2,1)S(1)}, u32[]{:S(2)}, u32[]{:S(2)}) collective-permute-start(bf16[24,16,64]{2,1,0:T(8,128)(2,1)S(1)} %reshape.76), channel_id=1, source_target_pairs={{0,62},{1,63},{2,0},{3,1},{4,2},{5,3},{6,4},{7,5},{8,6},{9,7},{10,... | collective-permute-start | bytes 147464 | tf_op jit(solution)/shard_map/ppermute | solution.py:10
  58.1 10.2 %collective-permute-start.6 = (bf16[24,16,64]{2,1,0:T(8,128)(2,1)S(1)}, bf16[24,16,64]{2,1,0:T(8,128)(2,1)S(1)}, u32[]{:S(2)}, u32[]{:S(2)}) collective-permute-start(bf16[24,16,64]{2,1,0:T(8,128)(2,1)S(1)} %reshape.76), channel_id=1, source_target_pairs={{0,63},{1,0},{2,1},{3,2},{4,3},{5,4},{6,5},{7,6},{8,7},{9,8},{10,9... | collective-permute-start | bytes 147464 | tf_op jit(solution)/shard_map/ppermute | solution.py:10
  69.0 1.6 %copy-start.1 = (f32[80,2048]{1,0:T(8,128)S(1)}, f32[80,2048]{1,0:T(8,128)}, u32[]{:S(2)}) copy-start(f32[80,2048]{1,0:T(8,128)} %param.20) | copy-start | bytes 1966084
  69.0 1.6 %copy-start.6 = (f32[80,24]{0,1:T(8,128)S(1)}, f32[80,24]{0,1:T(8,128)}, u32[]{:S(2)}) copy-start(f32[80,24]{0,1:T(8,128)} %param.22) | copy-start | bytes 23044
  69.7 2.8 %copy-start.9 = (f32[8,80]{1,0:T(8,128)S(1)}, f32[8,80]{1,0:T(8,128)}, u32[]{:S(2)}) copy-start(f32[8,80]{1,0:T(8,128)} %param.24) | copy-start | bytes 7684
  69.7 13.8 %copy-start.15 = (s32[32]{0:T(128)S(1)}, s32[32]{0:T(128)}, u32[]{:S(2)}) copy-start(s32[32]{0:T(128)} %iota_add_fusion.2) | copy-start | bytes 388
  69.8 13.9 %copy-start.14 = (s32[32]{0:T(128)S(1)}, s32[32]{0:T(128)}, u32[]{:S(2)}) copy-start(s32[32]{0:T(128)} %iota_add_fusion.3) | copy-start | bytes 388
  70.6 15.7 %copy-start.13 = (s32[32]{0:T(128)S(1)}, s32[32]{0:T(128)}, u32[]{:S(2)}) copy-start(s32[32]{0:T(128)} %iota_add_fusion) | copy-start | bytes 388
  72.5 19.8 %copy-start.2 = (f32[80,2048]{1,0:T(8,128)}, f32[80,2048]{1,0:T(8,128)S(1)}, u32[]{:S(2)}) copy-start(f32[80,2048]{1,0:T(8,128)S(1)} %fusion.1) | copy-start | bytes 1966084
  72.5 17.8 %copy-start.16 = (s32[32]{0:T(128)S(1)}, s32[32]{0:T(128)}, u32[]{:S(2)}) copy-start(s32[32]{0:T(128)} %iota_add_fusion.1) | copy-start | bytes 388
  73.1 19.3 %copy-start.4 = (f32[72,8,128]{0,2,1:T(8,128)S(1)}, f32[72,8,128]{0,2,1:T(8,128)}, u32[]{:S(2)}) copy-start(f32[72,8,128]{0,2,1:T(8,128)} %copy-done.3) | copy-start | bytes 884740
  73.1 19.3 %copy-start.10 = (f32[72,8]{0,1:T(8,128)S(1)}, f32[72,8]{0,1:T(8,128)}, u32[]{:S(2)}) copy-start(f32[72,8]{0,1:T(8,128)} %param.27) | copy-start | bytes 6916
  73.1 10.6 %collective-permute-start.9 = (bf16[8,32,64]{2,1,0:T(8,128)(2,1)S(1)}, bf16[8,32,64]{2,1,0:T(8,128)(2,1)S(1)}, u32[]{:S(2)}, u32[]{:S(2)}) collective-permute-start(bf16[8,32,64]{2,1,0:T(8,128)(2,1)S(1)} %reshape.79), channel_id=1, source_target_pairs={{0,1},{1,2},{2,3},{3,4},{4,5},{5,6},{6,7},{7,8},{8,9},{9,10},{10,1... | collective-permute-start | bytes 98312 | tf_op jit(solution)/shard_map/ppermute | solution.py:10
  75.2 8.8 %collective-permute-start.8 = (bf16[8,32,64]{2,1,0:T(8,128)(2,1)S(1)}, bf16[8,32,64]{2,1,0:T(8,128)(2,1)S(1)}, u32[]{:S(2)}, u32[]{:S(2)}) collective-permute-start(bf16[8,32,64]{2,1,0:T(8,128)(2,1)S(1)} %reshape.79), channel_id=1, source_target_pairs={{0,2},{1,3},{2,4},{3,5},{4,6},{5,7},{6,8},{7,9},{8,10},{9,11},{10,... | collective-permute-start | bytes 98312 | tf_op jit(solution)/shard_map/ppermute | solution.py:10
  77.1 9.2 %collective-permute-start.11 = (bf16[8,32,64]{2,1,0:T(8,128)(2,1)S(1)}, bf16[8,32,64]{2,1,0:T(8,128)(2,1)S(1)}, u32[]{:S(2)}, u32[]{:S(2)}) collective-permute-start(bf16[8,32,64]{2,1,0:T(8,128)(2,1)S(1)} %reshape.79), channel_id=1, source_target_pairs={{0,62},{1,63},{2,0},{3,1},{4,2},{5,3},{6,4},{7,5},{8,6},{9,7},{10,... | collective-permute-start | bytes 98312 | tf_op jit(solution)/shard_map/ppermute | solution.py:10
  80.5 9.8 %collective-permute-start.10 = (bf16[8,32,64]{2,1,0:T(8,128)(2,1)S(1)}, bf16[8,32,64]{2,1,0:T(8,128)(2,1)S(1)}, u32[]{:S(2)}, u32[]{:S(2)}) collective-permute-start(bf16[8,32,64]{2,1,0:T(8,128)(2,1)S(1)} %reshape.79), channel_id=1, source_target_pairs={{0,63},{1,0},{2,1},{3,2},{4,3},{5,4},{6,5},{7,6},{8,7},{9,8},{10,9... | collective-permute-start | bytes 98312 | tf_op jit(solution)/shard_map/ppermute | solution.py:10

commit v3 on v2

--- a/solution.py
+++ b/solution.py
@@ -49,17 +49,32 @@
     return relative * per_tile + cols % per_tile
 
 
+def pick(local, base, piece, count):
+    ids = base + jnp.arange(count, dtype=local.dtype)
+    onehot = (local[:, None] == ids[None, :]).astype(piece.dtype)
+    return jnp.einsum("qb,fbj->fqj", onehot, piece, preferred_element_type=jnp.float32)
+
+
 def exchange_and_pick(blocks, cols, here):
     fields, per_tile, cells = blocks.shape
     tiles = lax.axis_size("tile")
     local = near_index(cols, per_tile, tiles, here).reshape(-1)
-    picked = None
-    for slot, offset in enumerate((-2, -1, 0, 1, 2)):
-        piece = blocks if offset == 0 else from_behind(blocks, "tile", -offset)
-        ids = slot * per_tile + jnp.arange(per_tile, dtype=local.dtype)
-        onehot = (local[:, None] == ids[None, :]).astype(blocks.dtype)
-        part = jnp.einsum("qb,fbj->fqj", onehot, piece, preferred_element_type=jnp.float32)
-        picked = part if picked is None else picked + part
+    behind = from_behind(blocks, "tile", 2)
+    ahead = from_behind(blocks, "tile", -2)
+    even = here % 2 == 0
+    forward = jnp.where(even, ahead, behind)
+    bundle = jnp.concatenate([blocks, forward], axis=1)
+    partner = lax.ppermute(bundle, "tile", [(s, s ^ 1) for s in range(tiles)])
+    plus_one = jnp.where(even, 0, per_tile)
+    minus_one = per_tile - plus_one
+    ids = jnp.arange(per_tile, dtype=local.dtype)
+    slot = local // per_tile
+    within = local % per_tile
+    partner_local = jnp.where(slot == 3, plus_one + within, jnp.where(slot == 1, minus_one + within, -1))
+    picked = pick(local, 2 * per_tile, blocks, per_tile)
+    picked = picked + pick(local, 0, behind, per_tile)
+    picked = picked + pick(local, 4 * per_tile, ahead, per_tile)
+    picked = picked + pick(partner_local, 0, partner, 2 * per_tile)
     return picked.astype(blocks.dtype).reshape((fields,) + cols.shape + (cells,))
 
 

time: 94.9 us -> 92.6 us (0.976)
  starting transfers between devices: 52.1 us -> 50.2 us
    ppermute x12 -> x8, starting transfers between devices: 52.1 us -> 37.8 us  [from_behind(): return lax.ppermute(value, axis, pairs)]
    ppermute x0 -> x2, starting transfers between devices: none -> 12.4 us  [exchange_and_pick(): partner = lax.ppermute(bundle, 'tile', [(s, s ^ 1) for s in range(tiles)])]
    ppermute x0 -> x2, waiting for transfers between devices: none -> 1.47 us  [exchange_and_pick(): partner = lax.ppermute(bundle, 'tile', [(s, s ^ 1) for s in range(tiles)])]
    add x8 -> x4, other arithmetic: 2.25 us -> 1 us  [pick(): ids = base + jnp.arange(count, dtype=local.dtype)]
    ppermute x12 -> x8, waiting for transfers between devices: 15.5 us -> 14.8 us  [from_behind(): return lax.ppermute(value, axis, pairs)]
    dot_general x10 -> x8, matrix products: 2.73 us -> 2.18 us  [pick(): jnp.einsum('qb,fbj->fqj', onehot, piece, preferred_element_type=jnp.float32)]
    unnamed x38 -> x36, local copies, waits for them, and re-layouts: 3.09 us -> 3.07 us
  transfers between devices with their start and end apart: 12 -> 10, of which waited for: 6 -> 6; matrix products, arithmetic and copies ran while one was open for 10% -> 8% of each run, Pallas kernels for 0% -> 0%
where the time goes in v3:
time: 92.6 us; the launch traced here: 92.1 us
  starting transfers between devices  50.2 us (54%)
  waiting for transfers between devices  16.3 us (18%)
  matrix products  12.9 us (14%)
  local copies, waits for them, and re-layouts  8.74 us (9%)
  other arithmetic  2.77 us (3%)
  between operations  1.19 us (1%)
    ppermute x8, starting transfers between devices, from_behind(): return lax.ppermute(value, axis, pairs)  37.8 us
    ppermute x8, waiting for transfers between devices, from_behind(): return lax.ppermute(value, axis, pairs)  14.8 us
    ppermute x2, starting transfers between devices, exchange_and_pick(): partner = lax.ppermute(bundle, 'tile', [(s, s ^ 1) for s in range(tiles)])  12.4 us
    dot_general x4, matrix products, level_mix(): jnp.einsum('ml,l...->m...', matrix, field, precision=lax.Precision.HIGHEST)  3.37 us
    unnamed x36, local copies, waits for them, and re-layouts  3.07 us
    dot_general x1, matrix products, body(): jnp.dot(ocean_mix, ocean_state, precision=lax.Precision.HIGHEST)  2.79 us
    dot_general x2, matrix products, block_product(): jnp.einsum('okij,fokj->foi', weights, picked, preferred_element_type=jnp....  2.22 us
    dot_general x8, matrix products, pick(): jnp.einsum('qb,fbj->fqj', onehot, piece, preferred_element_type=jnp.float32)  2.18 us
  transfers between devices with their start and end apart: 10, of which 6 were waited for; matrix products, arithmetic and copies ran while one was open for 8% of the time, Pallas kernels for 0%

profile of v3, /device:TPU:47, one launch (start us, length us, event | category | flops | bytes accessed | tf_op | source)
XLA Modules:
  0.0 92.1 jit_solution(6434027993127495888)
XLA Ops:
  0.7 1.3 %copy.27 = f32[72,8,128]{0,2,1:T(8,128)S(1)} copy(f32[72,8,128]{2,1,0:T(8,128)} %param.14) | data formatting | bytes 589824 | tf_op args[0]
  2.0 0.9 copy.28
  3.4 6.0 %collective-permute-start = (f32[1168]{0:T(1024)S(1)}, f32[1168]{0:T(1024)S(1)}, u32[]{:S(2)}, u32[]{:S(2)}) collective-permute-start(f32[1168]{0:T(1024)S(1)} %reshape.166), channel_id=1, source_target_pairs={{0,1},{1,2},{2,3},{3,4},{4,5},{5,6},{6,7},{7,8},{8,9},{9,10},{10,1... | collective-permute-start | bytes 14024 | tf_op jit(solution)/shard_map/ppermute | solution.py:10
  9.9 1.9 %collective-permute-start.1 = (f32[1168]{0:T(1024)S(1)}, f32[1168]{0:T(1024)S(1)}, u32[]{:S(2)}, u32[]{:S(2)}) collective-permute-start(f32[1168]{0:T(1024)S(1)} %reshape.168), channel_id=1, source_target_pairs={{0,63},{1,0},{2,1},{3,2},{4,3},{5,4},{6,5},{7,6},{8,7},{9,8},{10,9... | collective-permute-start | bytes 14024 | tf_op jit(solution)/shard_map/ppermute | solution.py:10
  12.1 0.6 broadcast_compare_fusion
  12.9 2.8 %convolution_add_fusion = f32[80,2048]{1,0:T(8,128)} fusion(f32[80,2048]{1,0:T(8,128)} %param.20, f32[80,80]{1,0:T(8,128)S(1)} %copy-done.5), kind=kOutput, calls=%fused_computation | convolution fusion | flops 157450240 | bytes 1336320 | tf_op jit(solution)/shard_map/dot_general | solution.py:111
  15.7 0.6 compare_select_fusion.1
  17.2 1.8 %collective-permute-done.1 = f32[1168]{0:T(1024)S(1)} collective-permute-done((f32[1168]{0:T(1024)S(1)}, f32[1168]{0:T(1024)S(1)}, u32[]{:S(2)}, u32[]{:S(2)}) %collective-permute-start.1) | collective-permute-done | bytes 4704 | tf_op jit(solution)/shard_map/ppermute | solution.py:10
  19.7 2.4 %collective-permute-start.2 = (f32[73,2,132]{0,2,1:T(8,128)S(1)}, f32[73,2,132]{0,2,1:T(8,128)S(1)}, u32[]{:S(2)}, u32[]{:S(2)}) collective-permute-start(f32[73,2,132]{0,2,1:T(8,128)S(1)} %get-tuple-element.6), channel_id=1, source_target_pairs={{0,64},{64,128},{128,192},{192,256},{256,320},{320,384},{384,448},... | collective-permute-start | bytes 231272 | tf_op jit(solution)/shard_map/ppermute | solution.py:10
  22.1 16.8 %collective-permute-start.3 = (f32[73,2,132]{0,2,1:T(8,128)S(1)}, f32[73,2,132]{0,2,1:T(8,128)S(1)}, u32[]{:S(2)}, u32[]{:S(2)}) collective-permute-start(f32[73,2,132]{0,2,1:T(8,128)S(1)} %get-tuple-element.7), channel_id=1, source_target_pairs={{0,960},{64,0},{128,64},{192,128},{256,192},{320,256},{384,320},{4... | collective-permute-start | bytes 231272 | tf_op jit(solution)/shard_map/ppermute | solution.py:10
  39.4 1.5 %collective-permute-done.3 = f32[73,2,132]{0,2,1:T(8,128)S(1)} collective-permute-done((f32[73,2,132]{0,2,1:T(8,128)S(1)}, f32[73,2,132]{0,2,1:T(8,128)S(1)}, u32[]{:S(2)}, u32[]{:S(2)}) %collective-permute-start.3) | collective-permute-done | bytes 77120 | tf_op jit(solution)/shard_map/ppermute | solution.py:10
  41.1 0.7 slice_reduce_fusion
  42.0 1.1 %fusion.15 = f32[72,10,130]{0,2,1:T(8,128)S(1)} fusion(f32[73,12,132]{0,2,1:T(8,128)S(1)} %pad_maximum_fusion, f32[73,2,132]{0,2,1:T(8,128)S(1)} %collective-permute-done.2, f32[73,8,2]{0,2,1:T(2,128)S(1)} %copy.32, f32[73,8,2]{0,2,1:T(2,128)S(1)} %copy.31, f32[1,8,128]{0,2,1:T(8,128)S(1)} %copy.28, f32[72,8,128]{0,2,1:T(8,128)S(1)} %copy.27, ...), kind=kOutput, calls=%fused_computation.31 | convolution fusion | flops 82368000 | bytes 4556416 | tf_op jit(solution)/shard_map/ml,l...->m.../dot_general | solution.py:32
  43.1 0.7 fusion.6
  43.8 0.8 copy-done.3
  44.6 0.6 fusion.11
  45.3 1.9 %collective-permute-start.4 = (bf16[24,16,64]{2,1,0:T(8,128)(2,1)S(1)}, bf16[24,16,64]{2,1,0:T(8,128)(2,1)S(1)}, u32[]{:S(2)}, u32[]{:S(2)}) collective-permute-start(bf16[24,16,64]{2,1,0:T(8,128)(2,1)S(1)} %reshape.170), channel_id=1, source_target_pairs={{0,2},{1,3},{2,4},{3,5},{4,6},{5,7},{6,8},{7,9},{8,10},{9,11},{10,... | collective-permute-start | bytes 147464 | tf_op jit(solution)/shard_map/ppermute | solution.py:10
  47.2 3.4 %collective-permute-start.5 = (bf16[24,16,64]{2,1,0:T(8,128)(2,1)S(1)}, bf16[24,16,64]{2,1,0:T(8,128)(2,1)S(1)}, u32[]{:S(2)}, u32[]{:S(2)}) collective-permute-start(bf16[24,16,64]{2,1,0:T(8,128)(2,1)S(1)} %reshape.170), channel_id=1, source_target_pairs={{0,62},{1,63},{2,0},{3,1},{4,2},{5,3},{6,4},{7,5},{8,6},{9,7},{10,... | collective-permute-start | bytes 147464 | tf_op jit(solution)/shard_map/ppermute | solution.py:10
  50.9 5.9 %collective-permute-done.5 = bf16[24,16,64]{2,1,0:T(8,128)(2,1)S(1)} collective-permute-done((bf16[24,16,64]{2,1,0:T(8,128)(2,1)S(1)}, bf16[24,16,64]{2,1,0:T(8,128)(2,1)S(1)}, u32[]{:S(2)}, u32[]{:S(2)}) %collective-permute-start.5) | collective-permute-done | bytes 49184 | tf_op jit(solution)/shard_map/ppermute | solution.py:10
  56.9 8.9 %collective-permute-start.6 = (bf16[24,32,64]{2,1,0:T(8,128)(2,1)S(1)}, bf16[24,32,64]{2,1,0:T(8,128)(2,1)S(1)}, u32[]{:S(2)}, u32[]{:S(2)}) collective-permute-start(bf16[24,32,64]{2,1,0:T(8,128)(2,1)S(1)} %pad_maximum_fusion.9), channel_id=1, source_target_pairs={{0,1},{1,0},{2,3},{3,2},{4,5},{5,4},{6,7},{7,6},{8,9},{9,8},{10,11... | collective-permute-start | bytes 294920 | tf_op jit(solution)/shard_map/ppermute | solution.py:67
  66.1 0.7 collective-permute-done.6
  68.0 0.6 convolution_bitcast_fusion.4
  68.7 0.8 reshape.172
  69.5 1.8 %fusion.1 = f32[80,2048]{1,0:T(8,128)S(1)} fusion(f32[80,2048]{1,0:T(8,128)S(1)} %copy-done.1, f32[80,2048]{1,0:T(8,128)} %convolution_add_fusion, f32[24,2048]{1,0:T(8,128)} %reshape.172, f32[80,24]{0,1:T(8,128)S(1)} %copy-done.6, pred[2048]{0:T(1024)(128)(4,1)} %broadcast_compare_fusion), kind=kOutput, calls=%fused_computation.3 | convolution fusion | flops 47513600 | bytes 2172416 | tf_op jit(solution)/shard_map/dot_general | solution.py:115
  72.0 2.1 %collective-permute-start.7 = (bf16[8,32,64]{2,1,0:T(8,128)(2,1)S(1)}, bf16[8,32,64]{2,1,0:T(8,128)(2,1)S(1)}, u32[]{:S(2)}, u32[]{:S(2)}) collective-permute-start(bf16[8,32,64]{2,1,0:T(8,128)(2,1)S(1)} %reshape.173), channel_id=1, source_target_pairs={{0,2},{1,3},{2,4},{3,5},{4,6},{5,7},{6,8},{7,9},{8,10},{9,11},{10,... | collective-permute-start | bytes 98312 | tf_op jit(solution)/shard_map/ppermute | solution.py:10
  74.1 3.4 %collective-permute-start.8 = (bf16[8,32,64]{2,1,0:T(8,128)(2,1)S(1)}, bf16[8,32,64]{2,1,0:T(8,128)(2,1)S(1)}, u32[]{:S(2)}, u32[]{:S(2)}) collective-permute-start(bf16[8,32,64]{2,1,0:T(8,128)(2,1)S(1)} %reshape.173), channel_id=1, source_target_pairs={{0,62},{1,63},{2,0},{3,1},{4,2},{5,3},{6,4},{7,5},{8,6},{9,7},{10,... | collective-permute-start | bytes 98312 | tf_op jit(solution)/shard_map/ppermute | solution.py:10
  77.7 5.6 %collective-permute-done.8 = bf16[8,32,64]{2,1,0:T(8,128)(2,1)S(1)} collective-permute-done((bf16[8,32,64]{2,1,0:T(8,128)(2,1)S(1)}, bf16[8,32,64]{2,1,0:T(8,128)(2,1)S(1)}, u32[]{:S(2)}, u32[]{:S(2)}) %collective-permute-start.8) | collective-permute-done | bytes 32800 | tf_op jit(solution)/shard_map/ppermute | solution.py:10
  83.4 3.4 %collective-permute-start.9 = (bf16[8,64,64]{2,1,0:T(8,128)(2,1)S(1)}, bf16[8,64,64]{2,1,0:T(8,128)(2,1)S(1)}, u32[]{:S(2)}, u32[]{:S(2)}) collective-permute-start(bf16[8,64,64]{2,1,0:T(8,128)(2,1)S(1)} %pad_maximum_fusion.14), channel_id=1, source_target_pairs={{0,1},{1,0},{2,3},{3,2},{4,5},{5,4},{6,7},{7,6},{8,9},{9,8},{10,11... | collective-permute-start | bytes 196616 | tf_op jit(solution)/shard_map/ppermute | solution.py:67
  87.0 0.7 collective-permute-done.9
  88.4 1.6 %convolution_bitcast_fusion.5 = f32[8,16,64]{2,0,1:T(8,128)S(1)} fusion(bf16[8,16,4,64]{3,0,2,1:T(8,128)(2,1)S(1)} %bitcast.94, bf16[16,4,64,64]{3,2,1,0:T(8,128)(2,1)} %param.25), kind=kOutput, calls=%fused_computation.23 | convolution fusion | flops 4194304 | bytes 622592 | tf_op jit(solution)/shard_map/okij,fokj->foi/dot_general | solution.py:44
  90.2 1.0 %fusion.5 = f32[72,8,128]{0,2,1:T(8,128)S(1)} fusion(f32[72,8,128]{0,2,1:T(8,128)S(1)} %copy-done.4, f32[8,8,128]{2,1,0:T(8,128)S(1)} %reshape.175, f32[72,8]{0,1:T(8,128)S(1)} %copy-done.10), kind=kOutput, calls=%fused_computation.12 | convolution fusion | flops 7151616 | bytes 624896 | tf_op jit(solution)/shard_map/ml,l...->m.../dot_general | solution.py:32
  91.2 0.9 copy.46
  (82 shorter events, 7.6 us)
Async XLA Ops:
  0.6 67.3 %copy-start = (bf16[32,4,64,64]{3,2,1,0:T(8,128)(2,1)S(1)}, bf16[32,4,64,64]{3,2,1,0:T(8,128)(2,1)}, u32[]{:S(2)}) copy-start(bf16[32,4,64,64]{3,2,1,0:T(8,128)(2,1)} %param.18) | copy-start | bytes 3145732
  0.6 11.2 %copy-start.12 = (s32[32,4]{0,1:T(4,128)S(1)}, s32[32,4]{0,1:T(4,128)}, u32[]{:S(2)}) copy-start(s32[32,4]{0,1:T(4,128)} %param.19) | copy-start | bytes 1540
  0.7 11.4 %copy-start.8 = (s32[2048]{0:T(1024)S(1)}, s32[2048]{0:T(1024)}, u32[]{:S(2)}) copy-start(s32[2048]{0:T(1024)} %param.23) | copy-start | bytes 24580
  0.7 12.0 %copy-start.13 = (s32[16,4]{0,1:T(4,128)S(1)}, s32[16,4]{0,1:T(4,128)}, u32[]{:S(2)}) copy-start(s32[16,4]{0,1:T(4,128)} %param.26) | copy-start | bytes 772
  0.7 12.2 %copy-start.5 = (f32[80,80]{1,0:T(8,128)S(1)}, f32[80,80]{1,0:T(8,128)}, u32[]{:S(2)}) copy-start(f32[80,80]{1,0:T(8,128)} %param.21) | copy-start | bytes 76804
  3.4 13.4 %collective-permute-start = (f32[1168]{0:T(1024)S(1)}, f32[1168]{0:T(1024)S(1)}, u32[]{:S(2)}, u32[]{:S(2)}) collective-permute-start(f32[1168]{0:T(1024)S(1)} %reshape.166), channel_id=1, source_target_pairs={{0,1},{1,2},{2,3},{3,4},{4,5},{5,6},{6,7},{7,8},{8,9},{9,10},{10,1... | collective-permute-start | bytes 14024 | tf_op jit(solution)/shard_map/ppermute | solution.py:10
  9.9 9.2 %collective-permute-start.1 = (f32[1168]{0:T(1024)S(1)}, f32[1168]{0:T(1024)S(1)}, u32[]{:S(2)}, u32[]{:S(2)}) collective-permute-start(f32[1168]{0:T(1024)S(1)} %reshape.168), channel_id=1, source_target_pairs={{0,63},{1,0},{2,1},{3,2},{4,3},{5,4},{6,5},{7,6},{8,7},{9,8},{10,9... | collective-permute-start | bytes 14024 | tf_op jit(solution)/shard_map/ppermute | solution.py:10
  19.5 22.5 %copy-start.16 = (f32[72,72]{1,0:T(8,128)S(1)}, f32[72,72]{1,0:T(8,128)}, u32[]{:S(2)}) copy-start(f32[72,72]{1,0:T(8,128)} %param.16) | copy-start | bytes 62212
  19.7 19.7 %collective-permute-start.2 = (f32[73,2,132]{0,2,1:T(8,128)S(1)}, f32[73,2,132]{0,2,1:T(8,128)S(1)}, u32[]{:S(2)}, u32[]{:S(2)}) collective-permute-start(f32[73,2,132]{0,2,1:T(8,128)S(1)} %get-tuple-element.6), channel_id=1, source_target_pairs={{0,64},{64,128},{128,192},{192,256},{256,320},{320,384},{384,448},... | collective-permute-start | bytes 231272 | tf_op jit(solution)/shard_map/ppermute | solution.py:10
  22.1 18.8 %collective-permute-start.3 = (f32[73,2,132]{0,2,1:T(8,128)S(1)}, f32[73,2,132]{0,2,1:T(8,128)S(1)}, u32[]{:S(2)}, u32[]{:S(2)}) collective-permute-start(f32[73,2,132]{0,2,1:T(8,128)S(1)} %get-tuple-element.7), channel_id=1, source_target_pairs={{0,960},{64,0},{128,64},{192,128},{256,192},{320,256},{384,320},{4... | collective-permute-start | bytes 231272 | tf_op jit(solution)/shard_map/ppermute | solution.py:10
  42.0 2.6 %copy-start.7 = (f32[24,72]{1,0:T(8,128)S(1)}, f32[24,72]{1,0:T(8,128)}, u32[]{:S(2)}) copy-start(f32[24,72]{1,0:T(8,128)} %param.17) | copy-start | bytes 20740
  43.8 0.8 copy-start.3
  45.3 5.6 %collective-permute-start.4 = (bf16[24,16,64]{2,1,0:T(8,128)(2,1)S(1)}, bf16[24,16,64]{2,1,0:T(8,128)(2,1)S(1)}, u32[]{:S(2)}, u32[]{:S(2)}) collective-permute-start(bf16[24,16,64]{2,1,0:T(8,128)(2,1)S(1)} %reshape.170), channel_id=1, source_target_pairs={{0,2},{1,3},{2,4},{3,5},{4,6},{5,7},{6,8},{7,9},{8,10},{9,11},{10,... | collective-permute-start | bytes 147464 | tf_op jit(solution)/shard_map/ppermute | solution.py:10
  47.2 9.6 %collective-permute-start.5 = (bf16[24,16,64]{2,1,0:T(8,128)(2,1)S(1)}, bf16[24,16,64]{2,1,0:T(8,128)(2,1)S(1)}, u32[]{:S(2)}, u32[]{:S(2)}) collective-permute-start(bf16[24,16,64]{2,1,0:T(8,128)(2,1)S(1)} %reshape.170), channel_id=1, source_target_pairs={{0,62},{1,63},{2,0},{3,1},{4,2},{5,3},{6,4},{7,5},{8,6},{9,7},{10,... | collective-permute-start | bytes 147464 | tf_op jit(solution)/shard_map/ppermute | solution.py:10
  56.9 10.0 %collective-permute-start.6 = (bf16[24,32,64]{2,1,0:T(8,128)(2,1)S(1)}, bf16[24,32,64]{2,1,0:T(8,128)(2,1)S(1)}, u32[]{:S(2)}, u32[]{:S(2)}) collective-permute-start(bf16[24,32,64]{2,1,0:T(8,128)(2,1)S(1)} %pad_maximum_fusion.9), channel_id=1, source_target_pairs={{0,1},{1,0},{2,3},{3,2},{4,5},{5,4},{6,7},{7,6},{8,9},{9,8},{10,11... | collective-permute-start | bytes 294920 | tf_op jit(solution)/shard_map/ppermute | solution.py:67
  67.9 1.6 %copy-start.1 = (f32[80,2048]{1,0:T(8,128)S(1)}, f32[80,2048]{1,0:T(8,128)}, u32[]{:S(2)}) copy-start(f32[80,2048]{1,0:T(8,128)} %param.20) | copy-start | bytes 1966084
  68.0 1.6 %copy-start.6 = (f32[80,24]{0,1:T(8,128)S(1)}, f32[80,24]{0,1:T(8,128)}, u32[]{:S(2)}) copy-start(f32[80,24]{0,1:T(8,128)} %param.22) | copy-start | bytes 23044
  68.6 2.8 %copy-start.9 = (f32[8,80]{1,0:T(8,128)S(1)}, f32[8,80]{1,0:T(8,128)}, u32[]{:S(2)}) copy-start(f32[8,80]{1,0:T(8,128)} %param.24) | copy-start | bytes 7684
  68.6 8.9 %copy-start.14 = (s32[32]{0:T(128)S(1)}, s32[32]{0:T(128)}, u32[]{:S(2)}) copy-start(s32[32]{0:T(128)} %iota_add_fusion.1) | copy-start | bytes 388
  69.5 18.2 %copy-start.11 = (s32[64]{0:T(128)S(1)}, s32[64]{0:T(128)}, u32[]{:S(2)}) copy-start(s32[64]{0:T(128)} %compare_select_fusion.1) | copy-start | bytes 772
  71.4 18.6 %copy-start.2 = (f32[80,2048]{1,0:T(8,128)}, f32[80,2048]{1,0:T(8,128)S(1)}, u32[]{:S(2)}) copy-start(f32[80,2048]{1,0:T(8,128)S(1)} %fusion.1) | copy-start | bytes 1966084
  71.4 16.6 %copy-start.15 = (s32[32]{0:T(128)S(1)}, s32[32]{0:T(128)}, u32[]{:S(2)}) copy-start(s32[32]{0:T(128)} %iota_add_fusion) | copy-start | bytes 388
  72.0 18.1 %copy-start.4 = (f32[72,8,128]{0,2,1:T(8,128)S(1)}, f32[72,8,128]{0,2,1:T(8,128)}, u32[]{:S(2)}) copy-start(f32[72,8,128]{0,2,1:T(8,128)} %copy-done.3) | copy-start | bytes 884740
  72.0 18.1 %copy-start.10 = (f32[72,8]{0,1:T(8,128)S(1)}, f32[72,8]{0,1:T(8,128)}, u32[]{:S(2)}) copy-start(f32[72,8]{0,1:T(8,128)} %param.27) | copy-start | bytes 6916
  72.0 5.7 %collective-permute-start.7 = (bf16[8,32,64]{2,1,0:T(8,128)(2,1)S(1)}, bf16[8,32,64]{2,1,0:T(8,128)(2,1)S(1)}, u32[]{:S(2)}, u32[]{:S(2)}) collective-permute-start(bf16[8,32,64]{2,1,0:T(8,128)(2,1)S(1)} %reshape.173), channel_id=1, source_target_pairs={{0,2},{1,3},{2,4},{3,5},{4,6},{5,7},{6,8},{7,9},{8,10},{9,11},{10,... | collective-permute-start | bytes 98312 | tf_op jit(solution)/shard_map/ppermute | solution.py:10
  74.1 9.2 %collective-permute-start.8 = (bf16[8,32,64]{2,1,0:T(8,128)(2,1)S(1)}, bf16[8,32,64]{2,1,0:T(8,128)(2,1)S(1)}, u32[]{:S(2)}, u32[]{:S(2)}) collective-permute-start(bf16[8,32,64]{2,1,0:T(8,128)(2,1)S(1)} %reshape.173), channel_id=1, source_target_pairs={{0,62},{1,63},{2,0},{3,1},{4,2},{5,3},{6,4},{7,5},{8,6},{9,7},{10,... | collective-permute-start | bytes 98312 | tf_op jit(solution)/shard_map/ppermute | solution.py:10
  83.4 4.4 %collective-permute-start.9 = (bf16[8,64,64]{2,1,0:T(8,128)(2,1)S(1)}, bf16[8,64,64]{2,1,0:T(8,128)(2,1)S(1)}, u32[]{:S(2)}, u32[]{:S(2)}) collective-permute-start(bf16[8,64,64]{2,1,0:T(8,128)(2,1)S(1)} %pad_maximum_fusion.14), channel_id=1, source_target_pairs={{0,1},{1,0},{2,3},{3,2},{4,5},{5,4},{6,7},{7,6},{8,9},{9,8},{10,11... | collective-permute-start | bytes 196616 | tf_op jit(solution)/shard_map/ppermute | solution.py:67

commit v4 on v3

--- a/solution.py
+++ b/solution.py
@@ -10,21 +10,38 @@
     return lax.ppermute(value, axis, pairs)
 
 
+def swap(value, axis, stride, phase):
+    count = lax.axis_size(axis)
+    groups = count // stride
+    pairs = []
+    for source in range(count):
+        group = source // stride
+        step = 1 if group % 2 == phase else -1
+        pairs.append((source, ((group + step) % groups) * stride + source % stride))
+    return lax.ppermute(value, axis, pairs)
+
+
 def halo_cols(cells, width):
     levels, rows, cols = cells.shape
+    even = lax.axis_index("tile") % 2 == 0
     head = cells[:, :, :width].reshape(-1)
     tail = cells[:, :, cols - width:].reshape(-1)
-    left = from_behind(tail, "tile", 1).reshape(levels, rows, width)
-    right = from_behind(head, "tile", -1).reshape(levels, rows, width)
+    partner = swap(jnp.where(even, tail, head), "tile", 1, 0)
+    cross = swap(jnp.where(even, head, tail), "tile", 1, 1)
+    left = jnp.where(even, cross, partner).reshape(levels, rows, width)
+    right = jnp.where(even, partner, cross).reshape(levels, rows, width)
     return jnp.concatenate([left, cells, right], axis=2)
 
 
 def halo_rows(cells, width):
     levels, rows, cols = cells.shape
+    even = lax.axis_index("comp") % 2 == 0
     head = cells[:, :width, :]
     tail = cells[:, rows - width:, :]
-    up = from_behind(tail, "comp", 1)
-    down = from_behind(head, "comp", -1)
+    first = swap(jnp.where(even, tail, head), "comp", 1, 0)
+    second = swap(jnp.where(even, head, tail), "comp", 1, 1)
+    up = jnp.where(even, second, first)
+    down = jnp.where(even, first, second)
     return jnp.concatenate([up, cells, down], axis=1)
 
 
@@ -59,21 +76,23 @@
     fields, per_tile, cells = blocks.shape
     tiles = lax.axis_size("tile")
     local = near_index(cols, per_tile, tiles, here).reshape(-1)
-    behind = from_behind(blocks, "tile", 2)
-    ahead = from_behind(blocks, "tile", -2)
     even = here % 2 == 0
-    forward = jnp.where(even, ahead, behind)
+    chip_even = (here // 2) % 2 == 0
+    first = swap(blocks, "tile", 2, 0)
+    second = swap(blocks, "tile", 2, 1)
+    first_base = jnp.where(chip_even, 4 * per_tile, 0)
+    second_base = 4 * per_tile - first_base
+    forward = jnp.where(even == chip_even, first, second)
     bundle = jnp.concatenate([blocks, forward], axis=1)
-    partner = lax.ppermute(bundle, "tile", [(s, s ^ 1) for s in range(tiles)])
+    partner = swap(bundle, "tile", 1, 0)
     plus_one = jnp.where(even, 0, per_tile)
     minus_one = per_tile - plus_one
-    ids = jnp.arange(per_tile, dtype=local.dtype)
     slot = local // per_tile
     within = local % per_tile
     partner_local = jnp.where(slot == 3, plus_one + within, jnp.where(slot == 1, minus_one + within, -1))
     picked = pick(local, 2 * per_tile, blocks, per_tile)
-    picked = picked + pick(local, 0, behind, per_tile)
-    picked = picked + pick(local, 4 * per_tile, ahead, per_tile)
+    picked = picked + pick(local, first_base, first, per_tile)
+    picked = picked + pick(local, second_base, second, per_tile)
     picked = picked + pick(partner_local, 0, partner, 2 * per_tile)
     return picked.astype(blocks.dtype).reshape((fields,) + cols.shape + (cells,))
 

time: 92.6 us -> 92.4 us (level)
  the two profiles are of different devices: /device:TPU:47 before, /device:TPU:1 now
where the time goes in v4:
time: 92.4 us; the launch traced here: 91.8 us
  starting transfers between devices  57.4 us (62%)
  matrix products  14.1 us (15%)
  waiting for transfers between devices  8.34 us (9%)
  local copies, waits for them, and re-layouts  7.28 us (8%)
  other arithmetic  3.39 us (4%)
  between operations  1.28 us (1%)
    ppermute x10, starting transfers between devices, swap(): return lax.ppermute(value, axis, pairs)  57.4 us
    ppermute x10, waiting for transfers between devices, swap(): return lax.ppermute(value, axis, pairs)  8.34 us
    dot_general x4, matrix products, level_mix(): jnp.einsum('ml,l...->m...', matrix, field, precision=lax.Precision.HIGHEST)  4.38 us
    dot_general x1, matrix products, body(): jnp.dot(ocean_mix, ocean_state, precision=lax.Precision.HIGHEST)  2.79 us
    add x6, other arithmetic, pick(): ids = base + jnp.arange(count, dtype=local.dtype)  2.71 us
    unnamed x36, local copies, waits for them, and re-layouts  2.29 us
    dot_general x8, matrix products, pick(): jnp.einsum('qb,fbj->fqj', onehot, piece, preferred_element_type=jnp.float32)  2.24 us
    dot_general x2, matrix products, block_product(): jnp.einsum('okij,fokj->foi', weights, picked, preferred_element_type=jnp....  2.22 us
  transfers between devices with their start and end apart: 10, of which 5 were waited for; matrix products, arithmetic and copies ran while one was open for 8% of the time, Pallas kernels for 0%

profile of v4, /device:TPU:1, one launch (start us, length us, event | category | flops | bytes accessed | tf_op | source)
XLA Modules:
  0.0 91.8 jit_solution(18363447208813843188)
XLA Ops:
  0.7 1.3 %copy.27 = f32[72,8,128]{0,2,1:T(8,128)S(1)} copy(f32[72,8,128]{2,1,0:T(8,128)} %param.14) | data formatting | bytes 589824 | tf_op args[0]
  2.0 0.9 copy.28
  3.5 16.1 %collective-permute-start.1 = (f32[1168]{0:T(1024)S(1)}, f32[1168]{0:T(1024)S(1)}, u32[]{:S(2)}, u32[]{:S(2)}) collective-permute-start(f32[1168]{0:T(1024)S(1)} %select_n.213), channel_id=1, source_target_pairs={{0,1},{1,0},{2,3},{3,2},{4,5},{5,4},{6,7},{7,6},{8,9},{9,8},{10,11... | collective-permute-start | bytes 14024 | tf_op jit(solution)/shard_map/ppermute | solution.py:21
  19.9 1.9 %collective-permute-start = (f32[1168]{0:T(1024)S(1)}, f32[1168]{0:T(1024)S(1)}, u32[]{:S(2)}, u32[]{:S(2)}) collective-permute-start(f32[1168]{0:T(1024)S(1)} %select_n.211), channel_id=1, source_target_pairs={{0,63},{1,2},{2,1},{3,4},{4,3},{5,6},{6,5},{7,8},{8,7},{9,10},{10,... | collective-permute-start | bytes 14024 | tf_op jit(solution)/shard_map/ppermute | solution.py:21
  21.9 0.5 iota_add_fusion.4
  22.4 0.5 iota_add_fusion.2
  23.1 0.6 iota_add_fusion.3
  24.0 2.8 %convolution_add_fusion = f32[80,2048]{1,0:T(8,128)} fusion(f32[80,2048]{1,0:T(8,128)} %param.20, f32[80,80]{1,0:T(8,128)S(1)} %copy-done.3), kind=kOutput, calls=%fused_computation | convolution fusion | flops 157450240 | bytes 1336320 | tf_op jit(solution)/shard_map/dot_general | solution.py:130
  26.8 0.5 iota_add_fusion.1
  28.4 1.9 %collective-permute-start.3 = (f32[73,2,132]{0,2,1:T(8,128)S(1)}, f32[73,2,132]{0,2,1:T(8,128)S(1)}, u32[]{:S(2)}, u32[]{:S(2)}) collective-permute-start(f32[73,2,132]{0,2,1:T(8,128)S(1)} %broadcast_select_fusion.3), channel_id=1, source_target_pairs={{0,64},{64,0},{128,192},{192,128},{256,320},{320,256},{384,448},{4... | collective-permute-start | bytes 231272 | tf_op jit(solution)/shard_map/ppermute | solution.py:21
  30.3 6.7 %collective-permute-start.2 = (f32[73,2,132]{0,2,1:T(8,128)S(1)}, f32[73,2,132]{0,2,1:T(8,128)S(1)}, u32[]{:S(2)}, u32[]{:S(2)}) collective-permute-start(f32[73,2,132]{0,2,1:T(8,128)S(1)} %get-tuple-element.6), channel_id=1, source_target_pairs={{0,960},{64,128},{128,64},{192,256},{256,192},{320,384},{384,320},... | collective-permute-start | bytes 231272 | tf_op jit(solution)/shard_map/ppermute | solution.py:21
  37.0 0.6 iota_add_fusion
  37.6 1.8 %collective-permute-done.2 = f32[73,2,132]{0,2,1:T(8,128)S(1)} collective-permute-done((f32[73,2,132]{0,2,1:T(8,128)S(1)}, f32[73,2,132]{0,2,1:T(8,128)S(1)}, u32[]{:S(2)}, u32[]{:S(2)}) %collective-permute-start.2) | collective-permute-done | bytes 77120 | tf_op jit(solution)/shard_map/ppermute | solution.py:21
  39.7 0.7 slice_reduce_fusion
  40.6 1.1 %fusion.15 = f32[72,10,130]{0,2,1:T(8,128)S(1)} fusion(f32[73,12,132]{0,2,1:T(8,128)S(1)} %pad_maximum_fusion, f32[73,2,132]{0,2,1:T(8,128)S(1)} %get-tuple-element.12, f32[73,8,2]{0,2,1:T(2,128)S(1)} %copy.32, f32[73,8,2]{0,2,1:T(2,128)S(1)} %copy.31, f32[1,8,128]{0,2,1:T(8,128)S(1)} %copy.28, f32[72,8,128]{0,2,1:T(8,128)S(1)} %copy.27, ...), kind=kOutput, calls=%fused_computation.31 | convolution fusion | flops 82368000 | bytes 4556416 | tf_op jit(solution)/shard_map/ml,l...->m.../dot_general | solution.py:49
  41.6 0.7 fusion.6
  42.4 0.6 fusion.11
  43.1 6.0 %collective-permute-start.4 = (bf16[24,16,64]{2,1,0:T(8,128)(2,1)S(1)}, bf16[24,16,64]{2,1,0:T(8,128)(2,1)S(1)}, u32[]{:S(2)}, u32[]{:S(2)}) collective-permute-start(bf16[24,16,64]{2,1,0:T(8,128)(2,1)S(1)} %reshape.176), channel_id=1, source_target_pairs={{0,2},{1,3},{2,0},{3,1},{4,6},{5,7},{6,4},{7,5},{8,10},{9,11},{10,... | collective-permute-start | bytes 147464 | tf_op jit(solution)/shard_map/ppermute | solution.py:21
  49.1 8.2 %collective-permute-start.5 = (bf16[24,16,64]{2,1,0:T(8,128)(2,1)S(1)}, bf16[24,16,64]{2,1,0:T(8,128)(2,1)S(1)}, u32[]{:S(2)}, u32[]{:S(2)}) collective-permute-start(bf16[24,16,64]{2,1,0:T(8,128)(2,1)S(1)} %reshape.176), channel_id=1, source_target_pairs={{0,62},{1,63},{2,4},{3,5},{4,2},{5,3},{6,8},{7,9},{8,6},{9,7},{10,... | collective-permute-start | bytes 147464 | tf_op jit(solution)/shard_map/ppermute | solution.py:21
  57.6 1.7 %collective-permute-done.5 = bf16[24,16,64]{2,1,0:T(8,128)(2,1)S(1)} collective-permute-done((bf16[24,16,64]{2,1,0:T(8,128)(2,1)S(1)}, bf16[24,16,64]{2,1,0:T(8,128)(2,1)S(1)}, u32[]{:S(2)}, u32[]{:S(2)}) %collective-permute-start.5) | collective-permute-done | bytes 49184 | tf_op jit(solution)/shard_map/ppermute | solution.py:21
  59.3 5.8 %collective-permute-start.6 = (bf16[24,32,64]{2,1,0:T(8,128)(2,1)S(1)}, bf16[24,32,64]{2,1,0:T(8,128)(2,1)S(1)}, u32[]{:S(2)}, u32[]{:S(2)}) collective-permute-start(bf16[24,32,64]{2,1,0:T(8,128)(2,1)S(1)} %pad_maximum_fusion.9), channel_id=1, source_target_pairs={{0,1},{1,0},{2,3},{3,2},{4,5},{5,4},{6,7},{7,6},{8,9},{9,8},{10,11... | collective-permute-start | bytes 294920 | tf_op jit(solution)/shard_map/ppermute | solution.py:21
  65.5 0.7 collective-permute-done.6
  67.3 0.6 convolution_bitcast_fusion.4
  68.2 2.0 %fusion.1 = f32[80,2048]{1,0:T(8,128)S(1)} fusion(f32[80,2048]{1,0:T(8,128)} %param.20, f32[80,2048]{1,0:T(8,128)} %convolution_add_fusion, f32[24,2048]{1,0:T(8,128)S(1)} %reshape.178, f32[80,24]{0,1:T(8,128)S(1)} %copy-done.4, pred[2048]{0:T(1024)(128)(4,1)S(1)} %broadcast_compare_fusion), kind=kOutput, calls=%fused_computation.3 | convolution fusion | flops 47513600 | bytes 2172416 | tf_op jit(solution)/shard_map/dot_general | solution.py:134
  70.9 1.9 %collective-permute-start.7 = (bf16[8,32,64]{2,1,0:T(8,128)(2,1)S(1)}, bf16[8,32,64]{2,1,0:T(8,128)(2,1)S(1)}, u32[]{:S(2)}, u32[]{:S(2)}) collective-permute-start(bf16[8,32,64]{2,1,0:T(8,128)(2,1)S(1)} %reshape.179), channel_id=1, source_target_pairs={{0,2},{1,3},{2,0},{3,1},{4,6},{5,7},{6,4},{7,5},{8,10},{9,11},{10,... | collective-permute-start | bytes 98312 | tf_op jit(solution)/shard_map/ppermute | solution.py:21
  72.8 5.5 %collective-permute-start.8 = (bf16[8,32,64]{2,1,0:T(8,128)(2,1)S(1)}, bf16[8,32,64]{2,1,0:T(8,128)(2,1)S(1)}, u32[]{:S(2)}, u32[]{:S(2)}) collective-permute-start(bf16[8,32,64]{2,1,0:T(8,128)(2,1)S(1)} %reshape.179), channel_id=1, source_target_pairs={{0,62},{1,63},{2,4},{3,5},{4,2},{5,3},{6,8},{7,9},{8,6},{9,7},{10,... | collective-permute-start | bytes 98312 | tf_op jit(solution)/shard_map/ppermute | solution.py:21
  78.6 3.4 %collective-permute-done.8 = bf16[8,32,64]{2,1,0:T(8,128)(2,1)S(1)} collective-permute-done((bf16[8,32,64]{2,1,0:T(8,128)(2,1)S(1)}, bf16[8,32,64]{2,1,0:T(8,128)(2,1)S(1)}, u32[]{:S(2)}, u32[]{:S(2)}) %collective-permute-start.8) | collective-permute-done | bytes 32800 | tf_op jit(solution)/shard_map/ppermute | solution.py:21
  82.1 3.4 %collective-permute-start.9 = (bf16[8,64,64]{2,1,0:T(8,128)(2,1)S(1)}, bf16[8,64,64]{2,1,0:T(8,128)(2,1)S(1)}, u32[]{:S(2)}, u32[]{:S(2)}) collective-permute-start(bf16[8,64,64]{2,1,0:T(8,128)(2,1)S(1)} %pad_maximum_fusion.14), channel_id=1, source_target_pairs={{0,1},{1,0},{2,3},{3,2},{4,5},{5,4},{6,7},{7,6},{8,9},{9,8},{10,11... | collective-permute-start | bytes 196616 | tf_op jit(solution)/shard_map/ppermute | solution.py:21
  85.8 0.7 collective-permute-done.9
  87.1 1.6 %convolution_bitcast_fusion.5 = f32[8,16,64]{2,0,1:T(8,128)S(1)} fusion(bf16[8,16,4,64]{3,0,2,1:T(8,128)(2,1)S(1)} %bitcast.97, bf16[16,4,64,64]{3,2,1,0:T(8,128)(2,1)} %param.25), kind=kOutput, calls=%fused_computation.23 | convolution fusion | flops 4194304 | bytes 622592 | tf_op jit(solution)/shard_map/okij,fokj->foi/dot_general | solution.py:61
  88.9 2.0 %fusion.5 = f32[72,8,128]{0,2,1:T(8,128)S(1)} fusion(f32[72,8,128]{0,2,1:T(8,128)} %copy-done.2, f32[8,8,128]{2,1,0:T(8,128)S(1)} %reshape.181, f32[72,8]{0,1:T(8,128)S(1)} %copy-done.8), kind=kOutput, calls=%fused_computation.12 | convolution fusion | flops 7151616 | bytes 624896 | tf_op jit(solution)/shard_map/ml,l...->m.../dot_general | solution.py:49
  90.9 0.9 copy.46
  (88 shorter events, 6.8 us)
Async XLA Ops:
  0.6 66.7 %copy-start = (bf16[32,4,64,64]{3,2,1,0:T(8,128)(2,1)S(1)}, bf16[32,4,64,64]{3,2,1,0:T(8,128)(2,1)}, u32[]{:S(2)}) copy-start(bf16[32,4,64,64]{3,2,1,0:T(8,128)(2,1)} %param.18) | copy-start | bytes 3145732
  0.6 22.3 %copy-start.9 = (s32[32,4]{0,1:T(4,128)S(1)}, s32[32,4]{0,1:T(4,128)}, u32[]{:S(2)}) copy-start(s32[32,4]{0,1:T(4,128)} %param.19) | copy-start | bytes 1540
  0.7 23.1 %copy-start.6 = (s32[2048]{0:T(1024)S(1)}, s32[2048]{0:T(1024)}, u32[]{:S(2)}) copy-start(s32[2048]{0:T(1024)} %param.23) | copy-start | bytes 24580
  0.7 23.1 %copy-start.10 = (s32[16,4]{0,1:T(4,128)S(1)}, s32[16,4]{0,1:T(4,128)}, u32[]{:S(2)}) copy-start(s32[16,4]{0,1:T(4,128)} %param.26) | copy-start | bytes 772
  0.7 23.3 %copy-start.3 = (f32[80,80]{1,0:T(8,128)S(1)}, f32[80,80]{1,0:T(8,128)}, u32[]{:S(2)}) copy-start(f32[80,80]{1,0:T(8,128)} %param.21) | copy-start | bytes 76804
  3.5 23.9 %collective-permute-start.1 = (f32[1168]{0:T(1024)S(1)}, f32[1168]{0:T(1024)S(1)}, u32[]{:S(2)}, u32[]{:S(2)}) collective-permute-start(f32[1168]{0:T(1024)S(1)} %select_n.213), channel_id=1, source_target_pairs={{0,1},{1,0},{2,3},{3,2},{4,5},{5,4},{6,7},{7,6},{8,9},{9,8},{10,11... | collective-permute-start | bytes 14024 | tf_op jit(solution)/shard_map/ppermute | solution.py:21
  19.9 7.4 %collective-permute-start = (f32[1168]{0:T(1024)S(1)}, f32[1168]{0:T(1024)S(1)}, u32[]{:S(2)}, u32[]{:S(2)}) collective-permute-start(f32[1168]{0:T(1024)S(1)} %select_n.211), channel_id=1, source_target_pairs={{0,63},{1,2},{2,1},{3,4},{4,3},{5,6},{6,5},{7,8},{8,7},{9,10},{10,... | collective-permute-start | bytes 14024 | tf_op jit(solution)/shard_map/ppermute | solution.py:21
  28.4 12.2 %copy-start.16 = (f32[72,72]{1,0:T(8,128)S(1)}, f32[72,72]{1,0:T(8,128)}, u32[]{:S(2)}) copy-start(f32[72,72]{1,0:T(8,128)} %param.16) | copy-start | bytes 62212
  28.4 9.2 %collective-permute-start.3 = (f32[73,2,132]{0,2,1:T(8,128)S(1)}, f32[73,2,132]{0,2,1:T(8,128)S(1)}, u32[]{:S(2)}, u32[]{:S(2)}) collective-permute-start(f32[73,2,132]{0,2,1:T(8,128)S(1)} %broadcast_select_fusion.3), channel_id=1, source_target_pairs={{0,64},{64,0},{128,192},{192,128},{256,320},{320,256},{384,448},{4... | collective-permute-start | bytes 231272 | tf_op jit(solution)/shard_map/ppermute | solution.py:21
  30.3 9.1 %collective-permute-start.2 = (f32[73,2,132]{0,2,1:T(8,128)S(1)}, f32[73,2,132]{0,2,1:T(8,128)S(1)}, u32[]{:S(2)}, u32[]{:S(2)}) collective-permute-start(f32[73,2,132]{0,2,1:T(8,128)S(1)} %get-tuple-element.6), channel_id=1, source_target_pairs={{0,960},{64,128},{128,64},{192,256},{256,192},{320,384},{384,320},... | collective-permute-start | bytes 231272 | tf_op jit(solution)/shard_map/ppermute | solution.py:21
  40.6 1.8 %copy-start.5 = (f32[24,72]{1,0:T(8,128)S(1)}, f32[24,72]{1,0:T(8,128)}, u32[]{:S(2)}) copy-start(f32[24,72]{1,0:T(8,128)} %param.17) | copy-start | bytes 20740
  41.6 23.5 %copy-start.13 = (s32[16]{0:T(128)S(1)}, s32[16]{0:T(128)}, u32[]{:S(2)}) copy-start(s32[16]{0:T(128)} %iota_add_fusion.4) | copy-start | bytes 196
  42.4 6.7 %copy-start.2 = (f32[72,8,128]{0,2,1:T(8,128)}, f32[72,8,128]{0,2,1:T(8,128)S(1)}, u32[]{:S(2)}) copy-start(f32[72,8,128]{0,2,1:T(8,128)S(1)} %fusion.6) | copy-start | bytes 884740
  43.1 23.4 %copy-start.14 = (s32[16]{0:T(128)S(1)}, s32[16]{0:T(128)}, u32[]{:S(2)}) copy-start(s32[16]{0:T(128)} %iota_add_fusion.3) | copy-start | bytes 196
  43.1 14.5 %collective-permute-start.4 = (bf16[24,16,64]{2,1,0:T(8,128)(2,1)S(1)}, bf16[24,16,64]{2,1,0:T(8,128)(2,1)S(1)}, u32[]{:S(2)}, u32[]{:S(2)}) collective-permute-start(bf16[24,16,64]{2,1,0:T(8,128)(2,1)S(1)} %reshape.176), channel_id=1, source_target_pairs={{0,2},{1,3},{2,0},{3,1},{4,6},{5,7},{6,4},{7,5},{8,10},{9,11},{10,... | collective-permute-start | bytes 147464 | tf_op jit(solution)/shard_map/ppermute | solution.py:21
  49.1 10.2 %collective-permute-start.5 = (bf16[24,16,64]{2,1,0:T(8,128)(2,1)S(1)}, bf16[24,16,64]{2,1,0:T(8,128)(2,1)S(1)}, u32[]{:S(2)}, u32[]{:S(2)}) collective-permute-start(bf16[24,16,64]{2,1,0:T(8,128)(2,1)S(1)} %reshape.176), channel_id=1, source_target_pairs={{0,62},{1,63},{2,4},{3,5},{4,2},{5,3},{6,8},{7,9},{8,6},{9,7},{10,... | collective-permute-start | bytes 147464 | tf_op jit(solution)/shard_map/ppermute | solution.py:21
  59.3 6.9 %collective-permute-start.6 = (bf16[24,32,64]{2,1,0:T(8,128)(2,1)S(1)}, bf16[24,32,64]{2,1,0:T(8,128)(2,1)S(1)}, u32[]{:S(2)}, u32[]{:S(2)}) collective-permute-start(bf16[24,32,64]{2,1,0:T(8,128)(2,1)S(1)} %pad_maximum_fusion.9), channel_id=1, source_target_pairs={{0,1},{1,0},{2,3},{3,2},{4,5},{5,4},{6,7},{7,6},{8,9},{9,8},{10,11... | collective-permute-start | bytes 294920 | tf_op jit(solution)/shard_map/ppermute | solution.py:21
  67.3 0.9 copy-start.4
  68.0 2.3 %copy-start.7 = (f32[8,80]{1,0:T(8,128)S(1)}, f32[8,80]{1,0:T(8,128)}, u32[]{:S(2)}) copy-start(f32[8,80]{1,0:T(8,128)} %param.24) | copy-start | bytes 7684
  68.0 10.4 %copy-start.11 = (s32[32]{0:T(128)S(1)}, s32[32]{0:T(128)}, u32[]{:S(2)}) copy-start(s32[32]{0:T(128)} %iota_add_fusion.2) | copy-start | bytes 388
  68.1 17.5 %copy-start.12 = (s32[32]{0:T(128)S(1)}, s32[32]{0:T(128)}, u32[]{:S(2)}) copy-start(s32[32]{0:T(128)} %iota_add_fusion.1) | copy-start | bytes 388
  68.2 18.5 %copy-start.15 = (s32[32]{0:T(128)S(1)}, s32[32]{0:T(128)}, u32[]{:S(2)}) copy-start(s32[32]{0:T(128)} %iota_add_fusion) | copy-start | bytes 388
  70.3 18.5 %copy-start.1 = (f32[80,2048]{1,0:T(8,128)}, f32[80,2048]{1,0:T(8,128)S(1)}, u32[]{:S(2)}) copy-start(f32[80,2048]{1,0:T(8,128)S(1)} %fusion.1) | copy-start | bytes 1966084
  70.9 18.0 %copy-start.8 = (f32[72,8]{0,1:T(8,128)S(1)}, f32[72,8]{0,1:T(8,128)}, u32[]{:S(2)}) copy-start(f32[72,8]{0,1:T(8,128)} %param.27) | copy-start | bytes 6916
  70.9 7.7 %collective-permute-start.7 = (bf16[8,32,64]{2,1,0:T(8,128)(2,1)S(1)}, bf16[8,32,64]{2,1,0:T(8,128)(2,1)S(1)}, u32[]{:S(2)}, u32[]{:S(2)}) collective-permute-start(bf16[8,32,64]{2,1,0:T(8,128)(2,1)S(1)} %reshape.179), channel_id=1, source_target_pairs={{0,2},{1,3},{2,0},{3,1},{4,6},{5,7},{6,4},{7,5},{8,10},{9,11},{10,... | collective-permute-start | bytes 98312 | tf_op jit(solution)/shard_map/ppermute | solution.py:21
  72.8 9.2 %collective-permute-start.8 = (bf16[8,32,64]{2,1,0:T(8,128)(2,1)S(1)}, bf16[8,32,64]{2,1,0:T(8,128)(2,1)S(1)}, u32[]{:S(2)}, u32[]{:S(2)}) collective-permute-start(bf16[8,32,64]{2,1,0:T(8,128)(2,1)S(1)} %reshape.179), channel_id=1, source_target_pairs={{0,62},{1,63},{2,4},{3,5},{4,2},{5,3},{6,8},{7,9},{8,6},{9,7},{10,... | collective-permute-start | bytes 98312 | tf_op jit(solution)/shard_map/ppermute | solution.py:21
  82.1 4.4 %collective-permute-start.9 = (bf16[8,64,64]{2,1,0:T(8,128)(2,1)S(1)}, bf16[8,64,64]{2,1,0:T(8,128)(2,1)S(1)}, u32[]{:S(2)}, u32[]{:S(2)}) collective-permute-start(bf16[8,64,64]{2,1,0:T(8,128)(2,1)S(1)} %pad_maximum_fusion.14), channel_id=1, source_target_pairs={{0,1},{1,0},{2,3},{3,2},{4,5},{5,4},{6,7},{7,6},{8,9},{9,8},{10,11... | collective-permute-start | bytes 196616 | tf_op jit(solution)/shard_map/ppermute | solution.py:21

commit v5 on v4

--- a/solution.py
+++ b/solution.py
@@ -21,28 +21,56 @@
     return lax.ppermute(value, axis, pairs)
 
 
-def halo_cols(cells, width):
-    levels, rows, cols = cells.shape
+def halo_cols(field, coeff, width):
+    levels, rows, cols = field.shape
     even = lax.axis_index("tile") % 2 == 0
-    head = cells[:, :, :width].reshape(-1)
-    tail = cells[:, :, cols - width:].reshape(-1)
+    cut = levels * rows * width
+
+    def strip(start):
+        return jnp.concatenate(
+            [field[:, :, start:start + width].reshape(-1), coeff[:, start:start + width].reshape(-1)]
+        )
+
+    head = strip(0)
+    tail = strip(cols - width)
     partner = swap(jnp.where(even, tail, head), "tile", 1, 0)
     cross = swap(jnp.where(even, head, tail), "tile", 1, 1)
-    left = jnp.where(even, cross, partner).reshape(levels, rows, width)
-    right = jnp.where(even, partner, cross).reshape(levels, rows, width)
-    return jnp.concatenate([left, cells, right], axis=2)
+    left = jnp.where(even, cross, partner)
+    right = jnp.where(even, partner, cross)
+    field = jnp.concatenate(
+        [left[:cut].reshape(levels, rows, width), field, right[:cut].reshape(levels, rows, width)],
+        axis=2,
+    )
+    coeff = jnp.concatenate(
+        [left[cut:].reshape(rows, width), coeff, right[cut:].reshape(rows, width)], axis=1
+    )
+    return field, coeff
 
 
-def halo_rows(cells, width):
-    levels, rows, cols = cells.shape
+def halo_rows(field, coeff, width):
+    levels, rows, cols = field.shape
     even = lax.axis_index("comp") % 2 == 0
-    head = cells[:, :width, :]
-    tail = cells[:, rows - width:, :]
+    cut = levels * width * cols
+
+    def strip(start):
+        return jnp.concatenate(
+            [field[:, start:start + width, :].reshape(-1), coeff[start:start + width, :].reshape(-1)]
+        )
+
+    head = strip(0)
+    tail = strip(rows - width)
     first = swap(jnp.where(even, tail, head), "comp", 1, 0)
     second = swap(jnp.where(even, head, tail), "comp", 1, 1)
     up = jnp.where(even, second, first)
     down = jnp.where(even, first, second)
-    return jnp.concatenate([up, cells, down], axis=1)
+    field = jnp.concatenate(
+        [up[:cut].reshape(levels, width, cols), field, down[:cut].reshape(levels, width, cols)],
+        axis=1,
+    )
+    coeff = jnp.concatenate(
+        [up[cut:].reshape(width, cols), coeff, down[cut:].reshape(width, cols)], axis=0
+    )
+    return field, coeff
 
 
 def level_mix(matrix, field):
@@ -114,10 +142,7 @@
     back_proj,
 ):
     levels, rows_here, cols_here = atm_state.shape
-    joined = jnp.concatenate([atm_state, kappa[None]], axis=0)
-    padded = halo_rows(halo_cols(joined, 2), 2)
-    field = padded[:levels]
-    coeff = padded[levels]
+    field, coeff = halo_rows(*halo_cols(atm_state, kappa, 2), 2)
     first = inner_step(field, coeff[1:-1, 1:-1], vert_mix)
     atm_mid = inner_step(first, coeff[2:-2, 2:-2], vert_mix)
     surface = level_mix(flux_proj, atm_mid).astype(jnp.bfloat16)

time: 92.4 us -> 98 us (1.061)
  waiting for transfers between devices: 8.34 us -> 15.2 us
  starting transfers between devices: 57.4 us -> 51.3 us
  local copies, waits for them, and re-layouts: 7.28 us -> 11.6 us
  other arithmetic: 3.39 us -> 5.5 us
  matrix products: 14.1 us -> 12.3 us
    ppermute x10, waiting for transfers between devices: 8.34 us -> 15.2 us  [swap(): return lax.ppermute(value, axis, pairs)]
    ppermute x10, starting transfers between devices: 57.4 us -> 51.3 us  [swap(): return lax.ppermute(value, axis, pairs)]
    slice x3 -> x20, local copies, waits for them, and re-layouts: 0.89 us -> 5.28 us  [the longest x1 2.03 us: strip(): field[:, :, start:start + width].reshape(-1)]
    add x2, other arithmetic: 0.04 us -> 1.4 us  [near_index(): return relative * per_tile + cols % per_tile]
    eq x1, other arithmetic: 0.01 us -> 1.29 us  [body(): ocean_out = jnp.where(wet_mask[None] == 1, stepped, ocean_state)]
    reshape x4 -> x8, local copies, waits for them, and re-layouts: 0.86 us -> 2.1 us  [the longest x2 1.37 us: strip(): field[:, :, start:start + width].reshape(-1)]
    dot_general x4, matrix products: 4.38 us -> 3.31 us  [level_mix(): jnp.einsum('ml,l...->m...', matrix, field, precision=lax.Precision.HIGHEST)]
    add x6, other arithmetic: 2.71 us -> 1.7 us  [pick(): ids = base + jnp.arange(count, dtype=local.dtype)]
  transfers between devices with their start and end apart: 10 -> 10, of which waited for: 5 -> 6; matrix products, arithmetic and copies ran while one was open for 8% -> 9% of each run, Pallas kernels for 0% -> 0%
where the time goes in v5:
time: 98 us; the launch traced here: 97.3 us
  starting transfers between devices  51.3 us (52%)
  waiting for transfers between devices  15.2 us (16%)
  matrix products  12.3 us (13%)
  local copies, waits for them, and re-layouts  11.6 us (12%)
  other arithmetic  5.5 us (6%)
  between operations  1.36 us (1%)
    ppermute x10, starting transfers between devices, swap(): return lax.ppermute(value, axis, pairs)  51.3 us
    ppermute x10, waiting for transfers between devices, swap(): return lax.ppermute(value, axis, pairs)  15.2 us
    dot_general x4, matrix products, level_mix(): jnp.einsum('ml,l...->m...', matrix, field, precision=lax.Precision.HIGHEST)  3.31 us
    dot_general x1, matrix products, body(): jnp.dot(ocean_mix, ocean_state, precision=lax.Precision.HIGHEST)  2.28 us
    dot_general x2, matrix products, block_product(): jnp.einsum('okij,fokj->foi', weights, picked, preferred_element_type=jnp....  2.22 us
    dot_general x8, matrix products, pick(): jnp.einsum('qb,fbj->fqj', onehot, piece, preferred_element_type=jnp.float32)  2.22 us
    slice x1, local copies, waits for them, and re-layouts, strip(): field[:, :, start:start + width].reshape(-1)  2.03 us
    unnamed x38, local copies, waits for them, and re-layouts  1.99 us
  transfers between devices with their start and end apart: 10, of which 6 were waited for; matrix products, arithmetic and copies ran while one was open for 9% of the time, Pallas kernels for 0%

profile of v5, /device:TPU:1, one launch (start us, length us, event | category | flops | bytes accessed | tf_op | source)
XLA Modules:
  0.0 97.3 jit_solution(9987565273815678846)
XLA Ops:
  0.7 2.0 %fusion.75 = (f32[72,8,2]{2,1,0:T(8,128)}, f32[72,8,2]{2,1,0:T(8,128)S(1)}) fusion(f32[72,8,128]{2,1,0:T(8,128)} %param.14), kind=kLoop, calls=%fused_computation.165 | loop fusion | bytes 18432 | tf_op jit(solution)/shard_map/slice | solution.py:31
  2.7 1.2 %reshape.258 = f32[1152]{0:T(1024)S(1)} reshape(f32[72,8,2]{2,1,0:T(8,128)} %get-tuple-element.8) | data formatting | bytes 9216 | tf_op jit(solution)/shard_map/reshape | solution.py:31
  4.1 0.8 fusion.76
  5.2 4.5 %collective-permute-start = (f32[1168]{0:T(1024)S(1)}, f32[1168]{0:T(1024)S(1)}, u32[]{:S(2)}, u32[]{:S(2)}) collective-permute-start(f32[1168]{0:T(1024)S(1)} %get-tuple-element.16), channel_id=1, source_target_pairs={{0,63},{1,2},{2,1},{3,4},{4,3},{5,6},{6,5},{7,8},{8,7},{9,10},{10,... | collective-permute-start | bytes 14024 | tf_op jit(solution)/shard_map/ppermute | solution.py:21
  9.7 13.5 %collective-permute-start.1 = (f32[1168]{0:T(1024)S(1)}, f32[1168]{0:T(1024)S(1)}, u32[]{:S(2)}, u32[]{:S(2)}) collective-permute-start(f32[1168]{0:T(1024)S(1)} %get-tuple-element.17), channel_id=1, source_target_pairs={{0,1},{1,0},{2,3},{3,2},{4,5},{5,4},{6,7},{7,6},{8,9},{9,8},{10,11... | collective-permute-start | bytes 14024 | tf_op jit(solution)/shard_map/ppermute | solution.py:21
  23.8 0.7 fusion.67
  24.7 1.3 %broadcast_compare_fusion = pred[2048]{0:T(1024)(128)(4,1)} fusion(s32[2048]{0:T(1024)} %param.23), kind=kLoop, calls=%fused_computation.104 | loop fusion | flops 2048 | bytes 10240 | tf_op jit(solution)/shard_map/eq | solution.py:160
  26.0 0.7 fusion.72
  26.9 2.3 %convolution_add_fusion = f32[80,2048]{1,0:T(8,128)} fusion(f32[80,2048]{1,0:T(8,128)S(1)} %copy-done.2, f32[80,80]{1,0:T(8,128)} %param.21), kind=kOutput, calls=%fused_computation | convolution fusion | flops 157450240 | bytes 1336320 | tf_op jit(solution)/shard_map/dot_general | solution.py:155
  29.2 0.6 compare_select_fusion.1
  32.7 11.3 %collective-permute-start.2 = (f32[19272]{0:T(1024)S(1)}, f32[19272]{0:T(1024)S(1)}, u32[]{:S(2)}, u32[]{:S(2)}) collective-permute-start(f32[19272]{0:T(1024)S(1)} %get-tuple-element.10), channel_id=1, source_target_pairs={{0,960},{64,128},{128,64},{192,256},{256,192},{320,384},{384,320},... | collective-permute-start | bytes 231272 | tf_op jit(solution)/shard_map/ppermute | solution.py:21
  44.0 1.9 %collective-permute-start.3 = (f32[19272]{0:T(1024)S(1)}, f32[19272]{0:T(1024)S(1)}, u32[]{:S(2)}, u32[]{:S(2)}) collective-permute-start(f32[19272]{0:T(1024)S(1)} %get-tuple-element.11), channel_id=1, source_target_pairs={{0,64},{64,0},{128,192},{192,128},{256,320},{320,256},{384,448},{4... | collective-permute-start | bytes 231272 | tf_op jit(solution)/shard_map/ppermute | solution.py:21
  46.7 2.8 %collective-permute-done.3 = f32[19272]{0:T(1024)S(1)} collective-permute-done((f32[19272]{0:T(1024)S(1)}, f32[19272]{0:T(1024)S(1)}, u32[]{:S(2)}, u32[]{:S(2)}) %collective-permute-start.3) | collective-permute-done | bytes 77120 | tf_op jit(solution)/shard_map/ppermute | solution.py:21
  51.0 1.0 %fusion.4 = f32[72,10,130]{0,2,1:T(8,128)S(1)} fusion(f32[72,12,132]{0,2,1:T(8,128)S(1)} %pad_maximum_fusion, f32[72,2,132]{0,2,1:T(8,128)S(1)} %copy.32, f32[72,8,2]{0,2,1:T(2,128)S(1)} %copy.29, f32[72,8,128]{0,2,1:T(8,128)S(1)} %copy.28, f32[72,8,2]{0,2,1:T(2,128)S(1)} %copy.27, f32[72,2,132]{0,2,1:T(8,128)S(1)} %copy.33, ...), kind=kOutput, calls=%fused_computation.10 | convolution fusion | flops 82180800 | bytes 4032128 | tf_op jit(solution)/shard_map/ml,l...->m.../dot_general | solution.py:77
  52.0 0.7 fusion.7
  52.8 0.8 copy-done.5
  54.2 1.9 %collective-permute-start.4 = (bf16[24,16,64]{2,1,0:T(8,128)(2,1)S(1)}, bf16[24,16,64]{2,1,0:T(8,128)(2,1)S(1)}, u32[]{:S(2)}, u32[]{:S(2)}) collective-permute-start(bf16[24,16,64]{2,1,0:T(8,128)(2,1)S(1)} %reshape.266), channel_id=1, source_target_pairs={{0,2},{1,3},{2,0},{3,1},{4,6},{5,7},{6,4},{7,5},{8,10},{9,11},{10,... | collective-permute-start | bytes 147464 | tf_op jit(solution)/shard_map/ppermute | solution.py:21
  56.2 4.2 %collective-permute-start.5 = (bf16[24,16,64]{2,1,0:T(8,128)(2,1)S(1)}, bf16[24,16,64]{2,1,0:T(8,128)(2,1)S(1)}, u32[]{:S(2)}, u32[]{:S(2)}) collective-permute-start(bf16[24,16,64]{2,1,0:T(8,128)(2,1)S(1)} %reshape.266), channel_id=1, source_target_pairs={{0,62},{1,63},{2,4},{3,5},{4,2},{5,3},{6,8},{7,9},{8,6},{9,7},{10,... | collective-permute-start | bytes 147464 | tf_op jit(solution)/shard_map/ppermute | solution.py:21
  60.7 6.2 %collective-permute-done.5 = bf16[24,16,64]{2,1,0:T(8,128)(2,1)S(1)} collective-permute-done((bf16[24,16,64]{2,1,0:T(8,128)(2,1)S(1)}, bf16[24,16,64]{2,1,0:T(8,128)(2,1)S(1)}, u32[]{:S(2)}, u32[]{:S(2)}) %collective-permute-start.5) | collective-permute-done | bytes 49184 | tf_op jit(solution)/shard_map/ppermute | solution.py:21
  67.0 3.9 %collective-permute-start.6 = (bf16[24,32,64]{2,1,0:T(8,128)(2,1)S(1)}, bf16[24,32,64]{2,1,0:T(8,128)(2,1)S(1)}, u32[]{:S(2)}, u32[]{:S(2)}) collective-permute-start(bf16[24,32,64]{2,1,0:T(8,128)(2,1)S(1)} %pad_maximum_fusion.7), channel_id=1, source_target_pairs={{0,1},{1,0},{2,3},{3,2},{4,5},{5,4},{6,7},{7,6},{8,9},{9,8},{10,11... | collective-permute-start | bytes 294920 | tf_op jit(solution)/shard_map/ppermute | solution.py:21
  71.2 0.7 collective-permute-done.6
  73.0 0.6 convolution_bitcast_fusion.4
  73.8 0.8 reshape.268
  74.6 1.8 %fusion.1 = f32[80,2048]{1,0:T(8,128)S(1)} fusion(f32[80,2048]{1,0:T(8,128)S(1)} %copy-done.3, f32[80,2048]{1,0:T(8,128)} %convolution_add_fusion, f32[24,2048]{1,0:T(8,128)} %reshape.268, f32[80,24]{0,1:T(8,128)S(1)} %copy-done.8, pred[2048]{0:T(1024)(128)(4,1)} %broadcast_compare_fusion), kind=kOutput, calls=%fused_computation.3 | convolution fusion | flops 47513600 | bytes 2172416 | tf_op jit(solution)/shard_map/dot_general | solution.py:159
  77.1 2.1 %collective-permute-start.7 = (bf16[8,32,64]{2,1,0:T(8,128)(2,1)S(1)}, bf16[8,32,64]{2,1,0:T(8,128)(2,1)S(1)}, u32[]{:S(2)}, u32[]{:S(2)}) collective-permute-start(bf16[8,32,64]{2,1,0:T(8,128)(2,1)S(1)} %reshape.269), channel_id=1, source_target_pairs={{0,2},{1,3},{2,0},{3,1},{4,6},{5,7},{6,4},{7,5},{8,10},{9,11},{10,... | collective-permute-start | bytes 98312 | tf_op jit(solution)/shard_map/ppermute | solution.py:21
  79.2 4.8 %collective-permute-start.8 = (bf16[8,32,64]{2,1,0:T(8,128)(2,1)S(1)}, bf16[8,32,64]{2,1,0:T(8,128)(2,1)S(1)}, u32[]{:S(2)}, u32[]{:S(2)}) collective-permute-start(bf16[8,32,64]{2,1,0:T(8,128)(2,1)S(1)} %reshape.269), channel_id=1, source_target_pairs={{0,62},{1,63},{2,4},{3,5},{4,2},{5,3},{6,8},{7,9},{8,6},{9,7},{10,... | collective-permute-start | bytes 98312 | tf_op jit(solution)/shard_map/ppermute | solution.py:21
  84.2 4.5 %collective-permute-done.8 = bf16[8,32,64]{2,1,0:T(8,128)(2,1)S(1)} collective-permute-done((bf16[8,32,64]{2,1,0:T(8,128)(2,1)S(1)}, bf16[8,32,64]{2,1,0:T(8,128)(2,1)S(1)}, u32[]{:S(2)}, u32[]{:S(2)}) %collective-permute-start.8) | collective-permute-done | bytes 32800 | tf_op jit(solution)/shard_map/ppermute | solution.py:21
  88.8 3.3 %collective-permute-start.9 = (bf16[8,64,64]{2,1,0:T(8,128)(2,1)S(1)}, bf16[8,64,64]{2,1,0:T(8,128)(2,1)S(1)}, u32[]{:S(2)}, u32[]{:S(2)}) collective-permute-start(bf16[8,64,64]{2,1,0:T(8,128)(2,1)S(1)} %pad_maximum_fusion.11), channel_id=1, source_target_pairs={{0,1},{1,0},{2,3},{3,2},{4,5},{5,4},{6,7},{7,6},{8,9},{9,8},{10,11... | collective-permute-start | bytes 196616 | tf_op jit(solution)/shard_map/ppermute | solution.py:21
  92.4 0.7 collective-permute-done.9
  93.7 1.6 %convolution_bitcast_fusion.5 = f32[8,16,64]{2,0,1:T(8,128)S(1)} fusion(bf16[8,16,4,64]{3,0,2,1:T(8,128)(2,1)S(1)} %bitcast.97, bf16[16,4,64,64]{3,2,1,0:T(8,128)(2,1)} %param.25), kind=kOutput, calls=%fused_computation.24 | convolution fusion | flops 4194304 | bytes 622592 | tf_op jit(solution)/shard_map/okij,fokj->foi/dot_general | solution.py:89
  95.4 1.0 %fusion.6 = f32[72,8,128]{0,2,1:T(8,128)S(1)} fusion(f32[72,8,128]{0,2,1:T(8,128)S(1)} %copy-done.6, f32[8,8,128]{2,1,0:T(8,128)S(1)} %reshape.271, f32[72,8]{0,1:T(8,128)S(1)} %copy-done.11), kind=kOutput, calls=%fused_computation.13 | convolution fusion | flops 7151616 | bytes 624896 | tf_op jit(solution)/shard_map/ml,l...->m.../dot_general | solution.py:77
  96.4 0.9 copy.49
  (110 shorter events, 10.8 us)
Async XLA Ops:
  0.6 72.4 %copy-start = (bf16[32,4,64,64]{3,2,1,0:T(8,128)(2,1)S(1)}, bf16[32,4,64,64]{3,2,1,0:T(8,128)(2,1)}, u32[]{:S(2)}) copy-start(bf16[32,4,64,64]{3,2,1,0:T(8,128)(2,1)} %param.18) | copy-start | bytes 3145732
  0.6 29.7 %copy-start.1 = (f32[72,8,128]{2,1,0:T(8,128)S(1)}, f32[72,8,128]{2,1,0:T(8,128)}, u32[]{:S(2)}) copy-start(f32[72,8,128]{2,1,0:T(8,128)} %param.14) | copy-start | bytes 884740
  0.7 26.3 %copy-start.2 = (f32[80,2048]{1,0:T(8,128)S(1)}, f32[80,2048]{1,0:T(8,128)}, u32[]{:S(2)}) copy-start(f32[80,2048]{1,0:T(8,128)} %param.20) | copy-start | bytes 1966084
  5.2 25.5 %collective-permute-start = (f32[1168]{0:T(1024)S(1)}, f32[1168]{0:T(1024)S(1)}, u32[]{:S(2)}, u32[]{:S(2)}) collective-permute-start(f32[1168]{0:T(1024)S(1)} %get-tuple-element.16), channel_id=1, source_target_pairs={{0,63},{1,2},{2,1},{3,4},{4,3},{5,6},{6,5},{7,8},{8,7},{9,10},{10,... | collective-permute-start | bytes 14024 | tf_op jit(solution)/shard_map/ppermute | solution.py:21
  9.7 20.9 %collective-permute-start.1 = (f32[1168]{0:T(1024)S(1)}, f32[1168]{0:T(1024)S(1)}, u32[]{:S(2)}, u32[]{:S(2)}) collective-permute-start(f32[1168]{0:T(1024)S(1)} %get-tuple-element.17), channel_id=1, source_target_pairs={{0,1},{1,0},{2,3},{3,2},{4,5},{5,4},{6,7},{7,6},{8,9},{9,8},{10,11... | collective-permute-start | bytes 14024 | tf_op jit(solution)/shard_map/ppermute | solution.py:21
  29.2 3.2 %copy-start.7 = (f32[8,128]{1,0:T(8,128)S(1)}, f32[8,128]{1,0:T(8,128)}, u32[]{:S(2)}) copy-start(f32[8,128]{1,0:T(8,128)} %param.15) | copy-start | bytes 12292
  31.7 19.3 %copy-start.16 = (f32[72,72]{1,0:T(8,128)S(1)}, f32[72,72]{1,0:T(8,128)}, u32[]{:S(2)}) copy-start(f32[72,72]{1,0:T(8,128)} %param.16) | copy-start | bytes 62212
  32.7 14.0 %collective-permute-start.2 = (f32[19272]{0:T(1024)S(1)}, f32[19272]{0:T(1024)S(1)}, u32[]{:S(2)}, u32[]{:S(2)}) collective-permute-start(f32[19272]{0:T(1024)S(1)} %get-tuple-element.10), channel_id=1, source_target_pairs={{0,960},{64,128},{128,64},{192,256},{256,192},{320,384},{384,320},... | collective-permute-start | bytes 231272 | tf_op jit(solution)/shard_map/ppermute | solution.py:21
  44.0 5.6 %collective-permute-start.3 = (f32[19272]{0:T(1024)S(1)}, f32[19272]{0:T(1024)S(1)}, u32[]{:S(2)}, u32[]{:S(2)}) collective-permute-start(f32[19272]{0:T(1024)S(1)} %get-tuple-element.11), channel_id=1, source_target_pairs={{0,64},{64,0},{128,192},{192,128},{256,320},{320,256},{384,448},{4... | collective-permute-start | bytes 231272 | tf_op jit(solution)/shard_map/ppermute | solution.py:21
  51.0 2.5 %copy-start.9 = (f32[24,72]{1,0:T(8,128)S(1)}, f32[24,72]{1,0:T(8,128)}, u32[]{:S(2)}) copy-start(f32[24,72]{1,0:T(8,128)} %param.17) | copy-start | bytes 20740
  52.7 0.8 copy-start.5
  54.2 6.5 %collective-permute-start.4 = (bf16[24,16,64]{2,1,0:T(8,128)(2,1)S(1)}, bf16[24,16,64]{2,1,0:T(8,128)(2,1)S(1)}, u32[]{:S(2)}, u32[]{:S(2)}) collective-permute-start(bf16[24,16,64]{2,1,0:T(8,128)(2,1)S(1)} %reshape.266), channel_id=1, source_target_pairs={{0,2},{1,3},{2,0},{3,1},{4,6},{5,7},{6,4},{7,5},{8,10},{9,11},{10,... | collective-permute-start | bytes 147464 | tf_op jit(solution)/shard_map/ppermute | solution.py:21
  56.2 10.7 %collective-permute-start.5 = (bf16[24,16,64]{2,1,0:T(8,128)(2,1)S(1)}, bf16[24,16,64]{2,1,0:T(8,128)(2,1)S(1)}, u32[]{:S(2)}, u32[]{:S(2)}) collective-permute-start(bf16[24,16,64]{2,1,0:T(8,128)(2,1)S(1)} %reshape.266), channel_id=1, source_target_pairs={{0,62},{1,63},{2,4},{3,5},{4,2},{5,3},{6,8},{7,9},{8,6},{9,7},{10,... | collective-permute-start | bytes 147464 | tf_op jit(solution)/shard_map/ppermute | solution.py:21
  67.0 4.9 %collective-permute-start.6 = (bf16[24,32,64]{2,1,0:T(8,128)(2,1)S(1)}, bf16[24,32,64]{2,1,0:T(8,128)(2,1)S(1)}, u32[]{:S(2)}, u32[]{:S(2)}) collective-permute-start(bf16[24,32,64]{2,1,0:T(8,128)(2,1)S(1)} %pad_maximum_fusion.7), channel_id=1, source_target_pairs={{0,1},{1,0},{2,3},{3,2},{4,5},{5,4},{6,7},{7,6},{8,9},{9,8},{10,11... | collective-permute-start | bytes 294920 | tf_op jit(solution)/shard_map/ppermute | solution.py:21
  73.0 1.6 %copy-start.3 = (f32[80,2048]{1,0:T(8,128)S(1)}, f32[80,2048]{1,0:T(8,128)}, u32[]{:S(2)}) copy-start(f32[80,2048]{1,0:T(8,128)} %param.20) | copy-start | bytes 1966084
  73.0 1.6 %copy-start.8 = (f32[80,24]{0,1:T(8,128)S(1)}, f32[80,24]{0,1:T(8,128)}, u32[]{:S(2)}) copy-start(f32[80,24]{0,1:T(8,128)} %param.22) | copy-start | bytes 23044
  73.7 2.8 %copy-start.10 = (f32[8,80]{1,0:T(8,128)S(1)}, f32[8,80]{1,0:T(8,128)}, u32[]{:S(2)}) copy-start(f32[8,80]{1,0:T(8,128)} %param.24) | copy-start | bytes 7684
  73.7 10.3 %copy-start.13 = (s32[32]{0:T(128)S(1)}, s32[32]{0:T(128)}, u32[]{:S(2)}) copy-start(s32[32]{0:T(128)} %iota_add_fusion.2) | copy-start | bytes 388
  73.8 18.3 %copy-start.14 = (s32[32]{0:T(128)S(1)}, s32[32]{0:T(128)}, u32[]{:S(2)}) copy-start(s32[32]{0:T(128)} %iota_add_fusion.1) | copy-start | bytes 388
  74.6 18.5 %copy-start.12 = (s32[64]{0:T(128)S(1)}, s32[64]{0:T(128)}, u32[]{:S(2)}) copy-start(s32[64]{0:T(128)} %compare_select_fusion.1) | copy-start | bytes 772
  76.5 18.8 %copy-start.4 = (f32[80,2048]{1,0:T(8,128)}, f32[80,2048]{1,0:T(8,128)S(1)}, u32[]{:S(2)}) copy-start(f32[80,2048]{1,0:T(8,128)S(1)} %fusion.1) | copy-start | bytes 1966084
  76.5 16.8 %copy-start.15 = (s32[32]{0:T(128)S(1)}, s32[32]{0:T(128)}, u32[]{:S(2)}) copy-start(s32[32]{0:T(128)} %iota_add_fusion) | copy-start | bytes 388
  77.1 18.3 %copy-start.6 = (f32[72,8,128]{0,2,1:T(8,128)S(1)}, f32[72,8,128]{0,2,1:T(8,128)}, u32[]{:S(2)}) copy-start(f32[72,8,128]{0,2,1:T(8,128)} %copy-done.5) | copy-start | bytes 884740
  77.1 18.3 %copy-start.11 = (f32[72,8]{0,1:T(8,128)S(1)}, f32[72,8]{0,1:T(8,128)}, u32[]{:S(2)}) copy-start(f32[72,8]{0,1:T(8,128)} %param.27) | copy-start | bytes 6916
  77.1 7.1 %collective-permute-start.7 = (bf16[8,32,64]{2,1,0:T(8,128)(2,1)S(1)}, bf16[8,32,64]{2,1,0:T(8,128)(2,1)S(1)}, u32[]{:S(2)}, u32[]{:S(2)}) collective-permute-start(bf16[8,32,64]{2,1,0:T(8,128)(2,1)S(1)} %reshape.269), channel_id=1, source_target_pairs={{0,2},{1,3},{2,0},{3,1},{4,6},{5,7},{6,4},{7,5},{8,10},{9,11},{10,... | collective-permute-start | bytes 98312 | tf_op jit(solution)/shard_map/ppermute | solution.py:21
  79.2 9.6 %collective-permute-start.8 = (bf16[8,32,64]{2,1,0:T(8,128)(2,1)S(1)}, bf16[8,32,64]{2,1,0:T(8,128)(2,1)S(1)}, u32[]{:S(2)}, u32[]{:S(2)}) collective-permute-start(bf16[8,32,64]{2,1,0:T(8,128)(2,1)S(1)} %reshape.269), channel_id=1, source_target_pairs={{0,62},{1,63},{2,4},{3,5},{4,2},{5,3},{6,8},{7,9},{8,6},{9,7},{10,... | collective-permute-start | bytes 98312 | tf_op jit(solution)/shard_map/ppermute | solution.py:21
  88.8 4.3 %collective-permute-start.9 = (bf16[8,64,64]{2,1,0:T(8,128)(2,1)S(1)}, bf16[8,64,64]{2,1,0:T(8,128)(2,1)S(1)}, u32[]{:S(2)}, u32[]{:S(2)}) collective-permute-start(bf16[8,64,64]{2,1,0:T(8,128)(2,1)S(1)} %pad_maximum_fusion.11), channel_id=1, source_target_pairs={{0,1},{1,0},{2,3},{3,2},{4,5},{5,4},{6,7},{7,6},{8,9},{9,8},{10,11... | collective-permute-start | bytes 196616 | tf_op jit(solution)/shard_map/ppermute | solution.py:21

commit v6 on v4

--- a/solution.py
+++ b/solution.py
@@ -46,7 +46,15 @@
 
 
 def level_mix(matrix, field):
-    return jnp.einsum("ml,l...->m...", matrix, field, precision=lax.Precision.HIGHEST)
+    return jnp.einsum("ml,l...->m...", matrix, field, precision=lax.Precision.HIGH)
+
+
+def laplace(padded):
+    center = padded[:, 1:-1, 1:-1]
+    beside_all = (
+        padded[:, 2:, 1:-1] + padded[:, :-2, 1:-1] + padded[:, 1:-1, 2:] + padded[:, 1:-1, :-2]
+    )
+    return beside_all - 4.0 * center
 
 
 def inner_step(padded, coeff, vert_mix):
@@ -94,7 +102,7 @@
     picked = picked + pick(local, first_base, first, per_tile)
     picked = picked + pick(local, second_base, second, per_tile)
     picked = picked + pick(partner_local, 0, partner, 2 * per_tile)
-    return picked.astype(blocks.dtype).reshape((fields,) + cols.shape + (cells,))
+    return picked.astype(blocks.dtype).reshape((fields,) + cols.shape + (cells,)), first
 
 
 def body(
@@ -118,10 +126,17 @@
     padded = halo_rows(halo_cols(joined, 2), 2)
     field = padded[:levels]
     coeff = padded[levels]
-    first = inner_step(field, coeff[1:-1, 1:-1], vert_mix)
-    atm_mid = inner_step(first, coeff[2:-2, 2:-2], vert_mix)
-    surface = level_mix(flux_proj, atm_mid).astype(jnp.bfloat16)
-    fields = surface.shape[0]
+    inner = coeff[1:-1, 1:-1]
+    centre = coeff[2:-2, 2:-2]
+    step = jnp.eye(levels, dtype=vert_mix.dtype) + vert_mix
+    once = jnp.dot(flux_proj, step, precision=lax.Precision.HIGHEST)
+    twice = jnp.dot(once, step, precision=lax.Precision.HIGHEST)
+    fields = flux_proj.shape[0]
+    stacked = level_mix(jnp.concatenate([flux_proj, once, twice], axis=0), field)
+    plain, mixed_once, mixed_twice = stacked[:fields], stacked[fields:2 * fields], stacked[2 * fields:]
+    proj_first = mixed_once[:, 1:-1, 1:-1] + inner[None] * laplace(plain)
+    proj_mixed = mixed_twice[:, 2:-2, 2:-2] + centre[None] * laplace(mixed_once)[:, 1:-1, 1:-1]
+    surface = (proj_mixed + centre[None] * laplace(proj_first)).astype(jnp.bfloat16)
     atm_blocks = rows_here * cols_here // 64
     surface_blocks = surface.reshape(fields, atm_blocks, 64)
     ocean_blocks = remap_weight.shape[0]
@@ -129,13 +144,19 @@
     mixed = lax.optimization_barrier(
         ocean_state + jnp.dot(ocean_mix, ocean_state, precision=lax.Precision.HIGHEST)
     )
-    remapped = block_product(remap_weight, exchange_and_pick(surface_blocks, remap_cols, here))
+    remapped = block_product(remap_weight, exchange_and_pick(surface_blocks, remap_cols, here)[0])
+    field = lax.optimization_barrier((field, remapped))[0]
+    atm_mid = inner_step(inner_step(field, inner, vert_mix), centre, vert_mix)
     remapped = remapped.reshape(fields, ocean_blocks * 64)
-    stepped = mixed + jnp.dot(forcing, remapped, precision=lax.Precision.HIGHEST)
-    ocean_out = jnp.where(wet_mask[None] == 1, stepped, ocean_state)
-    sea = jnp.dot(surface_proj, ocean_out, precision=lax.Precision.HIGHEST).astype(jnp.bfloat16)
+    wet = wet_mask[None] == 1
+    stepped = mixed + jnp.dot(forcing, remapped, precision=lax.Precision.HIGH)
+    ocean_out = jnp.where(wet, stepped, ocean_state)
+    settled = jnp.dot(surface_proj, jnp.where(wet, mixed, ocean_state), precision=lax.Precision.HIGHEST)
+    sea_forcing = jnp.dot(surface_proj, forcing, precision=lax.Precision.HIGHEST)
+    moved = jnp.dot(sea_forcing, remapped, precision=lax.Precision.HIGH)
+    sea = (settled + jnp.where(wet, moved, 0.0)).astype(jnp.bfloat16)
     sea_blocks = sea.reshape(sea.shape[0], ocean_blocks, 64)
-    returned = block_product(back_weight, exchange_and_pick(sea_blocks, back_cols, here))
+    returned = block_product(back_weight, exchange_and_pick(sea_blocks, back_cols, here)[0])
     returned = returned.reshape(sea.shape[0], rows_here, cols_here)
     atm_out = atm_mid + level_mix(back_proj, returned)
     return (atm_out, ocean_out)

time: 92.4 us -> 98.2 us (1.063)
  other arithmetic: 3.39 us -> 8.41 us
  matrix products: 14.1 us -> 17.8 us
  waiting for transfers between devices: 8.34 us -> 5.66 us
  starting transfers between devices: 57.4 us -> 55.8 us
  local copies, waits for them, and re-layouts: 7.28 us -> 8.55 us
    dot_general x6 -> x10, matrix products: 6.85 us -> 11.1 us  [the longest x4 4.06 us: level_mix(): jnp.einsum('ml,l...->m...', matrix, field, precision=lax.Precision.HIGH)]
    ppermute x10, waiting for transfers between devices: 8.34 us -> 5.66 us  [swap(): return lax.ppermute(value, axis, pairs)]
    ppermute x10, starting transfers between devices: 57.4 us -> 55.8 us  [swap(): return lax.ppermute(value, axis, pairs)]
    dot_general x2, matrix products: 2.22 us -> 1 us  [block_product(): jnp.einsum('okij,fokj->foi', weights, picked, preferred_element_type=jnp....]
    slice x0 -> x1, other arithmetic: none -> 1.14 us  [laplace(): padded[:, 2:, 1:-1] + padded[:, :-2, 1:-1] + padded[:, 1:-1, 2:]]
    unnamed x36 -> x48, local copies, waits for them, and re-layouts: 2.29 us -> 2.32 us
  transfers between devices with their start and end apart: 10 -> 10, of which waited for: 5 -> 4; matrix products, arithmetic and copies ran while one was open for 8% -> 19% of each run, Pallas kernels for 0% -> 0%
where the time goes in v6:
time: 98.2 us; the launch traced here: 97.5 us
  starting transfers between devices  55.8 us (57%)
  matrix products  17.8 us (18%)
  local copies, waits for them, and re-layouts  8.55 us (9%)
  other arithmetic  8.41 us (9%)
  waiting for transfers between devices  5.66 us (6%)
  between operations  1.31 us (1%)
    ppermute x10, starting transfers between devices, swap(): return lax.ppermute(value, axis, pairs)  55.8 us
    ppermute x10, waiting for transfers between devices, swap(): return lax.ppermute(value, axis, pairs)  5.66 us
    dot_general x4, matrix products, level_mix(): jnp.einsum('ml,l...->m...', matrix, field, precision=lax.Precision.HIGH)  4.06 us
    add x6, other arithmetic, pick(): ids = base + jnp.arange(count, dtype=local.dtype)  3.34 us
    dot_general x8, matrix products, pick(): jnp.einsum('qb,fbj->fqj', onehot, piece, preferred_element_type=jnp.float32)  2.83 us
    dot_general x1, matrix products, body(): jnp.dot(ocean_mix, ocean_state, precision=lax.Precision.HIGHEST)  2.8 us
    dot_general x1, matrix products, body(): stepped = mixed + jnp.dot(forcing, remapped, precision=lax.Precision.HIGH)  2.59 us
    dot_general x1, matrix products, body(): jnp.dot(surface_proj, jnp.where(wet, mixed, ocean_state), precision=lax.P...  2.39 us
  transfers between devices with their start and end apart: 10, of which 4 were waited for; matrix products, arithmetic and copies ran while one was open for 19% of the time, Pallas kernels for 0%

profile of v6, /device:TPU:1, one launch (start us, length us, event | category | flops | bytes accessed | tf_op | source)
XLA Modules:
  0.0 97.5 jit_solution(7258379669608909684)
XLA Ops:
  0.7 1.3 %copy.30 = f32[72,8,128]{0,2,1:T(8,128)S(1)} copy(f32[72,8,128]{2,1,0:T(8,128)} %param.14) | data formatting | bytes 589824 | tf_op args[0]
  2.0 0.9 copy.31
  3.3 0.8 select_n.220
  4.1 16.1 %collective-permute-start.1 = (f32[1168]{0:T(1024)}, f32[1168]{0:T(1024)}, u32[]{:S(2)}, u32[]{:S(2)}) collective-permute-start(f32[1168]{0:T(1024)} %select_n.220), channel_id=1, source_target_pairs={{0,1},{1,0},{2,3},{3,2},{4,5},{5,4},{6,7},{7,6},{8,9},{9,8},{10,11... | collective-permute-start | bytes 14024 | tf_op jit(solution)/shard_map/ppermute | solution.py:21
  20.3 0.8 select_n.218
  21.1 1.9 %collective-permute-start = (f32[1168]{0:T(1024)}, f32[1168]{0:T(1024)S(1)}, u32[]{:S(2)}, u32[]{:S(2)}) collective-permute-start(f32[1168]{0:T(1024)} %select_n.218), channel_id=1, source_target_pairs={{0,63},{1,2},{2,1},{3,4},{4,3},{5,6},{6,5},{7,8},{8,7},{9,10},{10,... | collective-permute-start | bytes 14024 | tf_op jit(solution)/shard_map/ppermute | solution.py:21
  25.8 0.7 broadcast_compare_fusion
  26.5 2.8 %convolution_add_fusion = f32[80,2048]{1,0:T(8,128)} fusion(f32[80,2048]{1,0:T(8,128)} %param.20, f32[80,80]{1,0:T(8,128)} %param.21), kind=kOutput, calls=%fused_computation | convolution fusion | flops 157450240 | bytes 1336320 | tf_op jit(solution)/shard_map/dot_general | solution.py:145
  29.3 0.7 fusion.84
  30.3 0.7 fusion.90
  31.0 2.4 %convolution_bitcast_fusion.1 = f32[8,2048]{1,0:T(8,128)} fusion(f32[8,80]{1,0:T(8,128)S(1)} %copy-done.8, f32[80,2048]{1,0:T(8,128)} %convolution_add_fusion, f32[80,2048]{1,0:T(8,128)} %param.20, pred[2048]{0:T(1024)(128)(4,1)S(1)} %broadcast_compare_fusion), kind=kOutput, calls=%fused_computation.6 | convolution fusion | flops 15892480 | bytes 1380864 | tf_op jit(solution)/shard_map/dot_general | solution.py:154
  34.5 0.7 broadcast_select_fusion.9
  36.3 1.9 %collective-permute-start.3 = (f32[73,2,132]{0,2,1:T(8,128)S(1)}, f32[73,2,132]{0,2,1:T(8,128)S(1)}, u32[]{:S(2)}, u32[]{:S(2)}) collective-permute-start(f32[73,2,132]{0,2,1:T(8,128)S(1)} %broadcast_select_fusion.3), channel_id=1, source_target_pairs={{0,64},{64,0},{128,192},{192,128},{256,320},{320,256},{384,448},{4... | collective-permute-start | bytes 231272 | tf_op jit(solution)/shard_map/ppermute | solution.py:21
  38.2 6.6 %collective-permute-start.2 = (f32[73,2,132]{0,2,1:T(8,128)S(1)}, f32[73,2,132]{0,2,1:T(8,128)S(1)}, u32[]{:S(2)}, u32[]{:S(2)}) collective-permute-start(f32[73,2,132]{0,2,1:T(8,128)S(1)} %get-tuple-element.8), channel_id=1, source_target_pairs={{0,960},{64,128},{128,64},{192,256},{256,192},{320,384},{384,320},... | collective-permute-start | bytes 231272 | tf_op jit(solution)/shard_map/ppermute | solution.py:21
  45.4 1.9 %collective-permute-done.2 = f32[73,2,132]{0,2,1:T(8,128)S(1)} collective-permute-done((f32[73,2,132]{0,2,1:T(8,128)S(1)}, f32[73,2,132]{0,2,1:T(8,128)S(1)}, u32[]{:S(2)}, u32[]{:S(2)}) %collective-permute-start.2) | collective-permute-done | bytes 77120 | tf_op jit(solution)/shard_map/ppermute | solution.py:21
  47.6 0.7 slice_reduce_fusion
  49.0 1.1 %fusion.89 = (f32[24,10,130]{0,2,1:T(8,128)S(1)}, f32[24,10,130]{0,2,1:T(8,128)S(1)}, f32[24,10,130]{0,2,1:T(8,128)S(1)}, f32[24,10,130]{0,2,1:T(8,128)S(1)}, f3...) fusion(f32[72,12,132]{0,2,1:T(8,128)S(1)} %fusion.30, f32[10,130]{1,0:T(8,128)S(1)} %slice.169), kind=kLoop, calls=%fused_computation.179 | loop fusion | flops 218400 | bytes 2002000 | tf_op jit(solution)/shard_map/slice | solution.py:55
  51.0 6.0 %collective-permute-start.4 = (bf16[24,16,64]{2,1,0:T(8,128)(2,1)S(1)}, bf16[24,16,64]{2,1,0:T(8,128)(2,1)S(1)}, u32[]{:S(2)}, u32[]{:S(2)}) collective-permute-start(bf16[24,16,64]{2,1,0:T(8,128)(2,1)S(1)} %copy.37), channel_id=1, source_target_pairs={{0,2},{1,3},{2,0},{3,1},{4,6},{5,7},{6,4},{7,5},{8,10},{9,11},{10,... | collective-permute-start | bytes 147464 | tf_op jit(solution)/shard_map/ppermute | solution.py:21
  57.0 6.9 %collective-permute-start.5 = (bf16[24,16,64]{2,1,0:T(8,128)(2,1)S(1)}, bf16[24,16,64]{2,1,0:T(8,128)(2,1)S(1)}, u32[]{:S(2)}, u32[]{:S(2)}) collective-permute-start(bf16[24,16,64]{2,1,0:T(8,128)(2,1)S(1)} %copy.37), channel_id=1, source_target_pairs={{0,62},{1,63},{2,4},{3,5},{4,2},{5,3},{6,8},{7,9},{8,6},{9,7},{10,... | collective-permute-start | bytes 147464 | tf_op jit(solution)/shard_map/ppermute | solution.py:21
  64.2 2.4 %collective-permute-done.5 = bf16[24,16,64]{2,1,0:T(8,128)(2,1)S(1)} collective-permute-done((bf16[24,16,64]{2,1,0:T(8,128)(2,1)S(1)}, bf16[24,16,64]{2,1,0:T(8,128)(2,1)S(1)}, u32[]{:S(2)}, u32[]{:S(2)}) %collective-permute-start.5) | collective-permute-done | bytes 49184 | tf_op jit(solution)/shard_map/ppermute | solution.py:21
  66.6 6.4 %collective-permute-start.6 = (bf16[24,32,64]{2,1,0:T(8,128)(2,1)S(1)}, bf16[24,32,64]{2,1,0:T(8,128)(2,1)S(1)}, u32[]{:S(2)}, u32[]{:S(2)}) collective-permute-start(bf16[24,32,64]{2,1,0:T(8,128)(2,1)S(1)} %pad_maximum_fusion.1), channel_id=1, source_target_pairs={{0,1},{1,0},{2,3},{3,2},{4,5},{5,4},{6,7},{7,6},{8,9},{9,8},{10,11... | collective-permute-start | bytes 294920 | tf_op jit(solution)/shard_map/ppermute | solution.py:21
  73.4 0.7 collective-permute-done.6
  74.4 0.9 fusion.9
  76.7 1.0 %fusion.3 = bf16[8,2048]{1,0:T(8,128)(2,1)S(1)} fusion(f32[8,2048]{1,0:T(8,128)} %convolution_bitcast_fusion.1, f32[8,24]{1,0:T(8,128)} %fusion.90, f32[24,2048]{1,0:T(8,128)S(1)} %reshape.178, pred[2048]{0:T(1024)(128)(4,1)S(1)} %broadcast_compare_fusion), kind=kOutput, calls=%fused_computation.7 | convolution fusion | flops 2408448 | bytes 297728 | tf_op jit(solution)/shard_map/dot_general | solution.py:156
  77.9 1.9 %collective-permute-start.7 = (bf16[8,32,64]{2,1,0:T(8,128)(2,1)S(1)}, bf16[8,32,64]{2,1,0:T(8,128)(2,1)S(1)}, u32[]{:S(2)}, u32[]{:S(2)}) collective-permute-start(bf16[8,32,64]{2,1,0:T(8,128)(2,1)S(1)} %reshape.179), channel_id=1, source_target_pairs={{0,2},{1,3},{2,0},{3,1},{4,6},{5,7},{6,4},{7,5},{8,10},{9,11},{10,... | collective-permute-start | bytes 98312 | tf_op jit(solution)/shard_map/ppermute | solution.py:21
  79.8 5.5 %collective-permute-start.8 = (bf16[8,32,64]{2,1,0:T(8,128)(2,1)S(1)}, bf16[8,32,64]{2,1,0:T(8,128)(2,1)S(1)}, u32[]{:S(2)}, u32[]{:S(2)}) collective-permute-start(bf16[8,32,64]{2,1,0:T(8,128)(2,1)S(1)} %reshape.179), channel_id=1, source_target_pairs={{0,62},{1,63},{2,4},{3,5},{4,2},{5,3},{6,8},{7,9},{8,6},{9,7},{10,... | collective-permute-start | bytes 98312 | tf_op jit(solution)/shard_map/ppermute | solution.py:21
  85.4 2.6 %fusion.1 = f32[80,2048]{1,0:T(8,128)} fusion(f32[80,2048]{1,0:T(8,128)} %param.20, f32[80,2048]{1,0:T(8,128)} %convolution_add_fusion, f32[24,2048]{1,0:T(8,128)S(1)} %reshape.178, f32[80,24]{0,1:T(8,128)S(1)} %copy-done.6, pred[2048]{0:T(1024)(128)(4,1)S(1)} %broadcast_compare_fusion), kind=kOutput, calls=%fused_computation.3 | convolution fusion | flops 23920640 | bytes 2172416 | tf_op jit(solution)/shard_map/dot_general | solution.py:152
  88.7 1.3 %fusion.8 = f32[72,8,128]{0,2,1:T(8,128)} fusion(f32[72,10,130]{0,2,1:T(8,128)S(1)} %fusion.5, f32[8,128]{1,0:T(8,128)S(1)} %copy-done.10, f32[72,72]{1,0:T(8,128)S(1)} %copy-done.5), kind=kOutput, calls=%fused_computation.17 | convolution fusion | flops 32440320 | bytes 3481600 | tf_op jit(solution)/shard_map/ml,l...->m.../dot_general | solution.py:49
  90.3 2.6 %collective-permute-start.9 = (bf16[8,64,64]{2,1,0:T(8,128)(2,1)S(1)}, bf16[8,64,64]{2,1,0:T(8,128)(2,1)S(1)}, u32[]{:S(2)}, u32[]{:S(2)}) collective-permute-start(bf16[8,64,64]{2,1,0:T(8,128)(2,1)S(1)} %pad_maximum_fusion.6), channel_id=1, source_target_pairs={{0,1},{1,0},{2,3},{3,2},{4,5},{5,4},{6,7},{7,6},{8,9},{9,8},{10,11... | collective-permute-start | bytes 196616 | tf_op jit(solution)/shard_map/ppermute | solution.py:21
  93.1 0.7 collective-permute-done.9
  94.9 1.6 %fusion.7 = f32[72,8,128]{0,2,1:T(8,128)S(1)} fusion(f32[72,8,128]{0,2,1:T(8,128)} %fusion.8, f32[8,8,128]{2,1,0:T(8,128)S(1)} %reshape.181, f32[72,8]{0,1:T(8,128)S(1)} %copy-done.14), kind=kOutput, calls=%fused_computation.15 | convolution fusion | flops 3612672 | bytes 624896 | tf_op jit(solution)/shard_map/ml,l...->m.../dot_general | solution.py:49
  96.6 0.9 copy.51
  (105 shorter events, 12.6 us)
Async XLA Ops:
  0.6 75.2 %copy-start = (bf16[32,4,64,64]{3,2,1,0:T(8,128)(2,1)S(1)}, bf16[32,4,64,64]{3,2,1,0:T(8,128)(2,1)}, u32[]{:S(2)}) copy-start(bf16[32,4,64,64]{3,2,1,0:T(8,128)(2,1)} %param.18) | copy-start | bytes 3145732
  0.6 24.0 %copy-start.4 = (f32[72,72]{1,0:T(8,128)S(1)}, f32[72,72]{1,0:T(8,128)}, u32[]{:S(2)}) copy-start(f32[72,72]{1,0:T(8,128)} %param.16) | copy-start | bytes 62212
  0.7 24.0 %copy-start.7 = (f32[24,72]{1,0:T(8,128)S(1)}, f32[24,72]{1,0:T(8,128)}, u32[]{:S(2)}) copy-start(f32[24,72]{1,0:T(8,128)} %param.17) | copy-start | bytes 20740
  0.7 24.3 %copy-start.16 = (s32[32,4]{0,1:T(4,128)S(1)}, s32[32,4]{0,1:T(4,128)}, u32[]{:S(2)}) copy-start(s32[32,4]{0,1:T(4,128)} %param.19) | copy-start | bytes 1540
  2.9 27.4 %copy-start.6 = (f32[80,24]{0,1:T(8,128)S(1)}, f32[80,24]{0,1:T(8,128)}, u32[]{:S(2)}) copy-start(f32[80,24]{0,1:T(8,128)} %param.22) | copy-start | bytes 23044
  2.9 27.4 %copy-start.8 = (f32[8,80]{1,0:T(8,128)S(1)}, f32[8,80]{1,0:T(8,128)}, u32[]{:S(2)}) copy-start(f32[8,80]{1,0:T(8,128)} %param.24) | copy-start | bytes 7684
  4.1 30.5 %collective-permute-start.1 = (f32[1168]{0:T(1024)}, f32[1168]{0:T(1024)}, u32[]{:S(2)}, u32[]{:S(2)}) collective-permute-start(f32[1168]{0:T(1024)} %select_n.220), channel_id=1, source_target_pairs={{0,1},{1,0},{2,3},{3,2},{4,5},{5,4},{6,7},{7,6},{8,9},{9,8},{10,11... | collective-permute-start | bytes 14024 | tf_op jit(solution)/shard_map/ppermute | solution.py:21
  21.1 13.4 %collective-permute-start = (f32[1168]{0:T(1024)}, f32[1168]{0:T(1024)S(1)}, u32[]{:S(2)}, u32[]{:S(2)}) collective-permute-start(f32[1168]{0:T(1024)} %select_n.218), channel_id=1, source_target_pairs={{0,63},{1,2},{2,1},{3,4},{4,3},{5,6},{6,5},{7,8},{8,7},{9,10},{10,... | collective-permute-start | bytes 14024 | tf_op jit(solution)/shard_map/ppermute | solution.py:21
  25.2 47.8 %copy-start.11 = (s32[128]{0:T(128)}, s32[128]{0:T(128)S(1)}, u32[]{:S(2)}) copy-start(s32[128]{0:T(128)S(1)} %eq.182) | copy-start | bytes 1540
  30.2 4.3 %copy-start.12 = (s32[64]{0:T(128)}, s32[64]{0:T(128)S(1)}, u32[]{:S(2)}) copy-start(s32[64]{0:T(128)S(1)} %eq.200) | copy-start | bytes 772
  36.3 9.1 %collective-permute-start.3 = (f32[73,2,132]{0,2,1:T(8,128)S(1)}, f32[73,2,132]{0,2,1:T(8,128)S(1)}, u32[]{:S(2)}, u32[]{:S(2)}) collective-permute-start(f32[73,2,132]{0,2,1:T(8,128)S(1)} %broadcast_select_fusion.3), channel_id=1, source_target_pairs={{0,64},{64,0},{128,192},{192,128},{256,320},{320,256},{384,448},{4... | collective-permute-start | bytes 231272 | tf_op jit(solution)/shard_map/ppermute | solution.py:21
  38.2 9.1 %collective-permute-start.2 = (f32[73,2,132]{0,2,1:T(8,128)S(1)}, f32[73,2,132]{0,2,1:T(8,128)S(1)}, u32[]{:S(2)}, u32[]{:S(2)}) collective-permute-start(f32[73,2,132]{0,2,1:T(8,128)S(1)} %get-tuple-element.8), channel_id=1, source_target_pairs={{0,960},{64,128},{128,64},{192,256},{256,192},{320,384},{384,320},... | collective-permute-start | bytes 231272 | tf_op jit(solution)/shard_map/ppermute | solution.py:21
  48.5 1.7 %copy-start.9 = (f32[8,128]{1,0:T(8,128)}, f32[8,128]{1,0:T(8,128)S(1)}, u32[]{:S(2)}) copy-start(f32[8,128]{1,0:T(8,128)S(1)} %slice.158) | copy-start | bytes 12292
  50.1 13.7 %copy-start.18 = (s32[16]{0:T(128)S(1)}, s32[16]{0:T(128)}, u32[]{:S(2)}) copy-start(s32[16]{0:T(128)} %iota_add_fusion.5) | copy-start | bytes 196
  50.2 22.9 %copy-start.20 = (s32[16]{0:T(128)S(1)}, s32[16]{0:T(128)}, u32[]{:S(2)}) copy-start(s32[16]{0:T(128)} %iota_add_fusion.4) | copy-start | bytes 196
  51.0 23.4 %copy-start.21 = (s32[16]{0:T(128)S(1)}, s32[16]{0:T(128)}, u32[]{:S(2)}) copy-start(s32[16]{0:T(128)} %iota_add_fusion.3) | copy-start | bytes 196
  51.0 13.2 %collective-permute-start.4 = (bf16[24,16,64]{2,1,0:T(8,128)(2,1)S(1)}, bf16[24,16,64]{2,1,0:T(8,128)(2,1)S(1)}, u32[]{:S(2)}, u32[]{:S(2)}) collective-permute-start(bf16[24,16,64]{2,1,0:T(8,128)(2,1)S(1)} %copy.37), channel_id=1, source_target_pairs={{0,2},{1,3},{2,0},{3,1},{4,6},{5,7},{6,4},{7,5},{8,10},{9,11},{10,... | collective-permute-start | bytes 147464 | tf_op jit(solution)/shard_map/ppermute | solution.py:21
  57.0 9.6 %collective-permute-start.5 = (bf16[24,16,64]{2,1,0:T(8,128)(2,1)S(1)}, bf16[24,16,64]{2,1,0:T(8,128)(2,1)S(1)}, u32[]{:S(2)}, u32[]{:S(2)}) collective-permute-start(bf16[24,16,64]{2,1,0:T(8,128)(2,1)S(1)} %copy.37), channel_id=1, source_target_pairs={{0,62},{1,63},{2,4},{3,5},{4,2},{5,3},{6,8},{7,9},{8,6},{9,7},{10,... | collective-permute-start | bytes 147464 | tf_op jit(solution)/shard_map/ppermute | solution.py:21
  66.6 7.5 %collective-permute-start.6 = (bf16[24,32,64]{2,1,0:T(8,128)(2,1)S(1)}, bf16[24,32,64]{2,1,0:T(8,128)(2,1)S(1)}, u32[]{:S(2)}, u32[]{:S(2)}) collective-permute-start(bf16[24,32,64]{2,1,0:T(8,128)(2,1)S(1)} %pad_maximum_fusion.1), channel_id=1, source_target_pairs={{0,1},{1,0},{2,3},{3,2},{4,5},{5,4},{6,7},{7,6},{8,9},{9,8},{10,11... | collective-permute-start | bytes 294920 | tf_op jit(solution)/shard_map/ppermute | solution.py:21
  76.4 11.5 %copy-start.2 = (f32[73,12,132]{0,2,1:T(8,128)S(1)}, f32[73,12,132]{0,2,1:T(8,128)}, u32[]{:S(2)}) copy-start(f32[73,12,132]{0,2,1:T(8,128)} %copy-done.1) | copy-start | bytes 1387588
  76.7 11.3 %copy-start.5 = (f32[72,72]{1,0:T(8,128)S(1)}, f32[72,72]{1,0:T(8,128)}, u32[]{:S(2)}) copy-start(f32[72,72]{1,0:T(8,128)} %param.16) | copy-start | bytes 62212
  77.9 10.8 %copy-start.10 = (f32[8,128]{1,0:T(8,128)S(1)}, f32[8,128]{1,0:T(8,128)}, u32[]{:S(2)}) copy-start(f32[8,128]{1,0:T(8,128)} %copy-done.9) | copy-start | bytes 12292
  77.9 12.3 %collective-permute-start.7 = (bf16[8,32,64]{2,1,0:T(8,128)(2,1)S(1)}, bf16[8,32,64]{2,1,0:T(8,128)(2,1)S(1)}, u32[]{:S(2)}, u32[]{:S(2)}) collective-permute-start(bf16[8,32,64]{2,1,0:T(8,128)(2,1)S(1)} %reshape.179), channel_id=1, source_target_pairs={{0,2},{1,3},{2,0},{3,1},{4,6},{5,7},{6,4},{7,5},{8,10},{9,11},{10,... | collective-permute-start | bytes 98312 | tf_op jit(solution)/shard_map/ppermute | solution.py:21
  79.8 10.4 %collective-permute-start.8 = (bf16[8,32,64]{2,1,0:T(8,128)(2,1)S(1)}, bf16[8,32,64]{2,1,0:T(8,128)(2,1)S(1)}, u32[]{:S(2)}, u32[]{:S(2)}) collective-permute-start(bf16[8,32,64]{2,1,0:T(8,128)(2,1)S(1)} %reshape.179), channel_id=1, source_target_pairs={{0,62},{1,63},{2,4},{3,5},{4,2},{5,3},{6,8},{7,9},{8,6},{9,7},{10,... | collective-permute-start | bytes 98312 | tf_op jit(solution)/shard_map/ppermute | solution.py:21
  88.0 2.0 %copy-start.13 = (s32[64]{0:T(128)S(1)}, s32[64]{0:T(128)}, u32[]{:S(2)}) copy-start(s32[64]{0:T(128)} %copy-done.12) | copy-start | bytes 772
  88.0 2.0 %copy-start.17 = (s32[32]{0:T(128)S(1)}, s32[32]{0:T(128)}, u32[]{:S(2)}) copy-start(s32[32]{0:T(128)} %iota_add_fusion.2) | copy-start | bytes 388
  88.0 4.9 %copy-start.19 = (s32[32]{0:T(128)S(1)}, s32[32]{0:T(128)}, u32[]{:S(2)}) copy-start(s32[32]{0:T(128)} %iota_add_fusion.1) | copy-start | bytes 388
  88.6 5.2 %copy-start.15 = (s32[64]{0:T(128)S(1)}, s32[64]{0:T(128)}, u32[]{:S(2)}) copy-start(s32[64]{0:T(128)} %compare_select_fusion.1) | copy-start | bytes 772
  88.6 5.4 %copy-start.22 = (s32[32]{0:T(128)S(1)}, s32[32]{0:T(128)}, u32[]{:S(2)}) copy-start(s32[32]{0:T(128)} %iota_add_fusion) | copy-start | bytes 388
  88.7 5.8 %copy-start.3 = (bf16[16,4,64,64]{3,2,1,0:T(8,128)(2,1)S(1)}, bf16[16,4,64,64]{3,2,1,0:T(8,128)(2,1)}, u32[]{:S(2)}) copy-start(bf16[16,4,64,64]{3,2,1,0:T(8,128)(2,1)} %param.25) | copy-start | bytes 1572868
  90.0 5.0 %copy-start.14 = (f32[72,8]{0,1:T(8,128)S(1)}, f32[72,8]{0,1:T(8,128)}, u32[]{:S(2)}) copy-start(f32[72,8]{0,1:T(8,128)} %param.27) | copy-start | bytes 6916
  90.3 3.5 %collective-permute-start.9 = (bf16[8,64,64]{2,1,0:T(8,128)(2,1)S(1)}, bf16[8,64,64]{2,1,0:T(8,128)(2,1)S(1)}, u32[]{:S(2)}, u32[]{:S(2)}) collective-permute-start(bf16[8,64,64]{2,1,0:T(8,128)(2,1)S(1)} %pad_maximum_fusion.6), channel_id=1, source_target_pairs={{0,1},{1,0},{2,3},{3,2},{4,5},{5,4},{6,7},{7,6},{8,9},{9,8},{10,11... | collective-permute-start | bytes 196616 | tf_op jit(solution)/shard_map/ppermute | solution.py:21
  (1 other events, 0.9 us)

commit v7 on v4

--- a/solution.py
+++ b/solution.py
@@ -131,9 +131,13 @@
     )
     remapped = block_product(remap_weight, exchange_and_pick(surface_blocks, remap_cols, here))
     remapped = remapped.reshape(fields, ocean_blocks * 64)
+    wet = wet_mask[None] == 1
     stepped = mixed + jnp.dot(forcing, remapped, precision=lax.Precision.HIGHEST)
-    ocean_out = jnp.where(wet_mask[None] == 1, stepped, ocean_state)
-    sea = jnp.dot(surface_proj, ocean_out, precision=lax.Precision.HIGHEST).astype(jnp.bfloat16)
+    ocean_out = jnp.where(wet, stepped, ocean_state)
+    settled = jnp.dot(surface_proj, jnp.where(wet, mixed, ocean_state), precision=lax.Precision.HIGHEST)
+    sea_forcing = jnp.dot(surface_proj, forcing, precision=lax.Precision.HIGHEST)
+    moved = jnp.dot(sea_forcing, remapped, precision=lax.Precision.HIGHEST)
+    sea = (settled + jnp.where(wet, moved, 0.0)).astype(jnp.bfloat16)
     sea_blocks = sea.reshape(sea.shape[0], ocean_blocks, 64)
     returned = block_product(back_weight, exchange_and_pick(sea_blocks, back_cols, here))
     returned = returned.reshape(sea.shape[0], rows_here, cols_here)

time: 92.4 us -> 97.4 us (1.054)
  matrix products: 14.1 us -> 19.3 us
  waiting for transfers between devices: 8.34 us -> 6.39 us
  other arithmetic: 3.39 us -> 4.81 us
    dot_general x1 -> x3, matrix products: 0.46 us -> 4.19 us  [the longest x1 2.39 us: body(): jnp.dot(surface_proj, jnp.where(wet, mixed, ocean_state), precision=lax.P...]
    ppermute x10, waiting for transfers between devices: 8.34 us -> 6.39 us  [swap(): return lax.ppermute(value, axis, pairs)]
    dot_general x2, matrix products: 2.22 us -> 3.42 us  [block_product(): jnp.einsum('okij,fokj->foi', weights, picked, preferred_element_type=jnp....]
    dot_general x4, matrix products: 4.38 us -> 3.35 us  [level_mix(): jnp.einsum('ml,l...->m...', matrix, field, precision=lax.Precision.HIGHEST)]
    unnamed x36 -> x42, local copies, waits for them, and re-layouts: 2.29 us -> 2.3 us
  transfers between devices with their start and end apart: 10 -> 10, of which waited for: 5 -> 5; matrix products, arithmetic and copies ran while one was open for 8% -> 15% of each run, Pallas kernels for 0% -> 0%
where the time goes in v7:
time: 97.4 us; the launch traced here: 96.6 us
  starting transfers between devices  56.7 us (58%)
  matrix products  19.3 us (20%)
  local copies, waits for them, and re-layouts  8.14 us (8%)
  waiting for transfers between devices  6.39 us (7%)
  other arithmetic  4.81 us (5%)
  between operations  1.3 us (1%)
    ppermute x10, starting transfers between devices, swap(): return lax.ppermute(value, axis, pairs)  56.7 us
    ppermute x10, waiting for transfers between devices, swap(): return lax.ppermute(value, axis, pairs)  6.39 us
    dot_general x2, matrix products, block_product(): jnp.einsum('okij,fokj->foi', weights, picked, preferred_element_type=jnp....  3.42 us
    dot_general x4, matrix products, level_mix(): jnp.einsum('ml,l...->m...', matrix, field, precision=lax.Precision.HIGHEST)  3.35 us
    dot_general x8, matrix products, pick(): jnp.einsum('qb,fbj->fqj', onehot, piece, preferred_element_type=jnp.float32)  2.92 us
    dot_general x1, matrix products, body(): jnp.dot(ocean_mix, ocean_state, precision=lax.Precision.HIGHEST)  2.79 us
    dot_general x1, matrix products, body(): jnp.dot(forcing, remapped, precision=lax.Precision.HIGHEST)  2.65 us
    dot_general x1, matrix products, body(): jnp.dot(surface_proj, jnp.where(wet, mixed, ocean_state), precision=lax.P...  2.39 us
  transfers between devices with their start and end apart: 10, of which 5 were waited for; matrix products, arithmetic and copies ran while one was open for 15% of the time, Pallas kernels for 0%

profile of v7, /device:TPU:1, one launch (start us, length us, event | category | flops | bytes accessed | tf_op | source)
XLA Modules:
  0.0 96.6 jit_solution(4484992816848072790)
XLA Ops:
  0.7 1.3 %copy.27 = f32[72,8,128]{0,2,1:T(8,128)S(1)} copy(f32[72,8,128]{2,1,0:T(8,128)} %param.14) | data formatting | bytes 589824 | tf_op args[0]
  2.0 0.9 copy.28
  3.5 16.1 %collective-permute-start.1 = (f32[1168]{0:T(1024)S(1)}, f32[1168]{0:T(1024)S(1)}, u32[]{:S(2)}, u32[]{:S(2)}) collective-permute-start(f32[1168]{0:T(1024)S(1)} %select_n.220), channel_id=1, source_target_pairs={{0,1},{1,0},{2,3},{3,2},{4,5},{5,4},{6,7},{7,6},{8,9},{9,8},{10,11... | collective-permute-start | bytes 14024 | tf_op jit(solution)/shard_map/ppermute | solution.py:21
  20.0 1.9 %collective-permute-start = (f32[1168]{0:T(1024)S(1)}, f32[1168]{0:T(1024)S(1)}, u32[]{:S(2)}, u32[]{:S(2)}) collective-permute-start(f32[1168]{0:T(1024)S(1)} %select_n.218), channel_id=1, source_target_pairs={{0,63},{1,2},{2,1},{3,4},{4,3},{5,6},{6,5},{7,8},{8,7},{9,10},{10,... | collective-permute-start | bytes 14024 | tf_op jit(solution)/shard_map/ppermute | solution.py:21
  24.0 2.8 %convolution_add_fusion = f32[80,2048]{1,0:T(8,128)} fusion(f32[80,2048]{1,0:T(8,128)} %param.20, f32[80,80]{1,0:T(8,128)S(1)} %copy-done.5), kind=kOutput, calls=%fused_computation | convolution fusion | flops 157450240 | bytes 1336320 | tf_op jit(solution)/shard_map/dot_general | solution.py:130
  26.8 0.7 fusion.75
  27.7 0.7 fusion.78
  28.5 2.4 %convolution_bitcast_fusion.1 = f32[8,2048]{1,0:T(8,128)} fusion(f32[8,80]{1,0:T(8,128)S(1)} %copy-done.6, f32[80,2048]{1,0:T(8,128)} %convolution_add_fusion, f32[80,2048]{1,0:T(8,128)} %param.20, pred[2048]{0:T(1024)(128)(4,1)S(1)} %broadcast_compare_fusion), kind=kOutput, calls=%fused_computation.6 | convolution fusion | flops 15892480 | bytes 1380864 | tf_op jit(solution)/shard_map/dot_general | solution.py:137
  33.0 1.9 %collective-permute-start.3 = (f32[73,2,132]{0,2,1:T(8,128)S(1)}, f32[73,2,132]{0,2,1:T(8,128)S(1)}, u32[]{:S(2)}, u32[]{:S(2)}) collective-permute-start(f32[73,2,132]{0,2,1:T(8,128)S(1)} %broadcast_select_fusion.3), channel_id=1, source_target_pairs={{0,64},{64,0},{128,192},{192,128},{256,320},{320,256},{384,448},{4... | collective-permute-start | bytes 231272 | tf_op jit(solution)/shard_map/ppermute | solution.py:21
  34.9 6.7 %collective-permute-start.2 = (f32[73,2,132]{0,2,1:T(8,128)S(1)}, f32[73,2,132]{0,2,1:T(8,128)S(1)}, u32[]{:S(2)}, u32[]{:S(2)}) collective-permute-start(f32[73,2,132]{0,2,1:T(8,128)S(1)} %get-tuple-element.6), channel_id=1, source_target_pairs={{0,960},{64,128},{128,64},{192,256},{256,192},{320,384},{384,320},... | collective-permute-start | bytes 231272 | tf_op jit(solution)/shard_map/ppermute | solution.py:21
  42.2 1.8 %collective-permute-done.2 = f32[73,2,132]{0,2,1:T(8,128)S(1)} collective-permute-done((f32[73,2,132]{0,2,1:T(8,128)S(1)}, f32[73,2,132]{0,2,1:T(8,128)S(1)}, u32[]{:S(2)}, u32[]{:S(2)}) %collective-permute-start.2) | collective-permute-done | bytes 77120 | tf_op jit(solution)/shard_map/ppermute | solution.py:21
  44.3 0.7 slice_reduce_fusion
  45.2 1.1 %fusion.16 = f32[72,10,130]{0,2,1:T(8,128)S(1)} fusion(f32[73,12,132]{0,2,1:T(8,128)S(1)} %pad_maximum_fusion, f32[73,2,132]{0,2,1:T(8,128)S(1)} %get-tuple-element.12, f32[73,8,2]{0,2,1:T(2,128)S(1)} %copy.32, f32[73,8,2]{0,2,1:T(2,128)S(1)} %copy.31, f32[1,8,128]{0,2,1:T(8,128)S(1)} %copy.28, f32[72,8,128]{0,2,1:T(8,128)S(1)} %copy.27, ...), kind=kOutput, calls=%fused_computation.33 | convolution fusion | flops 82368000 | bytes 4556416 | tf_op jit(solution)/shard_map/ml,l...->m.../dot_general | solution.py:49
  46.2 0.7 fusion.7
  47.7 6.0 %collective-permute-start.4 = (bf16[24,16,64]{2,1,0:T(8,128)(2,1)S(1)}, bf16[24,16,64]{2,1,0:T(8,128)(2,1)S(1)}, u32[]{:S(2)}, u32[]{:S(2)}) collective-permute-start(bf16[24,16,64]{2,1,0:T(8,128)(2,1)S(1)} %reshape.176), channel_id=1, source_target_pairs={{0,2},{1,3},{2,0},{3,1},{4,6},{5,7},{6,4},{7,5},{8,10},{9,11},{10,... | collective-permute-start | bytes 147464 | tf_op jit(solution)/shard_map/ppermute | solution.py:21
  53.7 6.9 %collective-permute-start.5 = (bf16[24,16,64]{2,1,0:T(8,128)(2,1)S(1)}, bf16[24,16,64]{2,1,0:T(8,128)(2,1)S(1)}, u32[]{:S(2)}, u32[]{:S(2)}) collective-permute-start(bf16[24,16,64]{2,1,0:T(8,128)(2,1)S(1)} %reshape.176), channel_id=1, source_target_pairs={{0,62},{1,63},{2,4},{3,5},{4,2},{5,3},{6,8},{7,9},{8,6},{9,7},{10,... | collective-permute-start | bytes 147464 | tf_op jit(solution)/shard_map/ppermute | solution.py:21
  60.9 2.4 %collective-permute-done.5 = bf16[24,16,64]{2,1,0:T(8,128)(2,1)S(1)} collective-permute-done((bf16[24,16,64]{2,1,0:T(8,128)(2,1)S(1)}, bf16[24,16,64]{2,1,0:T(8,128)(2,1)S(1)}, u32[]{:S(2)}, u32[]{:S(2)}) %collective-permute-start.5) | collective-permute-done | bytes 49184 | tf_op jit(solution)/shard_map/ppermute | solution.py:21
  63.3 6.4 %collective-permute-start.6 = (bf16[24,32,64]{2,1,0:T(8,128)(2,1)S(1)}, bf16[24,32,64]{2,1,0:T(8,128)(2,1)S(1)}, u32[]{:S(2)}, u32[]{:S(2)}) collective-permute-start(bf16[24,32,64]{2,1,0:T(8,128)(2,1)S(1)} %pad_maximum_fusion.9), channel_id=1, source_target_pairs={{0,1},{1,0},{2,3},{3,2},{4,5},{5,4},{6,7},{7,6},{8,9},{9,8},{10,11... | collective-permute-start | bytes 294920 | tf_op jit(solution)/shard_map/ppermute | solution.py:21
  70.1 0.7 collective-permute-done.6
  71.1 1.0 %fusion.8 = bf16[24,128,64]{1,2,0:T(8,128)(2,1)S(1)} fusion(f32[24,64,128]{2,1,0:T(8,128)S(1)} %fusion.35, f32[24,64,128]{2,1,0:T(8,128)S(1)} %convolution_add_fusion.2, bf16[24,16,64]{2,1,0:T(8,128)(2,1)S(1)} %collective-permute-done.5, s32[128]{0:T(128)} %copy-done.7, s32[16]{0:T(128)S(1)} %copy-done.17), kind=kOutput, calls=%fused_computation.17 | convolution fusion | flops 6883328 | bytes 2015808 | tf_op jit(solution)/shard_map/qb,fbj->fqj/dot_general | solution.py:72
  72.2 1.3 %copy.38 = bf16[24,128,64]{2,0,1:T(8,128)(2,1)} copy(bf16[24,128,64]{1,2,0:T(8,128)(2,1)S(1)} %fusion.8) | data formatting | bytes 786432 | tf_op jit(solution)/shard_map/convert_element_type | solution.py:97
  73.4 1.8 %convolution_bitcast_fusion.5 = f32[24,32,64]{2,0,1:T(8,128)S(1)} fusion(bf16[24,32,4,64]{3,0,2,1:T(8,128)(2,1)} %bitcast.99, bf16[32,4,64,64]{3,2,1,0:T(8,128)(2,1)S(1)} %copy-done), kind=kOutput, calls=%fused_computation.18 | convolution fusion | flops 25165824 | bytes 1638400 | tf_op jit(solution)/shard_map/okij,fokj->foi/dot_general | solution.py:61
  75.6 1.1 %fusion.3 = bf16[8,2048]{1,0:T(8,128)(2,1)S(1)} fusion(f32[8,2048]{1,0:T(8,128)} %convolution_bitcast_fusion.1, f32[8,24]{1,0:T(8,128)} %fusion.78, f32[24,2048]{1,0:T(8,128)S(1)} %reshape.178, pred[2048]{0:T(1024)(128)(4,1)S(1)} %broadcast_compare_fusion), kind=kOutput, calls=%fused_computation.7 | convolution fusion | flops 4767744 | bytes 297728 | tf_op jit(solution)/shard_map/dot_general | solution.py:139
  76.8 1.9 %collective-permute-start.7 = (bf16[8,32,64]{2,1,0:T(8,128)(2,1)S(1)}, bf16[8,32,64]{2,1,0:T(8,128)(2,1)S(1)}, u32[]{:S(2)}, u32[]{:S(2)}) collective-permute-start(bf16[8,32,64]{2,1,0:T(8,128)(2,1)S(1)} %reshape.179), channel_id=1, source_target_pairs={{0,2},{1,3},{2,0},{3,1},{4,6},{5,7},{6,4},{7,5},{8,10},{9,11},{10,... | collective-permute-start | bytes 98312 | tf_op jit(solution)/shard_map/ppermute | solution.py:21
  78.7 5.5 %collective-permute-start.8 = (bf16[8,32,64]{2,1,0:T(8,128)(2,1)S(1)}, bf16[8,32,64]{2,1,0:T(8,128)(2,1)S(1)}, u32[]{:S(2)}, u32[]{:S(2)}) collective-permute-start(bf16[8,32,64]{2,1,0:T(8,128)(2,1)S(1)} %reshape.179), channel_id=1, source_target_pairs={{0,62},{1,63},{2,4},{3,5},{4,2},{5,3},{6,8},{7,9},{8,6},{9,7},{10,... | collective-permute-start | bytes 98312 | tf_op jit(solution)/shard_map/ppermute | solution.py:21
  84.3 2.6 %fusion.1 = f32[80,2048]{1,0:T(8,128)} fusion(f32[80,2048]{1,0:T(8,128)S(1)} %copy-done.1, f32[80,2048]{1,0:T(8,128)} %convolution_add_fusion, f32[24,2048]{1,0:T(8,128)S(1)} %reshape.178, f32[80,24]{0,1:T(8,128)S(1)} %copy-done.4, pred[2048]{0:T(1024)(128)(4,1)S(1)} %broadcast_compare_fusion), kind=kOutput, calls=%fused_computation.3 | convolution fusion | flops 47513600 | bytes 2172416 | tf_op jit(solution)/shard_map/dot_general | solution.py:135
  87.2 0.8 collective-permute-done.8
  88.0 3.4 %collective-permute-start.9 = (bf16[8,64,64]{2,1,0:T(8,128)(2,1)S(1)}, bf16[8,64,64]{2,1,0:T(8,128)(2,1)S(1)}, u32[]{:S(2)}, u32[]{:S(2)}) collective-permute-start(bf16[8,64,64]{2,1,0:T(8,128)(2,1)S(1)} %pad_maximum_fusion.14), channel_id=1, source_target_pairs={{0,1},{1,0},{2,3},{3,2},{4,5},{5,4},{6,7},{7,6},{8,9},{9,8},{10,11... | collective-permute-start | bytes 196616 | tf_op jit(solution)/shard_map/ppermute | solution.py:21
  91.7 0.7 collective-permute-done.9
  93.0 1.6 %convolution_bitcast_fusion.6 = f32[8,16,64]{2,0,1:T(8,128)S(1)} fusion(bf16[8,16,4,64]{3,0,2,1:T(8,128)(2,1)S(1)} %bitcast.100, bf16[16,4,64,64]{3,2,1,0:T(8,128)(2,1)} %param.25), kind=kOutput, calls=%fused_computation.25 | convolution fusion | flops 4194304 | bytes 622592 | tf_op jit(solution)/shard_map/okij,fokj->foi/dot_general | solution.py:61
  94.7 1.0 %fusion.6 = f32[72,8,128]{0,2,1:T(8,128)S(1)} fusion(f32[72,8,128]{0,2,1:T(8,128)S(1)} %copy-done.3, f32[8,8,128]{2,1,0:T(8,128)S(1)} %reshape.181, f32[72,8]{0,1:T(8,128)S(1)} %copy-done.12), kind=kOutput, calls=%fused_computation.14 | convolution fusion | flops 7151616 | bytes 624896 | tf_op jit(solution)/shard_map/ml,l...->m.../dot_general | solution.py:49
  95.7 0.9 copy.46
  (96 shorter events, 9.6 us)
Async XLA Ops:
  0.6 72.8 %copy-start = (bf16[32,4,64,64]{3,2,1,0:T(8,128)(2,1)S(1)}, bf16[32,4,64,64]{3,2,1,0:T(8,128)(2,1)}, u32[]{:S(2)}) copy-start(bf16[32,4,64,64]{3,2,1,0:T(8,128)(2,1)} %param.18) | copy-start | bytes 3145732
  0.6 21.9 %copy-start.14 = (s32[32,4]{0,1:T(4,128)S(1)}, s32[32,4]{0,1:T(4,128)}, u32[]{:S(2)}) copy-start(s32[32,4]{0,1:T(4,128)} %param.19) | copy-start | bytes 1540
  0.7 23.3 %copy-start.5 = (f32[80,80]{1,0:T(8,128)S(1)}, f32[80,80]{1,0:T(8,128)}, u32[]{:S(2)}) copy-start(f32[80,80]{1,0:T(8,128)} %param.21) | copy-start | bytes 76804
  2.0 25.7 %copy-start.4 = (f32[80,24]{0,1:T(8,128)S(1)}, f32[80,24]{0,1:T(8,128)}, u32[]{:S(2)}) copy-start(f32[80,24]{0,1:T(8,128)} %param.22) | copy-start | bytes 23044
  2.0 25.7 %copy-start.6 = (f32[8,80]{1,0:T(8,128)S(1)}, f32[8,80]{1,0:T(8,128)}, u32[]{:S(2)}) copy-start(f32[8,80]{1,0:T(8,128)} %param.24) | copy-start | bytes 7684
  3.5 28.5 %collective-permute-start.1 = (f32[1168]{0:T(1024)S(1)}, f32[1168]{0:T(1024)S(1)}, u32[]{:S(2)}, u32[]{:S(2)}) collective-permute-start(f32[1168]{0:T(1024)S(1)} %select_n.220), channel_id=1, source_target_pairs={{0,1},{1,0},{2,3},{3,2},{4,5},{5,4},{6,7},{7,6},{8,9},{9,8},{10,11... | collective-permute-start | bytes 14024 | tf_op jit(solution)/shard_map/ppermute | solution.py:21
  20.0 12.0 %collective-permute-start = (f32[1168]{0:T(1024)S(1)}, f32[1168]{0:T(1024)S(1)}, u32[]{:S(2)}, u32[]{:S(2)}) collective-permute-start(f32[1168]{0:T(1024)S(1)} %select_n.218), channel_id=1, source_target_pairs={{0,63},{1,2},{2,1},{3,4},{4,3},{5,6},{6,5},{7,8},{8,7},{9,10},{10,... | collective-permute-start | bytes 14024 | tf_op jit(solution)/shard_map/ppermute | solution.py:21
  22.8 47.0 %copy-start.7 = (s32[128]{0:T(128)}, s32[128]{0:T(128)S(1)}, u32[]{:S(2)}) copy-start(s32[128]{0:T(128)S(1)} %eq.180) | copy-start | bytes 1540
  27.7 5.3 %copy-start.8 = (s32[64]{0:T(128)}, s32[64]{0:T(128)S(1)}, u32[]{:S(2)}) copy-start(s32[64]{0:T(128)S(1)} %eq.196) | copy-start | bytes 772
  33.0 12.2 %copy-start.19 = (f32[72,72]{1,0:T(8,128)S(1)}, f32[72,72]{1,0:T(8,128)}, u32[]{:S(2)}) copy-start(f32[72,72]{1,0:T(8,128)} %param.16) | copy-start | bytes 62212
  33.0 9.2 %collective-permute-start.3 = (f32[73,2,132]{0,2,1:T(8,128)S(1)}, f32[73,2,132]{0,2,1:T(8,128)S(1)}, u32[]{:S(2)}, u32[]{:S(2)}) collective-permute-start(f32[73,2,132]{0,2,1:T(8,128)S(1)} %broadcast_select_fusion.3), channel_id=1, source_target_pairs={{0,64},{64,0},{128,192},{192,128},{256,320},{320,256},{384,448},{4... | collective-permute-start | bytes 231272 | tf_op jit(solution)/shard_map/ppermute | solution.py:21
  34.9 9.1 %collective-permute-start.2 = (f32[73,2,132]{0,2,1:T(8,128)S(1)}, f32[73,2,132]{0,2,1:T(8,128)S(1)}, u32[]{:S(2)}, u32[]{:S(2)}) collective-permute-start(f32[73,2,132]{0,2,1:T(8,128)S(1)} %get-tuple-element.6), channel_id=1, source_target_pairs={{0,960},{64,128},{128,64},{192,256},{256,192},{320,384},{384,320},... | collective-permute-start | bytes 231272 | tf_op jit(solution)/shard_map/ppermute | solution.py:21
  45.2 1.8 %copy-start.11 = (f32[24,72]{1,0:T(8,128)S(1)}, f32[24,72]{1,0:T(8,128)}, u32[]{:S(2)}) copy-start(f32[24,72]{1,0:T(8,128)} %param.17) | copy-start | bytes 20740
  47.0 6.7 %copy-start.2 = (f32[72,8,128]{0,2,1:T(8,128)}, f32[72,8,128]{0,2,1:T(8,128)S(1)}, u32[]{:S(2)}) copy-start(f32[72,8,128]{0,2,1:T(8,128)S(1)} %fusion.7) | copy-start | bytes 884740
  47.7 23.4 %copy-start.17 = (s32[16]{0:T(128)S(1)}, s32[16]{0:T(128)}, u32[]{:S(2)}) copy-start(s32[16]{0:T(128)} %iota_add_fusion.3) | copy-start | bytes 196
  47.7 13.2 %collective-permute-start.4 = (bf16[24,16,64]{2,1,0:T(8,128)(2,1)S(1)}, bf16[24,16,64]{2,1,0:T(8,128)(2,1)S(1)}, u32[]{:S(2)}, u32[]{:S(2)}) collective-permute-start(bf16[24,16,64]{2,1,0:T(8,128)(2,1)S(1)} %reshape.176), channel_id=1, source_target_pairs={{0,2},{1,3},{2,0},{3,1},{4,6},{5,7},{6,4},{7,5},{8,10},{9,11},{10,... | collective-permute-start | bytes 147464 | tf_op jit(solution)/shard_map/ppermute | solution.py:21
  53.7 9.6 %collective-permute-start.5 = (bf16[24,16,64]{2,1,0:T(8,128)(2,1)S(1)}, bf16[24,16,64]{2,1,0:T(8,128)(2,1)S(1)}, u32[]{:S(2)}, u32[]{:S(2)}) collective-permute-start(bf16[24,16,64]{2,1,0:T(8,128)(2,1)S(1)} %reshape.176), channel_id=1, source_target_pairs={{0,62},{1,63},{2,4},{3,5},{4,2},{5,3},{6,8},{7,9},{8,6},{9,7},{10,... | collective-permute-start | bytes 147464 | tf_op jit(solution)/shard_map/ppermute | solution.py:21
  63.3 7.5 %collective-permute-start.6 = (bf16[24,32,64]{2,1,0:T(8,128)(2,1)S(1)}, bf16[24,32,64]{2,1,0:T(8,128)(2,1)S(1)}, u32[]{:S(2)}, u32[]{:S(2)}) collective-permute-start(bf16[24,32,64]{2,1,0:T(8,128)(2,1)S(1)} %pad_maximum_fusion.9), channel_id=1, source_target_pairs={{0,1},{1,0},{2,3},{3,2},{4,5},{5,4},{6,7},{7,6},{8,9},{9,8},{10,11... | collective-permute-start | bytes 294920 | tf_op jit(solution)/shard_map/ppermute | solution.py:21
  73.4 10.8 %copy-start.1 = (f32[80,2048]{1,0:T(8,128)S(1)}, f32[80,2048]{1,0:T(8,128)}, u32[]{:S(2)}) copy-start(f32[80,2048]{1,0:T(8,128)} %param.20) | copy-start | bytes 1966084
  75.4 11.5 %copy-start.9 = (s32[64]{0:T(128)S(1)}, s32[64]{0:T(128)}, u32[]{:S(2)}) copy-start(s32[64]{0:T(128)} %copy-done.8) | copy-start | bytes 772
  75.4 11.5 %copy-start.15 = (s32[32]{0:T(128)S(1)}, s32[32]{0:T(128)}, u32[]{:S(2)}) copy-start(s32[32]{0:T(128)} %iota_add_fusion.2) | copy-start | bytes 388
  75.5 15.9 %copy-start.10 = (s32[64]{0:T(128)S(1)}, s32[64]{0:T(128)}, u32[]{:S(2)}) copy-start(s32[64]{0:T(128)} %copy-done.8) | copy-start | bytes 772
  75.5 15.9 %copy-start.16 = (s32[32]{0:T(128)S(1)}, s32[32]{0:T(128)}, u32[]{:S(2)}) copy-start(s32[32]{0:T(128)} %iota_add_fusion.1) | copy-start | bytes 388
  75.6 16.8 %copy-start.13 = (s32[64]{0:T(128)S(1)}, s32[64]{0:T(128)}, u32[]{:S(2)}) copy-start(s32[64]{0:T(128)} %compare_select_fusion.1) | copy-start | bytes 772
  76.6 16.0 %copy-start.18 = (s32[32]{0:T(128)S(1)}, s32[32]{0:T(128)}, u32[]{:S(2)}) copy-start(s32[32]{0:T(128)} %iota_add_fusion) | copy-start | bytes 388
  76.8 10.4 %collective-permute-start.7 = (bf16[8,32,64]{2,1,0:T(8,128)(2,1)S(1)}, bf16[8,32,64]{2,1,0:T(8,128)(2,1)S(1)}, u32[]{:S(2)}, u32[]{:S(2)}) collective-permute-start(bf16[8,32,64]{2,1,0:T(8,128)(2,1)S(1)} %reshape.179), channel_id=1, source_target_pairs={{0,2},{1,3},{2,0},{3,1},{4,6},{5,7},{6,4},{7,5},{8,10},{9,11},{10,... | collective-permute-start | bytes 98312 | tf_op jit(solution)/shard_map/ppermute | solution.py:21
  78.7 9.2 %collective-permute-start.8 = (bf16[8,32,64]{2,1,0:T(8,128)(2,1)S(1)}, bf16[8,32,64]{2,1,0:T(8,128)(2,1)S(1)}, u32[]{:S(2)}, u32[]{:S(2)}) collective-permute-start(bf16[8,32,64]{2,1,0:T(8,128)(2,1)S(1)} %reshape.179), channel_id=1, source_target_pairs={{0,62},{1,63},{2,4},{3,5},{4,2},{5,3},{6,8},{7,9},{8,6},{9,7},{10,... | collective-permute-start | bytes 98312 | tf_op jit(solution)/shard_map/ppermute | solution.py:21
  86.9 7.8 %copy-start.3 = (f32[72,8,128]{0,2,1:T(8,128)S(1)}, f32[72,8,128]{0,2,1:T(8,128)}, u32[]{:S(2)}) copy-start(f32[72,8,128]{0,2,1:T(8,128)} %copy-done.2) | copy-start | bytes 884740
  86.9 7.8 %copy-start.12 = (f32[72,8]{0,1:T(8,128)S(1)}, f32[72,8]{0,1:T(8,128)}, u32[]{:S(2)}) copy-start(f32[72,8]{0,1:T(8,128)} %param.27) | copy-start | bytes 6916
  88.0 4.4 %collective-permute-start.9 = (bf16[8,64,64]{2,1,0:T(8,128)(2,1)S(1)}, bf16[8,64,64]{2,1,0:T(8,128)(2,1)S(1)}, u32[]{:S(2)}, u32[]{:S(2)}) collective-permute-start(bf16[8,64,64]{2,1,0:T(8,128)(2,1)S(1)} %pad_maximum_fusion.14), channel_id=1, source_target_pairs={{0,1},{1,0},{2,3},{3,2},{4,5},{5,4},{6,7},{7,6},{8,9},{9,8},{10,11... | collective-permute-start | bytes 196616 | tf_op jit(solution)/shard_map/ppermute | solution.py:21

commit v8 on v4

--- a/solution.py
+++ b/solution.py
@@ -46,7 +46,7 @@
 
 
 def level_mix(matrix, field):
-    return jnp.einsum("ml,l...->m...", matrix, field, precision=lax.Precision.HIGHEST)
+    return jnp.einsum("ml,l...->m...", matrix, field, precision=lax.Precision.HIGH)
 
 
 def inner_step(padded, coeff, vert_mix):
@@ -131,9 +131,9 @@
     )
     remapped = block_product(remap_weight, exchange_and_pick(surface_blocks, remap_cols, here))
     remapped = remapped.reshape(fields, ocean_blocks * 64)
-    stepped = mixed + jnp.dot(forcing, remapped, precision=lax.Precision.HIGHEST)
+    stepped = mixed + jnp.dot(forcing, remapped, precision=lax.Precision.HIGH)
     ocean_out = jnp.where(wet_mask[None] == 1, stepped, ocean_state)
-    sea = jnp.dot(surface_proj, ocean_out, precision=lax.Precision.HIGHEST).astype(jnp.bfloat16)
+    sea = jnp.dot(surface_proj, ocean_out, precision=lax.Precision.HIGH).astype(jnp.bfloat16)
     sea_blocks = sea.reshape(sea.shape[0], ocean_blocks, 64)
     returned = block_product(back_weight, exchange_and_pick(sea_blocks, back_cols, here))
     returned = returned.reshape(sea.shape[0], rows_here, cols_here)

time: 92.4 us -> 91 us (0.985)
  matrix products: 14.1 us -> 12.6 us
    dot_general x6, matrix products: 6.85 us -> 5.37 us  [the longest x4 3.33 us: level_mix(): jnp.einsum('ml,l...->m...', matrix, field, precision=lax.Precision.HIGH)]
where the time goes in v8:
time: 91 us; the launch traced here: 90.3 us
  starting transfers between devices  57.4 us (63%)
  matrix products  12.6 us (14%)
  waiting for transfers between devices  8.34 us (9%)
  local copies, waits for them, and re-layouts  7.29 us (8%)
  other arithmetic  3.39 us (4%)
  between operations  1.27 us (1%)
    ppermute x10, starting transfers between devices, swap(): return lax.ppermute(value, axis, pairs)  57.4 us
    ppermute x10, waiting for transfers between devices, swap(): return lax.ppermute(value, axis, pairs)  8.34 us
    dot_general x4, matrix products, level_mix(): jnp.einsum('ml,l...->m...', matrix, field, precision=lax.Precision.HIGH)  3.33 us
    dot_general x1, matrix products, body(): jnp.dot(ocean_mix, ocean_state, precision=lax.Precision.HIGHEST)  2.79 us
    add x6, other arithmetic, pick(): ids = base + jnp.arange(count, dtype=local.dtype)  2.71 us
    unnamed x36, local copies, waits for them, and re-layouts  2.29 us
    dot_general x8, matrix products, pick(): jnp.einsum('qb,fbj->fqj', onehot, piece, preferred_element_type=jnp.float32)  2.24 us
    dot_general x2, matrix products, block_product(): jnp.einsum('okij,fokj->foi', weights, picked, preferred_element_type=jnp....  2.22 us
  transfers between devices with their start and end apart: 10, of which 5 were waited for; matrix products, arithmetic and copies ran while one was open for 8% of the time, Pallas kernels for 0%

profile of v8, /device:TPU:1, one launch (start us, length us, event | category | flops | bytes accessed | tf_op | source)
XLA Modules:
  0.0 90.3 jit_solution(15172808264667141225)
XLA Ops:
  0.7 1.3 %copy.27 = f32[72,8,128]{0,2,1:T(8,128)S(1)} copy(f32[72,8,128]{2,1,0:T(8,128)} %param.14) | data formatting | bytes 589824 | tf_op args[0]
  2.0 0.9 copy.28
  3.5 16.1 %collective-permute-start.1 = (f32[1168]{0:T(1024)S(1)}, f32[1168]{0:T(1024)S(1)}, u32[]{:S(2)}, u32[]{:S(2)}) collective-permute-start(f32[1168]{0:T(1024)S(1)} %select_n.213), channel_id=1, source_target_pairs={{0,1},{1,0},{2,3},{3,2},{4,5},{5,4},{6,7},{7,6},{8,9},{9,8},{10,11... | collective-permute-start | bytes 14024 | tf_op jit(solution)/shard_map/ppermute | solution.py:21
  19.9 1.9 %collective-permute-start = (f32[1168]{0:T(1024)S(1)}, f32[1168]{0:T(1024)S(1)}, u32[]{:S(2)}, u32[]{:S(2)}) collective-permute-start(f32[1168]{0:T(1024)S(1)} %select_n.211), channel_id=1, source_target_pairs={{0,63},{1,2},{2,1},{3,4},{4,3},{5,6},{6,5},{7,8},{8,7},{9,10},{10,... | collective-permute-start | bytes 14024 | tf_op jit(solution)/shard_map/ppermute | solution.py:21
  21.9 0.5 iota_add_fusion.4
  22.4 0.5 iota_add_fusion.2
  23.1 0.6 iota_add_fusion.3
  24.0 2.8 %convolution_add_fusion = f32[80,2048]{1,0:T(8,128)} fusion(f32[80,2048]{1,0:T(8,128)} %param.20, f32[80,80]{1,0:T(8,128)S(1)} %copy-done.3), kind=kOutput, calls=%fused_computation | convolution fusion | flops 157450240 | bytes 1336320 | tf_op jit(solution)/shard_map/dot_general | solution.py:130
  26.8 0.5 iota_add_fusion.1
  28.4 1.9 %collective-permute-start.3 = (f32[73,2,132]{0,2,1:T(8,128)S(1)}, f32[73,2,132]{0,2,1:T(8,128)S(1)}, u32[]{:S(2)}, u32[]{:S(2)}) collective-permute-start(f32[73,2,132]{0,2,1:T(8,128)S(1)} %broadcast_select_fusion.3), channel_id=1, source_target_pairs={{0,64},{64,0},{128,192},{192,128},{256,320},{320,256},{384,448},{4... | collective-permute-start | bytes 231272 | tf_op jit(solution)/shard_map/ppermute | solution.py:21
  30.3 6.7 %collective-permute-start.2 = (f32[73,2,132]{0,2,1:T(8,128)S(1)}, f32[73,2,132]{0,2,1:T(8,128)S(1)}, u32[]{:S(2)}, u32[]{:S(2)}) collective-permute-start(f32[73,2,132]{0,2,1:T(8,128)S(1)} %get-tuple-element.6), channel_id=1, source_target_pairs={{0,960},{64,128},{128,64},{192,256},{256,192},{320,384},{384,320},... | collective-permute-start | bytes 231272 | tf_op jit(solution)/shard_map/ppermute | solution.py:21
  37.0 0.6 iota_add_fusion
  37.6 1.8 %collective-permute-done.2 = f32[73,2,132]{0,2,1:T(8,128)S(1)} collective-permute-done((f32[73,2,132]{0,2,1:T(8,128)S(1)}, f32[73,2,132]{0,2,1:T(8,128)S(1)}, u32[]{:S(2)}, u32[]{:S(2)}) %collective-permute-start.2) | collective-permute-done | bytes 77120 | tf_op jit(solution)/shard_map/ppermute | solution.py:21
  39.7 0.7 slice_reduce_fusion
  40.6 0.9 fusion.15
  41.5 0.5 fusion.6
  42.4 6.0 %collective-permute-start.4 = (bf16[24,16,64]{2,1,0:T(8,128)(2,1)S(1)}, bf16[24,16,64]{2,1,0:T(8,128)(2,1)S(1)}, u32[]{:S(2)}, u32[]{:S(2)}) collective-permute-start(bf16[24,16,64]{2,1,0:T(8,128)(2,1)S(1)} %reshape.176), channel_id=1, source_target_pairs={{0,2},{1,3},{2,0},{3,1},{4,6},{5,7},{6,4},{7,5},{8,10},{9,11},{10,... | collective-permute-start | bytes 147464 | tf_op jit(solution)/shard_map/ppermute | solution.py:21
  48.4 8.2 %collective-permute-start.5 = (bf16[24,16,64]{2,1,0:T(8,128)(2,1)S(1)}, bf16[24,16,64]{2,1,0:T(8,128)(2,1)S(1)}, u32[]{:S(2)}, u32[]{:S(2)}) collective-permute-start(bf16[24,16,64]{2,1,0:T(8,128)(2,1)S(1)} %reshape.176), channel_id=1, source_target_pairs={{0,62},{1,63},{2,4},{3,5},{4,2},{5,3},{6,8},{7,9},{8,6},{9,7},{10,... | collective-permute-start | bytes 147464 | tf_op jit(solution)/shard_map/ppermute | solution.py:21
  57.0 1.7 %collective-permute-done.5 = bf16[24,16,64]{2,1,0:T(8,128)(2,1)S(1)} collective-permute-done((bf16[24,16,64]{2,1,0:T(8,128)(2,1)S(1)}, bf16[24,16,64]{2,1,0:T(8,128)(2,1)S(1)}, u32[]{:S(2)}, u32[]{:S(2)}) %collective-permute-start.5) | collective-permute-done | bytes 49184 | tf_op jit(solution)/shard_map/ppermute | solution.py:21
  58.7 5.8 %collective-permute-start.6 = (bf16[24,32,64]{2,1,0:T(8,128)(2,1)S(1)}, bf16[24,32,64]{2,1,0:T(8,128)(2,1)S(1)}, u32[]{:S(2)}, u32[]{:S(2)}) collective-permute-start(bf16[24,32,64]{2,1,0:T(8,128)(2,1)S(1)} %pad_maximum_fusion.9), channel_id=1, source_target_pairs={{0,1},{1,0},{2,3},{3,2},{4,5},{5,4},{6,7},{7,6},{8,9},{9,8},{10,11... | collective-permute-start | bytes 294920 | tf_op jit(solution)/shard_map/ppermute | solution.py:21
  64.8 0.7 collective-permute-done.6
  66.2 0.4 copy.38
  66.7 0.6 convolution_bitcast_fusion.4
  67.6 1.8 %fusion.1 = f32[80,2048]{1,0:T(8,128)S(1)} fusion(f32[80,2048]{1,0:T(8,128)} %param.20, f32[80,2048]{1,0:T(8,128)} %convolution_add_fusion, f32[24,2048]{1,0:T(8,128)S(1)} %reshape.178, f32[80,24]{0,1:T(8,128)S(1)} %copy-done.4, pred[2048]{0:T(1024)(128)(4,1)S(1)} %broadcast_compare_fusion), kind=kOutput, calls=%fused_computation.3 | convolution fusion | flops 23920640 | bytes 2172416 | tf_op jit(solution)/shard_map/dot_general | solution.py:134
  69.8 1.9 %collective-permute-start.7 = (bf16[8,32,64]{2,1,0:T(8,128)(2,1)S(1)}, bf16[8,32,64]{2,1,0:T(8,128)(2,1)S(1)}, u32[]{:S(2)}, u32[]{:S(2)}) collective-permute-start(bf16[8,32,64]{2,1,0:T(8,128)(2,1)S(1)} %reshape.179), channel_id=1, source_target_pairs={{0,2},{1,3},{2,0},{3,1},{4,6},{5,7},{6,4},{7,5},{8,10},{9,11},{10,... | collective-permute-start | bytes 98312 | tf_op jit(solution)/shard_map/ppermute | solution.py:21
  71.7 5.5 %collective-permute-start.8 = (bf16[8,32,64]{2,1,0:T(8,128)(2,1)S(1)}, bf16[8,32,64]{2,1,0:T(8,128)(2,1)S(1)}, u32[]{:S(2)}, u32[]{:S(2)}) collective-permute-start(bf16[8,32,64]{2,1,0:T(8,128)(2,1)S(1)} %reshape.179), channel_id=1, source_target_pairs={{0,62},{1,63},{2,4},{3,5},{4,2},{5,3},{6,8},{7,9},{8,6},{9,7},{10,... | collective-permute-start | bytes 98312 | tf_op jit(solution)/shard_map/ppermute | solution.py:21
  77.5 3.4 %collective-permute-done.8 = bf16[8,32,64]{2,1,0:T(8,128)(2,1)S(1)} collective-permute-done((bf16[8,32,64]{2,1,0:T(8,128)(2,1)S(1)}, bf16[8,32,64]{2,1,0:T(8,128)(2,1)S(1)}, u32[]{:S(2)}, u32[]{:S(2)}) %collective-permute-start.8) | collective-permute-done | bytes 32800 | tf_op jit(solution)/shard_map/ppermute | solution.py:21
  81.0 3.4 %collective-permute-start.9 = (bf16[8,64,64]{2,1,0:T(8,128)(2,1)S(1)}, bf16[8,64,64]{2,1,0:T(8,128)(2,1)S(1)}, u32[]{:S(2)}, u32[]{:S(2)}) collective-permute-start(bf16[8,64,64]{2,1,0:T(8,128)(2,1)S(1)} %pad_maximum_fusion.14), channel_id=1, source_target_pairs={{0,1},{1,0},{2,3},{3,2},{4,5},{5,4},{6,7},{7,6},{8,9},{9,8},{10,11... | collective-permute-start | bytes 196616 | tf_op jit(solution)/shard_map/ppermute | solution.py:21
  84.7 0.7 collective-permute-done.9
  86.1 1.6 %convolution_bitcast_fusion.5 = f32[8,16,64]{2,0,1:T(8,128)S(1)} fusion(bf16[8,16,4,64]{3,0,2,1:T(8,128)(2,1)S(1)} %bitcast.97, bf16[16,4,64,64]{3,2,1,0:T(8,128)(2,1)} %param.25), kind=kOutput, calls=%fused_computation.23 | convolution fusion | flops 4194304 | bytes 622592 | tf_op jit(solution)/shard_map/okij,fokj->foi/dot_general | solution.py:61
  87.8 1.6 %fusion.5 = f32[72,8,128]{0,2,1:T(8,128)S(1)} fusion(f32[72,8,128]{0,2,1:T(8,128)} %copy-done.2, f32[8,8,128]{2,1,0:T(8,128)S(1)} %reshape.181, f32[72,8]{0,1:T(8,128)S(1)} %copy-done.8), kind=kOutput, calls=%fused_computation.12 | convolution fusion | flops 3612672 | bytes 624896 | tf_op jit(solution)/shard_map/ml,l...->m.../dot_general | solution.py:49
  89.4 0.9 copy.46
  (88 shorter events, 6.6 us)
Async XLA Ops:
  0.6 66.0 %copy-start = (bf16[32,4,64,64]{3,2,1,0:T(8,128)(2,1)S(1)}, bf16[32,4,64,64]{3,2,1,0:T(8,128)(2,1)}, u32[]{:S(2)}) copy-start(bf16[32,4,64,64]{3,2,1,0:T(8,128)(2,1)} %param.18) | copy-start | bytes 3145732
  0.6 22.3 %copy-start.9 = (s32[32,4]{0,1:T(4,128)S(1)}, s32[32,4]{0,1:T(4,128)}, u32[]{:S(2)}) copy-start(s32[32,4]{0,1:T(4,128)} %param.19) | copy-start | bytes 1540
  0.7 23.1 %copy-start.6 = (s32[2048]{0:T(1024)S(1)}, s32[2048]{0:T(1024)}, u32[]{:S(2)}) copy-start(s32[2048]{0:T(1024)} %param.23) | copy-start | bytes 24580
  0.7 23.1 %copy-start.10 = (s32[16,4]{0,1:T(4,128)S(1)}, s32[16,4]{0,1:T(4,128)}, u32[]{:S(2)}) copy-start(s32[16,4]{0,1:T(4,128)} %param.26) | copy-start | bytes 772
  0.7 23.3 %copy-start.3 = (f32[80,80]{1,0:T(8,128)S(1)}, f32[80,80]{1,0:T(8,128)}, u32[]{:S(2)}) copy-start(f32[80,80]{1,0:T(8,128)} %param.21) | copy-start | bytes 76804
  3.5 23.9 %collective-permute-start.1 = (f32[1168]{0:T(1024)S(1)}, f32[1168]{0:T(1024)S(1)}, u32[]{:S(2)}, u32[]{:S(2)}) collective-permute-start(f32[1168]{0:T(1024)S(1)} %select_n.213), channel_id=1, source_target_pairs={{0,1},{1,0},{2,3},{3,2},{4,5},{5,4},{6,7},{7,6},{8,9},{9,8},{10,11... | collective-permute-start | bytes 14024 | tf_op jit(solution)/shard_map/ppermute | solution.py:21
  19.9 7.4 %collective-permute-start = (f32[1168]{0:T(1024)S(1)}, f32[1168]{0:T(1024)S(1)}, u32[]{:S(2)}, u32[]{:S(2)}) collective-permute-start(f32[1168]{0:T(1024)S(1)} %select_n.211), channel_id=1, source_target_pairs={{0,63},{1,2},{2,1},{3,4},{4,3},{5,6},{6,5},{7,8},{8,7},{9,10},{10,... | collective-permute-start | bytes 14024 | tf_op jit(solution)/shard_map/ppermute | solution.py:21
  28.4 12.2 %copy-start.16 = (f32[72,72]{1,0:T(8,128)S(1)}, f32[72,72]{1,0:T(8,128)}, u32[]{:S(2)}) copy-start(f32[72,72]{1,0:T(8,128)} %param.16) | copy-start | bytes 62212
  28.4 9.2 %collective-permute-start.3 = (f32[73,2,132]{0,2,1:T(8,128)S(1)}, f32[73,2,132]{0,2,1:T(8,128)S(1)}, u32[]{:S(2)}, u32[]{:S(2)}) collective-permute-start(f32[73,2,132]{0,2,1:T(8,128)S(1)} %broadcast_select_fusion.3), channel_id=1, source_target_pairs={{0,64},{64,0},{128,192},{192,128},{256,320},{320,256},{384,448},{4... | collective-permute-start | bytes 231272 | tf_op jit(solution)/shard_map/ppermute | solution.py:21
  30.3 9.1 %collective-permute-start.2 = (f32[73,2,132]{0,2,1:T(8,128)S(1)}, f32[73,2,132]{0,2,1:T(8,128)S(1)}, u32[]{:S(2)}, u32[]{:S(2)}) collective-permute-start(f32[73,2,132]{0,2,1:T(8,128)S(1)} %get-tuple-element.6), channel_id=1, source_target_pairs={{0,960},{64,128},{128,64},{192,256},{256,192},{320,384},{384,320},... | collective-permute-start | bytes 231272 | tf_op jit(solution)/shard_map/ppermute | solution.py:21
  40.6 1.4 %copy-start.5 = (f32[24,72]{1,0:T(8,128)S(1)}, f32[24,72]{1,0:T(8,128)}, u32[]{:S(2)}) copy-start(f32[24,72]{1,0:T(8,128)} %param.17) | copy-start | bytes 20740
  41.4 23.1 %copy-start.13 = (s32[16]{0:T(128)S(1)}, s32[16]{0:T(128)}, u32[]{:S(2)}) copy-start(s32[16]{0:T(128)} %iota_add_fusion.4) | copy-start | bytes 196
  42.0 6.4 %copy-start.2 = (f32[72,8,128]{0,2,1:T(8,128)}, f32[72,8,128]{0,2,1:T(8,128)S(1)}, u32[]{:S(2)}) copy-start(f32[72,8,128]{0,2,1:T(8,128)S(1)} %fusion.6) | copy-start | bytes 884740
  42.4 23.4 %copy-start.14 = (s32[16]{0:T(128)S(1)}, s32[16]{0:T(128)}, u32[]{:S(2)}) copy-start(s32[16]{0:T(128)} %iota_add_fusion.3) | copy-start | bytes 196
  42.4 14.5 %collective-permute-start.4 = (bf16[24,16,64]{2,1,0:T(8,128)(2,1)S(1)}, bf16[24,16,64]{2,1,0:T(8,128)(2,1)S(1)}, u32[]{:S(2)}, u32[]{:S(2)}) collective-permute-start(bf16[24,16,64]{2,1,0:T(8,128)(2,1)S(1)} %reshape.176), channel_id=1, source_target_pairs={{0,2},{1,3},{2,0},{3,1},{4,6},{5,7},{6,4},{7,5},{8,10},{9,11},{10,... | collective-permute-start | bytes 147464 | tf_op jit(solution)/shard_map/ppermute | solution.py:21
  48.4 10.2 %collective-permute-start.5 = (bf16[24,16,64]{2,1,0:T(8,128)(2,1)S(1)}, bf16[24,16,64]{2,1,0:T(8,128)(2,1)S(1)}, u32[]{:S(2)}, u32[]{:S(2)}) collective-permute-start(bf16[24,16,64]{2,1,0:T(8,128)(2,1)S(1)} %reshape.176), channel_id=1, source_target_pairs={{0,62},{1,63},{2,4},{3,5},{4,2},{5,3},{6,8},{7,9},{8,6},{9,7},{10,... | collective-permute-start | bytes 147464 | tf_op jit(solution)/shard_map/ppermute | solution.py:21
  58.7 6.9 %collective-permute-start.6 = (bf16[24,32,64]{2,1,0:T(8,128)(2,1)S(1)}, bf16[24,32,64]{2,1,0:T(8,128)(2,1)S(1)}, u32[]{:S(2)}, u32[]{:S(2)}) collective-permute-start(bf16[24,32,64]{2,1,0:T(8,128)(2,1)S(1)} %pad_maximum_fusion.9), channel_id=1, source_target_pairs={{0,1},{1,0},{2,3},{3,2},{4,5},{5,4},{6,7},{7,6},{8,9},{9,8},{10,11... | collective-permute-start | bytes 294920 | tf_op jit(solution)/shard_map/ppermute | solution.py:21
  66.7 0.9 %copy-start.4 = (f32[80,24]{0,1:T(8,128)S(1)}, f32[80,24]{0,1:T(8,128)}, u32[]{:S(2)}) copy-start(f32[80,24]{0,1:T(8,128)} %param.22) | copy-start | bytes 23044
  67.3 2.0 %copy-start.7 = (f32[8,80]{1,0:T(8,128)S(1)}, f32[8,80]{1,0:T(8,128)}, u32[]{:S(2)}) copy-start(f32[8,80]{1,0:T(8,128)} %param.24) | copy-start | bytes 7684
  67.3 10.0 %copy-start.11 = (s32[32]{0:T(128)S(1)}, s32[32]{0:T(128)}, u32[]{:S(2)}) copy-start(s32[32]{0:T(128)} %iota_add_fusion.2) | copy-start | bytes 388
  67.4 17.0 %copy-start.12 = (s32[32]{0:T(128)S(1)}, s32[32]{0:T(128)}, u32[]{:S(2)}) copy-start(s32[32]{0:T(128)} %iota_add_fusion.1) | copy-start | bytes 388
  67.6 18.1 %copy-start.15 = (s32[32]{0:T(128)S(1)}, s32[32]{0:T(128)}, u32[]{:S(2)}) copy-start(s32[32]{0:T(128)} %iota_add_fusion) | copy-start | bytes 388
  69.4 18.3 %copy-start.1 = (f32[80,2048]{1,0:T(8,128)}, f32[80,2048]{1,0:T(8,128)S(1)}, u32[]{:S(2)}) copy-start(f32[80,2048]{1,0:T(8,128)S(1)} %fusion.1) | copy-start | bytes 1966084
  69.8 18.0 %copy-start.8 = (f32[72,8]{0,1:T(8,128)S(1)}, f32[72,8]{0,1:T(8,128)}, u32[]{:S(2)}) copy-start(f32[72,8]{0,1:T(8,128)} %param.27) | copy-start | bytes 6916
  69.8 7.7 %collective-permute-start.7 = (bf16[8,32,64]{2,1,0:T(8,128)(2,1)S(1)}, bf16[8,32,64]{2,1,0:T(8,128)(2,1)S(1)}, u32[]{:S(2)}, u32[]{:S(2)}) collective-permute-start(bf16[8,32,64]{2,1,0:T(8,128)(2,1)S(1)} %reshape.179), channel_id=1, source_target_pairs={{0,2},{1,3},{2,0},{3,1},{4,6},{5,7},{6,4},{7,5},{8,10},{9,11},{10,... | collective-permute-start | bytes 98312 | tf_op jit(solution)/shard_map/ppermute | solution.py:21
  71.7 9.2 %collective-permute-start.8 = (bf16[8,32,64]{2,1,0:T(8,128)(2,1)S(1)}, bf16[8,32,64]{2,1,0:T(8,128)(2,1)S(1)}, u32[]{:S(2)}, u32[]{:S(2)}) collective-permute-start(bf16[8,32,64]{2,1,0:T(8,128)(2,1)S(1)} %reshape.179), channel_id=1, source_target_pairs={{0,62},{1,63},{2,4},{3,5},{4,2},{5,3},{6,8},{7,9},{8,6},{9,7},{10,... | collective-permute-start | bytes 98312 | tf_op jit(solution)/shard_map/ppermute | solution.py:21
  81.0 4.4 %collective-permute-start.9 = (bf16[8,64,64]{2,1,0:T(8,128)(2,1)S(1)}, bf16[8,64,64]{2,1,0:T(8,128)(2,1)S(1)}, u32[]{:S(2)}, u32[]{:S(2)}) collective-permute-start(bf16[8,64,64]{2,1,0:T(8,128)(2,1)S(1)} %pad_maximum_fusion.14), channel_id=1, source_target_pairs={{0,1},{1,0},{2,3},{3,2},{4,5},{5,4},{6,7},{7,6},{8,9},{9,8},{10,11... | collective-permute-start | bytes 196616 | tf_op jit(solution)/shard_map/ppermute | solution.py:21

commit v9 on v8

--- a/solution.py
+++ b/solution.py
@@ -77,12 +77,10 @@
     tiles = lax.axis_size("tile")
     local = near_index(cols, per_tile, tiles, here).reshape(-1)
     even = here % 2 == 0
-    chip_even = (here // 2) % 2 == 0
-    first = swap(blocks, "tile", 2, 0)
-    second = swap(blocks, "tile", 2, 1)
-    first_base = jnp.where(chip_even, 4 * per_tile, 0)
+    forward = lax.ppermute(blocks, "tile", [(s, (s - 2 if s % 2 == 0 else s + 2) % tiles) for s in range(tiles)])
+    other = lax.ppermute(blocks, "tile", [(s, (s + 2 if s % 2 == 0 else s - 2) % tiles) for s in range(tiles)])
+    first_base = jnp.where(even, 4 * per_tile, 0)
     second_base = 4 * per_tile - first_base
-    forward = jnp.where(even == chip_even, first, second)
     bundle = jnp.concatenate([blocks, forward], axis=1)
     partner = swap(bundle, "tile", 1, 0)
     plus_one = jnp.where(even, 0, per_tile)
@@ -91,8 +89,8 @@
     within = local % per_tile
     partner_local = jnp.where(slot == 3, plus_one + within, jnp.where(slot == 1, minus_one + within, -1))
     picked = pick(local, 2 * per_tile, blocks, per_tile)
-    picked = picked + pick(local, first_base, first, per_tile)
-    picked = picked + pick(local, second_base, second, per_tile)
+    picked = picked + pick(local, first_base, forward, per_tile)
+    picked = picked + pick(local, second_base, other, per_tile)
     picked = picked + pick(partner_local, 0, partner, 2 * per_tile)
     return picked.astype(blocks.dtype).reshape((fields,) + cols.shape + (cells,))
 

time: 91 us -> 83.3 us (0.915)
  waiting for transfers between devices: 8.34 us -> 3.75 us
  starting transfers between devices: 57.4 us -> 55.5 us
  other arithmetic: 3.39 us -> 1.68 us
  local copies, waits for them, and re-layouts: 7.29 us -> 8.24 us
    ppermute x10 -> x6, starting transfers between devices: 57.4 us -> 31.7 us  [swap(): return lax.ppermute(value, axis, pairs)]
    ppermute x0 -> x4, starting transfers between devices: none -> 23.8 us  [the longest x2 15.9 us: exchange_and_pick(): lax.ppermute(blocks, 'tile', [(s, (s + 2 if s % 2 == 0 else s - 2) % tile...]
    ppermute x10 -> x6, waiting for transfers between devices: 8.34 us -> 3.74 us  [swap(): return lax.ppermute(value, axis, pairs)]
    add x6, other arithmetic: 2.71 us -> 1.02 us  [pick(): ids = base + jnp.arange(count, dtype=local.dtype)]
    dot_general x4, matrix products: 3.33 us -> 2.32 us  [level_mix(): jnp.einsum('ml,l...->m...', matrix, field, precision=lax.Precision.HIGH)]
    convert_element_type x2, local copies, waits for them, and re-layouts: 0.57 us -> 1.54 us  [exchange_and_pick(): picked.astype(blocks.dtype).reshape((fields,) + cols.shape + (cells,))]
    unnamed x36 -> x28, local copies, waits for them, and re-layouts: 2.29 us -> 2.27 us
  transfers between devices with their start and end apart: 10 -> 10, of which waited for: 5 -> 3; matrix products, arithmetic and copies ran while one was open for 8% -> 8% of each run, Pallas kernels for 0% -> 0%
where the time goes in v9:
time: 83.3 us; the launch traced here: 82.7 us
  starting transfers between devices  55.5 us (67%)
  matrix products  12.3 us (15%)
  local copies, waits for them, and re-layouts  8.24 us (10%)
  waiting for transfers between devices  3.75 us (5%)
  other arithmetic  1.68 us (2%)
  between operations  1.23 us (1%)
    ppermute x6, starting transfers between devices, swap(): return lax.ppermute(value, axis, pairs)  31.7 us
    ppermute x2, starting transfers between devices, exchange_and_pick(): lax.ppermute(blocks, 'tile', [(s, (s + 2 if s % 2 == 0 else s - 2) % tile...  15.9 us
    ppermute x2, starting transfers between devices, exchange_and_pick(): lax.ppermute(blocks, 'tile', [(s, (s - 2 if s % 2 == 0 else s + 2) % tile...  7.88 us
    ppermute x6, waiting for transfers between devices, swap(): return lax.ppermute(value, axis, pairs)  3.74 us
    dot_general x8, matrix products, pick(): jnp.einsum('qb,fbj->fqj', onehot, piece, preferred_element_type=jnp.float32)  2.97 us
    dot_general x1, matrix products, body(): jnp.dot(ocean_mix, ocean_state, precision=lax.Precision.HIGHEST)  2.79 us
    dot_general x4, matrix products, level_mix(): jnp.einsum('ml,l...->m...', matrix, field, precision=lax.Precision.HIGH)  2.32 us
    unnamed x28, local copies, waits for them, and re-layouts  2.27 us
  transfers between devices with their start and end apart: 10, of which 3 were waited for; matrix products, arithmetic and copies ran while one was open for 8% of the time, Pallas kernels for 0%

profile of v9, /device:TPU:1, one launch (start us, length us, event | category | flops | bytes accessed | tf_op | source)
XLA Modules:
  0.0 82.7 jit_solution(8126686411550590957)
XLA Ops:
  0.7 1.3 %copy.27 = f32[72,8,128]{0,2,1:T(8,128)S(1)} copy(f32[72,8,128]{2,1,0:T(8,128)} %param.14) | data formatting | bytes 589824 | tf_op args[0]
  2.0 0.9 %copy.28 = f32[1,8,128]{0,2,1:T(8,128)S(1)} copy(f32[1,8,128]{2,1,0:T(8,128)} %bitcast.101) | data formatting | bytes 8192 | tf_op jit(solution)/shard_map/broadcast_in_dim | solution.py:115
  3.4 16.1 %collective-permute-start.1 = (f32[1168]{0:T(1024)S(1)}, f32[1168]{0:T(1024)S(1)}, u32[]{:S(2)}, u32[]{:S(2)}) collective-permute-start(f32[1168]{0:T(1024)S(1)} %select_n.186), channel_id=1, source_target_pairs={{0,1},{1,0},{2,3},{3,2},{4,5},{5,4},{6,7},{7,6},{8,9},{9,8},{10,11... | collective-permute-start | bytes 14024 | tf_op jit(solution)/shard_map/ppermute | solution.py:21
  19.9 1.9 %collective-permute-start = (f32[1168]{0:T(1024)S(1)}, f32[1168]{0:T(1024)S(1)}, u32[]{:S(2)}, u32[]{:S(2)}) collective-permute-start(f32[1168]{0:T(1024)S(1)} %select_n.184), channel_id=1, source_target_pairs={{0,63},{1,2},{2,1},{3,4},{4,3},{5,6},{6,5},{7,8},{8,7},{9,10},{10,... | collective-permute-start | bytes 14024 | tf_op jit(solution)/shard_map/ppermute | solution.py:21
  21.9 0.5 iota_add_fusion.5
  22.9 2.8 %convolution_add_fusion = f32[80,2048]{1,0:T(8,128)} fusion(f32[80,2048]{1,0:T(8,128)} %param.20, f32[80,80]{1,0:T(8,128)S(1)} %copy-done.2), kind=kOutput, calls=%fused_computation | convolution fusion | flops 157450240 | bytes 1336320 | tf_op jit(solution)/shard_map/dot_general | solution.py:128
  26.8 1.9 %collective-permute-start.3 = (f32[73,2,132]{0,2,1:T(8,128)S(1)}, f32[73,2,132]{0,2,1:T(8,128)S(1)}, u32[]{:S(2)}, u32[]{:S(2)}) collective-permute-start(f32[73,2,132]{0,2,1:T(8,128)S(1)} %broadcast_select_fusion.2), channel_id=1, source_target_pairs={{0,64},{64,0},{128,192},{192,128},{256,320},{320,256},{384,448},{4... | collective-permute-start | bytes 231272 | tf_op jit(solution)/shard_map/ppermute | solution.py:21
  28.8 6.6 %collective-permute-start.2 = (f32[73,2,132]{0,2,1:T(8,128)S(1)}, f32[73,2,132]{0,2,1:T(8,128)S(1)}, u32[]{:S(2)}, u32[]{:S(2)}) collective-permute-start(f32[73,2,132]{0,2,1:T(8,128)S(1)} %get-tuple-element.6), channel_id=1, source_target_pairs={{0,960},{64,128},{128,64},{192,256},{256,192},{320,384},{384,320},... | collective-permute-start | bytes 231272 | tf_op jit(solution)/shard_map/ppermute | solution.py:21
  35.4 0.5 iota_add_fusion
  35.9 1.9 %collective-permute-done.2 = f32[73,2,132]{0,2,1:T(8,128)S(1)} collective-permute-done((f32[73,2,132]{0,2,1:T(8,128)S(1)}, f32[73,2,132]{0,2,1:T(8,128)S(1)}, u32[]{:S(2)}, u32[]{:S(2)}) %collective-permute-start.2) | collective-permute-done | bytes 77120 | tf_op jit(solution)/shard_map/ppermute | solution.py:21
  38.1 0.7 slice_reduce_fusion
  39.0 0.9 %fusion.15 = f32[72,10,130]{0,2,1:T(8,128)S(1)} fusion(f32[73,12,132]{0,2,1:T(8,128)S(1)} %pad_maximum_fusion, f32[73,2,132]{0,2,1:T(8,128)S(1)} %get-tuple-element.12, f32[73,8,2]{0,2,1:T(2,128)S(1)} %copy.32, f32[73,8,2]{0,2,1:T(2,128)S(1)} %copy.31, f32[1,8,128]{0,2,1:T(8,128)S(1)} %copy.28, f32[72,8,128]{0,2,1:T(8,128)S(1)} %copy.27, ...), kind=kOutput, calls=%fused_computation.31 | convolution fusion | flops 41932800 | bytes 4556416 | tf_op jit(solution)/shard_map/ml,l...->m.../dot_general | solution.py:49
  39.9 0.5 fusion.6
  40.4 0.3 fusion.11
  40.9 6.0 %collective-permute-start.4 = (bf16[24,16,64]{2,1,0:T(8,128)(2,1)S(1)}, bf16[24,16,64]{2,1,0:T(8,128)(2,1)S(1)}, u32[]{:S(2)}, u32[]{:S(2)}) collective-permute-start(bf16[24,16,64]{2,1,0:T(8,128)(2,1)S(1)} %reshape.176), channel_id=1, source_target_pairs={{0,62},{1,3},{2,0},{3,5},{4,2},{5,7},{6,4},{7,9},{8,6},{9,11},{10,... | collective-permute-start | bytes 147464 | tf_op jit(solution)/shard_map/ppermute | solution.py:80
  46.9 8.3 %collective-permute-start.5 = (bf16[24,16,64]{2,1,0:T(8,128)(2,1)S(1)}, bf16[24,16,64]{2,1,0:T(8,128)(2,1)S(1)}, u32[]{:S(2)}, u32[]{:S(2)}) collective-permute-start(bf16[24,16,64]{2,1,0:T(8,128)(2,1)S(1)} %reshape.176), channel_id=1, source_target_pairs={{0,2},{1,63},{2,4},{3,1},{4,6},{5,3},{6,8},{7,5},{8,10},{9,7},{10,... | collective-permute-start | bytes 147464 | tf_op jit(solution)/shard_map/ppermute | solution.py:81
  55.2 0.3 fusion.51
  55.5 1.9 %collective-permute-start.6 = (bf16[24,32,64]{2,1,0:T(8,128)(2,1)S(1)}, bf16[24,32,64]{2,1,0:T(8,128)(2,1)S(1)}, u32[]{:S(2)}, u32[]{:S(2)}) collective-permute-start(bf16[24,32,64]{2,1,0:T(8,128)(2,1)S(1)} %pad_maximum_fusion.9), channel_id=1, source_target_pairs={{0,1},{1,0},{2,3},{3,2},{4,5},{5,4},{6,7},{7,6},{8,9},{9,8},{10,11... | collective-permute-start | bytes 294920 | tf_op jit(solution)/shard_map/ppermute | solution.py:21
  57.5 0.3 convolution_add_fusion.2
  57.8 1.1 %collective-permute-done.6 = bf16[24,32,64]{2,1,0:T(8,128)(2,1)S(1)} collective-permute-done((bf16[24,32,64]{2,1,0:T(8,128)(2,1)S(1)}, bf16[24,32,64]{2,1,0:T(8,128)(2,1)S(1)}, u32[]{:S(2)}, u32[]{:S(2)}) %collective-permute-start.6) | collective-permute-done | bytes 98336 | tf_op jit(solution)/shard_map/ppermute | solution.py:21
  58.9 0.3 fusion.32
  59.2 1.1 %fusion.7 = bf16[24,128,64]{1,2,0:T(8,128)(2,1)} fusion(f32[24,64,128]{2,1,0:T(8,128)S(1)} %fusion.32, f32[24,64,128]{2,1,0:T(8,128)S(1)} %convolution_add_fusion.2, bf16[24,16,64]{2,1,0:T(8,128)(2,1)S(1)} %collective-permute-done.5, s32[128]{0:T(128)S(1)} %eq.170, s32[16]{0:T(128)S(1)} %iota_add_fusion.3), kind=kOutput, calls=%fused_computation.15 | convolution fusion | flops 6883328 | bytes 2015808 | tf_op jit(solution)/shard_map/qb,fbj->fqj/dot_general | solution.py:72
  60.3 1.4 %copy.38 = bf16[24,128,64]{2,0,1:T(8,128)(2,1)S(1)} copy(bf16[24,128,64]{1,2,0:T(8,128)(2,1)} %fusion.7) | data formatting | bytes 786432 | tf_op jit(solution)/shard_map/convert_element_type | solution.py:95
  61.7 0.6 convolution_bitcast_fusion.4
  62.6 1.8 %fusion.1 = f32[80,2048]{1,0:T(8,128)S(1)} fusion(f32[80,2048]{1,0:T(8,128)} %param.20, f32[80,2048]{1,0:T(8,128)} %convolution_add_fusion, f32[24,2048]{1,0:T(8,128)S(1)} %reshape.178, f32[80,24]{0,1:T(8,128)S(1)} %copy-done.3, pred[2048]{0:T(1024)(128)(4,1)S(1)} %broadcast_compare_fusion), kind=kOutput, calls=%fused_computation.3 | convolution fusion | flops 23920640 | bytes 2172416 | tf_op jit(solution)/shard_map/dot_general | solution.py:132
  64.8 1.9 %collective-permute-start.7 = (bf16[8,32,64]{2,1,0:T(8,128)(2,1)S(1)}, bf16[8,32,64]{2,1,0:T(8,128)(2,1)S(1)}, u32[]{:S(2)}, u32[]{:S(2)}) collective-permute-start(bf16[8,32,64]{2,1,0:T(8,128)(2,1)S(1)} %reshape.179), channel_id=1, source_target_pairs={{0,62},{1,3},{2,0},{3,5},{4,2},{5,7},{6,4},{7,9},{8,6},{9,11},{10,... | collective-permute-start | bytes 98312 | tf_op jit(solution)/shard_map/ppermute | solution.py:80
  66.7 7.6 %collective-permute-start.8 = (bf16[8,32,64]{2,1,0:T(8,128)(2,1)S(1)}, bf16[8,32,64]{2,1,0:T(8,128)(2,1)S(1)}, u32[]{:S(2)}, u32[]{:S(2)}) collective-permute-start(bf16[8,32,64]{2,1,0:T(8,128)(2,1)S(1)} %reshape.179), channel_id=1, source_target_pairs={{0,2},{1,63},{2,4},{3,1},{4,6},{5,3},{6,8},{7,5},{8,10},{9,7},{10,... | collective-permute-start | bytes 98312 | tf_op jit(solution)/shard_map/ppermute | solution.py:81
  74.7 3.2 %collective-permute-start.9 = (bf16[8,64,64]{2,1,0:T(8,128)(2,1)S(1)}, bf16[8,64,64]{2,1,0:T(8,128)(2,1)S(1)}, u32[]{:S(2)}, u32[]{:S(2)}) collective-permute-start(bf16[8,64,64]{2,1,0:T(8,128)(2,1)S(1)} %pad_maximum_fusion.14), channel_id=1, source_target_pairs={{0,1},{1,0},{2,3},{3,2},{4,5},{5,4},{6,7},{7,6},{8,9},{9,8},{10,11... | collective-permute-start | bytes 196616 | tf_op jit(solution)/shard_map/ppermute | solution.py:21
  78.1 0.7 collective-permute-done.9
  79.5 1.6 %convolution_bitcast_fusion.5 = f32[8,16,64]{2,0,1:T(8,128)S(1)} fusion(bf16[8,16,4,64]{3,0,2,1:T(8,128)(2,1)S(1)} %bitcast.97, bf16[16,4,64,64]{3,2,1,0:T(8,128)(2,1)} %param.25), kind=kOutput, calls=%fused_computation.23 | convolution fusion | flops 4194304 | bytes 622592 | tf_op jit(solution)/shard_map/okij,fokj->foi/dot_general | solution.py:61
  81.2 0.6 fusion.5
  81.8 0.9 %copy.46 = f32[72,8,128]{2,1,0:T(8,128)} copy(f32[72,8,128]{0,2,1:T(8,128)S(1)} %fusion.5) | data formatting | bytes 589824
  (78 shorter events, 4.9 us)
Async XLA Ops:
  0.6 61.1 %copy-start = (bf16[32,4,64,64]{3,2,1,0:T(8,128)(2,1)S(1)}, bf16[32,4,64,64]{3,2,1,0:T(8,128)(2,1)}, u32[]{:S(2)}) copy-start(bf16[32,4,64,64]{3,2,1,0:T(8,128)(2,1)} %param.18) | copy-start | bytes 3145732
  0.6 21.7 %copy-start.8 = (s32[32,4]{0,1:T(4,128)S(1)}, s32[32,4]{0,1:T(4,128)}, u32[]{:S(2)}) copy-start(s32[32,4]{0,1:T(4,128)} %param.19) | copy-start | bytes 1540
  0.7 22.0 %copy-start.5 = (s32[2048]{0:T(1024)S(1)}, s32[2048]{0:T(1024)}, u32[]{:S(2)}) copy-start(s32[2048]{0:T(1024)} %param.23) | copy-start | bytes 24580
  0.7 22.0 %copy-start.9 = (s32[16,4]{0,1:T(4,128)S(1)}, s32[16,4]{0,1:T(4,128)}, u32[]{:S(2)}) copy-start(s32[16,4]{0,1:T(4,128)} %param.26) | copy-start | bytes 772
  0.7 22.2 %copy-start.2 = (f32[80,80]{1,0:T(8,128)S(1)}, f32[80,80]{1,0:T(8,128)}, u32[]{:S(2)}) copy-start(f32[80,80]{1,0:T(8,128)} %param.21) | copy-start | bytes 76804
  3.4 22.3 %collective-permute-start.1 = (f32[1168]{0:T(1024)S(1)}, f32[1168]{0:T(1024)S(1)}, u32[]{:S(2)}, u32[]{:S(2)}) collective-permute-start(f32[1168]{0:T(1024)S(1)} %select_n.186), channel_id=1, source_target_pairs={{0,1},{1,0},{2,3},{3,2},{4,5},{5,4},{6,7},{7,6},{8,9},{9,8},{10,11... | collective-permute-start | bytes 14024 | tf_op jit(solution)/shard_map/ppermute | solution.py:21
  19.9 5.8 %collective-permute-start = (f32[1168]{0:T(1024)S(1)}, f32[1168]{0:T(1024)S(1)}, u32[]{:S(2)}, u32[]{:S(2)}) collective-permute-start(f32[1168]{0:T(1024)S(1)} %select_n.184), channel_id=1, source_target_pairs={{0,63},{1,2},{2,1},{3,4},{4,3},{5,6},{6,5},{7,8},{8,7},{9,10},{10,... | collective-permute-start | bytes 14024 | tf_op jit(solution)/shard_map/ppermute | solution.py:21
  26.8 12.2 %copy-start.12 = (f32[72,72]{1,0:T(8,128)S(1)}, f32[72,72]{1,0:T(8,128)}, u32[]{:S(2)}) copy-start(f32[72,72]{1,0:T(8,128)} %param.16) | copy-start | bytes 62212
  26.8 9.1 %collective-permute-start.3 = (f32[73,2,132]{0,2,1:T(8,128)S(1)}, f32[73,2,132]{0,2,1:T(8,128)S(1)}, u32[]{:S(2)}, u32[]{:S(2)}) collective-permute-start(f32[73,2,132]{0,2,1:T(8,128)S(1)} %broadcast_select_fusion.2), channel_id=1, source_target_pairs={{0,64},{64,0},{128,192},{192,128},{256,320},{320,256},{384,448},{4... | collective-permute-start | bytes 231272 | tf_op jit(solution)/shard_map/ppermute | solution.py:21
  28.8 9.1 %collective-permute-start.2 = (f32[73,2,132]{0,2,1:T(8,128)S(1)}, f32[73,2,132]{0,2,1:T(8,128)S(1)}, u32[]{:S(2)}, u32[]{:S(2)}) collective-permute-start(f32[73,2,132]{0,2,1:T(8,128)S(1)} %get-tuple-element.6), channel_id=1, source_target_pairs={{0,960},{64,128},{128,64},{192,256},{256,192},{320,384},{384,320},... | collective-permute-start | bytes 231272 | tf_op jit(solution)/shard_map/ppermute | solution.py:21
  39.0 1.4 %copy-start.4 = (f32[24,72]{1,0:T(8,128)S(1)}, f32[24,72]{1,0:T(8,128)}, u32[]{:S(2)}) copy-start(f32[24,72]{1,0:T(8,128)} %param.17) | copy-start | bytes 20740
  39.9 15.2 %copy-start.10 = (s32[16]{0:T(128)S(1)}, s32[16]{0:T(128)}, u32[]{:S(2)}) copy-start(s32[16]{0:T(128)} %iota_add_fusion.5) | copy-start | bytes 196
  40.9 14.6 %collective-permute-start.4 = (bf16[24,16,64]{2,1,0:T(8,128)(2,1)S(1)}, bf16[24,16,64]{2,1,0:T(8,128)(2,1)S(1)}, u32[]{:S(2)}, u32[]{:S(2)}) collective-permute-start(bf16[24,16,64]{2,1,0:T(8,128)(2,1)S(1)} %reshape.176), channel_id=1, source_target_pairs={{0,62},{1,3},{2,0},{3,5},{4,2},{5,7},{6,4},{7,9},{8,6},{9,11},{10,... | collective-permute-start | bytes 147464 | tf_op jit(solution)/shard_map/ppermute | solution.py:80
  46.9 12.3 %collective-permute-start.5 = (bf16[24,16,64]{2,1,0:T(8,128)(2,1)S(1)}, bf16[24,16,64]{2,1,0:T(8,128)(2,1)S(1)}, u32[]{:S(2)}, u32[]{:S(2)}) collective-permute-start(bf16[24,16,64]{2,1,0:T(8,128)(2,1)S(1)} %reshape.176), channel_id=1, source_target_pairs={{0,2},{1,63},{2,4},{3,1},{4,6},{5,3},{6,8},{7,5},{8,10},{9,7},{10,... | collective-permute-start | bytes 147464 | tf_op jit(solution)/shard_map/ppermute | solution.py:81
  55.5 3.3 %collective-permute-start.6 = (bf16[24,32,64]{2,1,0:T(8,128)(2,1)S(1)}, bf16[24,32,64]{2,1,0:T(8,128)(2,1)S(1)}, u32[]{:S(2)}, u32[]{:S(2)}) collective-permute-start(bf16[24,32,64]{2,1,0:T(8,128)(2,1)S(1)} %pad_maximum_fusion.9), channel_id=1, source_target_pairs={{0,1},{1,0},{2,3},{3,2},{4,5},{5,4},{6,7},{7,6},{8,9},{9,8},{10,11... | collective-permute-start | bytes 294920 | tf_op jit(solution)/shard_map/ppermute | solution.py:21
  61.7 0.9 %copy-start.3 = (f32[80,24]{0,1:T(8,128)S(1)}, f32[80,24]{0,1:T(8,128)}, u32[]{:S(2)}) copy-start(f32[80,24]{0,1:T(8,128)} %param.22) | copy-start | bytes 23044
  62.4 2.0 %copy-start.6 = (f32[8,80]{1,0:T(8,128)S(1)}, f32[8,80]{1,0:T(8,128)}, u32[]{:S(2)}) copy-start(f32[8,80]{1,0:T(8,128)} %param.24) | copy-start | bytes 7684
  62.6 16.5 %copy-start.11 = (s32[32]{0:T(128)S(1)}, s32[32]{0:T(128)}, u32[]{:S(2)}) copy-start(s32[32]{0:T(128)} %iota_add_fusion) | copy-start | bytes 388
  64.4 16.7 %copy-start.1 = (f32[80,2048]{1,0:T(8,128)}, f32[80,2048]{1,0:T(8,128)S(1)}, u32[]{:S(2)}) copy-start(f32[80,2048]{1,0:T(8,128)S(1)} %fusion.1) | copy-start | bytes 1966084
  64.7 16.5 %copy-start.7 = (f32[72,8]{0,1:T(8,128)S(1)}, f32[72,8]{0,1:T(8,128)}, u32[]{:S(2)}) copy-start(f32[72,8]{0,1:T(8,128)} %param.27) | copy-start | bytes 6916
  64.8 9.8 %collective-permute-start.7 = (bf16[8,32,64]{2,1,0:T(8,128)(2,1)S(1)}, bf16[8,32,64]{2,1,0:T(8,128)(2,1)S(1)}, u32[]{:S(2)}, u32[]{:S(2)}) collective-permute-start(bf16[8,32,64]{2,1,0:T(8,128)(2,1)S(1)} %reshape.179), channel_id=1, source_target_pairs={{0,62},{1,3},{2,0},{3,5},{4,2},{5,7},{6,4},{7,9},{8,6},{9,11},{10,... | collective-permute-start | bytes 98312 | tf_op jit(solution)/shard_map/ppermute | solution.py:80
  66.7 12.3 %collective-permute-start.8 = (bf16[8,32,64]{2,1,0:T(8,128)(2,1)S(1)}, bf16[8,32,64]{2,1,0:T(8,128)(2,1)S(1)}, u32[]{:S(2)}, u32[]{:S(2)}) collective-permute-start(bf16[8,32,64]{2,1,0:T(8,128)(2,1)S(1)} %reshape.179), channel_id=1, source_target_pairs={{0,2},{1,63},{2,4},{3,1},{4,6},{5,3},{6,8},{7,5},{8,10},{9,7},{10,... | collective-permute-start | bytes 98312 | tf_op jit(solution)/shard_map/ppermute | solution.py:81
  74.7 4.2 %collective-permute-start.9 = (bf16[8,64,64]{2,1,0:T(8,128)(2,1)S(1)}, bf16[8,64,64]{2,1,0:T(8,128)(2,1)S(1)}, u32[]{:S(2)}, u32[]{:S(2)}) collective-permute-start(bf16[8,64,64]{2,1,0:T(8,128)(2,1)S(1)} %pad_maximum_fusion.14), channel_id=1, source_target_pairs={{0,1},{1,0},{2,3},{3,2},{4,5},{5,4},{6,7},{7,6},{8,9},{9,8},{10,11... | collective-permute-start | bytes 196616 | tf_op jit(solution)/shard_map/ppermute | solution.py:21

commit v10 on v9

--- a/solution.py
+++ b/solution.py
@@ -88,11 +88,16 @@
     slot = local // per_tile
     within = local % per_tile
     partner_local = jnp.where(slot == 3, plus_one + within, jnp.where(slot == 1, minus_one + within, -1))
-    picked = pick(local, 2 * per_tile, blocks, per_tile)
-    picked = picked + pick(local, first_base, forward, per_tile)
-    picked = picked + pick(local, second_base, other, per_tile)
-    picked = picked + pick(partner_local, 0, partner, 2 * per_tile)
-    return picked.astype(blocks.dtype).reshape((fields,) + cols.shape + (cells,))
+    early = pick(local, 2 * per_tile, blocks, per_tile)
+    early = early + pick(local, first_base, forward, per_tile)
+    early = early + pick(partner_local, 0, partner, 2 * per_tile)
+    shape = (fields,) + cols.shape + (cells,)
+    def finish(early_product):
+        later, early_product = lax.optimization_barrier((other, early_product))
+        late = pick(local, second_base, later, per_tile).astype(blocks.dtype).reshape(shape)
+        return early_product, late
+
+    return early.astype(blocks.dtype).reshape(shape), finish
 
 
 def body(
@@ -127,13 +132,17 @@
     mixed = lax.optimization_barrier(
         ocean_state + jnp.dot(ocean_mix, ocean_state, precision=lax.Precision.HIGHEST)
     )
-    remapped = block_product(remap_weight, exchange_and_pick(surface_blocks, remap_cols, here))
+    early, finish = exchange_and_pick(surface_blocks, remap_cols, here)
+    first_part, late = finish(block_product(remap_weight, early))
+    remapped = first_part + block_product(remap_weight, late)
     remapped = remapped.reshape(fields, ocean_blocks * 64)
     stepped = mixed + jnp.dot(forcing, remapped, precision=lax.Precision.HIGH)
     ocean_out = jnp.where(wet_mask[None] == 1, stepped, ocean_state)
     sea = jnp.dot(surface_proj, ocean_out, precision=lax.Precision.HIGH).astype(jnp.bfloat16)
     sea_blocks = sea.reshape(sea.shape[0], ocean_blocks, 64)
-    returned = block_product(back_weight, exchange_and_pick(sea_blocks, back_cols, here))
+    early, finish = exchange_and_pick(sea_blocks, back_cols, here)
+    first_part, late = finish(block_product(back_weight, early))
+    returned = first_part + block_product(back_weight, late)
     returned = returned.reshape(sea.shape[0], rows_here, cols_here)
     atm_out = atm_mid + level_mix(back_proj, returned)
     return (atm_out, ocean_out)

time: 83.3 us -> 87.3 us (1.048)
  local copies, waits for them, and re-layouts: 8.24 us -> 10.8 us
  matrix products: 12.3 us -> 14.2 us
  starting transfers between devices: 55.5 us -> 54.5 us
    unnamed x28 -> x32, local copies, waits for them, and re-layouts: 2.27 us -> 4.31 us
    dot_general x4, matrix products: 2.32 us -> 3.36 us  [level_mix(): jnp.einsum('ml,l...->m...', matrix, field, precision=lax.Precision.HIGH)]
    dot_general x8, matrix products: 2.97 us -> 3.89 us  [pick(): jnp.einsum('qb,fbj->fqj', onehot, piece, preferred_element_type=jnp.float32)]
    ppermute x6, starting transfers between devices: 31.7 us -> 30.8 us  [swap(): return lax.ppermute(value, axis, pairs)]
    convert_element_type x2 -> x4, local copies, waits for them, and re-layouts: 1.54 us -> 2.11 us  [the longest x2 1.54 us: finish(): pick(local, second_base, later, per_tile).astype(blocks.dtype)]
    dot_general x2 -> x4, matrix products: 2.22 us -> 1.99 us  [block_product(): jnp.einsum('okij,fokj->foi', weights, picked, preferred_element_type=jnp....]
  transfers between devices with their start and end apart: 10 -> 10, of which waited for: 3 -> 4; matrix products, arithmetic and copies ran while one was open for 8% -> 9% of each run, Pallas kernels for 0% -> 0%
where the time goes in v10:
time: 87.3 us; the launch traced here: 86.6 us
  starting transfers between devices  54.5 us (62%)
  matrix products  14.2 us (16%)
  local copies, waits for them, and re-layouts  10.8 us (12%)
  waiting for transfers between devices  4.05 us (5%)
  other arithmetic  1.82 us (2%)
  between operations  1.22 us (1%)
    ppermute x6, starting transfers between devices, swap(): return lax.ppermute(value, axis, pairs)  30.8 us
    ppermute x2, starting transfers between devices, exchange_and_pick(): lax.ppermute(blocks, 'tile', [(s, (s + 2 if s % 2 == 0 else s - 2) % tile...  15.9 us
    ppermute x2, starting transfers between devices, exchange_and_pick(): lax.ppermute(blocks, 'tile', [(s, (s - 2 if s % 2 == 0 else s + 2) % tile...  7.87 us
    unnamed x32, local copies, waits for them, and re-layouts  4.31 us
    dot_general x8, matrix products, pick(): jnp.einsum('qb,fbj->fqj', onehot, piece, preferred_element_type=jnp.float32)  3.89 us
    ppermute x6, waiting for transfers between devices, swap(): return lax.ppermute(value, axis, pairs)  3.69 us
    dot_general x4, matrix products, level_mix(): jnp.einsum('ml,l...->m...', matrix, field, precision=lax.Precision.HIGH)  3.36 us
    dot_general x1, matrix products, body(): jnp.dot(ocean_mix, ocean_state, precision=lax.Precision.HIGHEST)  2.79 us
  transfers between devices with their start and end apart: 10, of which 4 were waited for; matrix products, arithmetic and copies ran while one was open for 9% of the time, Pallas kernels for 0%

profile of v10, /device:TPU:1, one launch (start us, length us, event | category | flops | bytes accessed | tf_op | source)
XLA Modules:
  0.0 86.6 jit_solution(4607823996658031270)
XLA Ops:
  0.7 1.3 %copy.29 = f32[72,8,128]{0,2,1:T(8,128)S(1)} copy(f32[72,8,128]{2,1,0:T(8,128)} %param.14) | data formatting | bytes 589824 | tf_op args[0]
  2.0 0.9 %copy.30 = f32[1,8,128]{0,2,1:T(8,128)S(1)} copy(f32[1,8,128]{2,1,0:T(8,128)} %bitcast.123) | data formatting | bytes 8192 | tf_op jit(solution)/shard_map/broadcast_in_dim | solution.py:120
  3.5 16.1 %collective-permute-start.1 = (f32[1168]{0:T(1024)S(1)}, f32[1168]{0:T(1024)S(1)}, u32[]{:S(2)}, u32[]{:S(2)}) collective-permute-start(f32[1168]{0:T(1024)S(1)} %select_n.186), channel_id=1, source_target_pairs={{0,1},{1,0},{2,3},{3,2},{4,5},{5,4},{6,7},{7,6},{8,9},{9,8},{10,11... | collective-permute-start | bytes 14024 | tf_op jit(solution)/shard_map/ppermute | solution.py:21
  19.9 1.9 %collective-permute-start = (f32[1168]{0:T(1024)S(1)}, f32[1168]{0:T(1024)S(1)}, u32[]{:S(2)}, u32[]{:S(2)}) collective-permute-start(f32[1168]{0:T(1024)S(1)} %select_n.184), channel_id=1, source_target_pairs={{0,63},{1,2},{2,1},{3,4},{4,3},{5,6},{6,5},{7,8},{8,7},{9,10},{10,... | collective-permute-start | bytes 14024 | tf_op jit(solution)/shard_map/ppermute | solution.py:21
  22.1 0.5 iota_add_fusion.3
  22.9 2.8 %convolution_add_fusion = f32[80,2048]{1,0:T(8,128)} fusion(f32[80,2048]{1,0:T(8,128)} %param.20, f32[80,80]{1,0:T(8,128)S(1)} %copy-done.4), kind=kOutput, calls=%fused_computation | convolution fusion | flops 157450240 | bytes 1336320 | tf_op jit(solution)/shard_map/dot_general | solution.py:133
  26.9 1.9 %collective-permute-start.3 = (f32[73,2,132]{0,2,1:T(8,128)S(1)}, f32[73,2,132]{0,2,1:T(8,128)S(1)}, u32[]{:S(2)}, u32[]{:S(2)}) collective-permute-start(f32[73,2,132]{0,2,1:T(8,128)S(1)} %broadcast_select_fusion.2), channel_id=1, source_target_pairs={{0,64},{64,0},{128,192},{192,128},{256,320},{320,256},{384,448},{4... | collective-permute-start | bytes 231272 | tf_op jit(solution)/shard_map/ppermute | solution.py:21
  28.8 6.7 %collective-permute-start.2 = (f32[73,2,132]{0,2,1:T(8,128)S(1)}, f32[73,2,132]{0,2,1:T(8,128)S(1)}, u32[]{:S(2)}, u32[]{:S(2)}) collective-permute-start(f32[73,2,132]{0,2,1:T(8,128)S(1)} %get-tuple-element.14), channel_id=1, source_target_pairs={{0,960},{64,128},{128,64},{192,256},{256,192},{320,384},{384,320},... | collective-permute-start | bytes 231272 | tf_op jit(solution)/shard_map/ppermute | solution.py:21
  35.4 0.5 iota_add_fusion
  36.0 1.9 %collective-permute-done.2 = f32[73,2,132]{0,2,1:T(8,128)S(1)} collective-permute-done((f32[73,2,132]{0,2,1:T(8,128)S(1)}, f32[73,2,132]{0,2,1:T(8,128)S(1)}, u32[]{:S(2)}, u32[]{:S(2)}) %collective-permute-start.2) | collective-permute-done | bytes 77120 | tf_op jit(solution)/shard_map/ppermute | solution.py:21
  38.1 0.7 slice_reduce_fusion
  39.0 0.9 %fusion.15 = f32[72,10,130]{0,2,1:T(8,128)S(1)} fusion(f32[73,12,132]{0,2,1:T(8,128)S(1)} %pad_maximum_fusion, f32[73,2,132]{0,2,1:T(8,128)S(1)} %get-tuple-element.20, f32[73,8,2]{0,2,1:T(2,128)S(1)} %copy.34, f32[73,8,2]{0,2,1:T(2,128)S(1)} %copy.33, f32[1,8,128]{0,2,1:T(8,128)S(1)} %copy.30, f32[72,8,128]{0,2,1:T(8,128)S(1)} %copy.29, ...), kind=kOutput, calls=%fused_computation.35 | convolution fusion | flops 41932800 | bytes 4556416 | tf_op jit(solution)/shard_map/ml,l...->m.../dot_general | solution.py:49
  39.9 0.5 fusion.5
  40.4 0.8 copy-done.3
  41.7 6.0 %collective-permute-start.5 = (bf16[24,16,64]{2,1,0:T(8,128)(2,1)S(1)}, bf16[24,16,64]{2,1,0:T(8,128)(2,1)S(1)}, u32[]{:S(2)}, u32[]{:S(2)}) collective-permute-start(bf16[24,16,64]{2,1,0:T(8,128)(2,1)S(1)} %reshape.182), channel_id=1, source_target_pairs={{0,62},{1,3},{2,0},{3,5},{4,2},{5,7},{6,4},{7,9},{8,6},{9,11},{10,... | collective-permute-start | bytes 147464 | tf_op jit(solution)/shard_map/ppermute | solution.py:80
  47.6 8.3 %collective-permute-start.4 = (bf16[24,16,64]{2,1,0:T(8,128)(2,1)S(1)}, bf16[24,16,64]{2,1,0:T(8,128)(2,1)S(1)}, u32[]{:S(2)}, u32[]{:S(2)}) collective-permute-start(bf16[24,16,64]{2,1,0:T(8,128)(2,1)S(1)} %reshape.182), channel_id=1, source_target_pairs={{0,2},{1,63},{2,4},{3,1},{4,6},{5,3},{6,8},{7,5},{8,10},{9,7},{10,... | collective-permute-start | bytes 147464 | tf_op jit(solution)/shard_map/ppermute | solution.py:81
  56.7 1.9 %collective-permute-start.6 = (bf16[24,32,64]{2,1,0:T(8,128)(2,1)S(1)}, bf16[24,32,64]{2,1,0:T(8,128)(2,1)S(1)}, u32[]{:S(2)}, u32[]{:S(2)}) collective-permute-start(bf16[24,32,64]{2,1,0:T(8,128)(2,1)S(1)} %pad_maximum_fusion.9), channel_id=1, source_target_pairs={{0,1},{1,0},{2,3},{3,2},{4,5},{5,4},{6,7},{7,6},{8,9},{9,8},{10,11... | collective-permute-start | bytes 294920 | tf_op jit(solution)/shard_map/ppermute | solution.py:21
  58.9 1.1 %collective-permute-done.6 = bf16[24,32,64]{2,1,0:T(8,128)(2,1)S(1)} collective-permute-done((bf16[24,32,64]{2,1,0:T(8,128)(2,1)S(1)}, bf16[24,32,64]{2,1,0:T(8,128)(2,1)S(1)}, u32[]{:S(2)}, u32[]{:S(2)}) %collective-permute-start.6) | collective-permute-done | bytes 98336 | tf_op jit(solution)/shard_map/ppermute | solution.py:21
  60.3 0.4 copy.40
  60.8 0.6 convolution_bitcast_fusion.5
  61.4 1.1 %fusion.6 = bf16[24,128,64]{1,2,0:T(8,128)(2,1)} fusion(bf16[24,16,64]{2,1,0:T(8,128)(2,1)S(1)} %collective-permute-done.4, s32[128]{0:T(128)S(1)} %eq.170, s32[16]{0:T(128)S(1)} %copy-done.13), kind=kOutput, calls=%fused_computation.15 | convolution fusion | flops 6490112 | bytes 442944 | tf_op jit(solution)/shard_map/qb,fbj->fqj/dot_general | solution.py:72
  62.5 1.4 %copy.41 = bf16[24,128,64]{2,0,1:T(8,128)(2,1)S(1)} copy(bf16[24,128,64]{1,2,0:T(8,128)(2,1)} %fusion.6) | data formatting | bytes 786432 | tf_op jit(solution)/shard_map/convert_element_type | solution.py:97
  63.9 0.6 convolution_bitcast_fusion.4
  65.3 1.9 %fusion.1 = f32[80,2048]{1,0:T(8,128)S(1)} fusion(f32[80,2048]{1,0:T(8,128)} %param.20, f32[80,2048]{1,0:T(8,128)} %convolution_add_fusion, f32[24,2048]{1,0:T(8,128)S(1)} %reshape.185, f32[80,24]{0,1:T(8,128)S(1)} %copy-done.5, pred[2048]{0:T(1024)(128)(4,1)S(1)} %broadcast_compare_fusion), kind=kOutput, calls=%fused_computation.3 | convolution fusion | flops 23920640 | bytes 2172416 | tf_op jit(solution)/shard_map/dot_general | solution.py:139
  67.2 0.8 copy-done.2
  68.4 1.9 %collective-permute-start.8 = (bf16[8,32,64]{2,1,0:T(8,128)(2,1)S(1)}, bf16[8,32,64]{2,1,0:T(8,128)(2,1)S(1)}, u32[]{:S(2)}, u32[]{:S(2)}) collective-permute-start(bf16[8,32,64]{2,1,0:T(8,128)(2,1)S(1)} %reshape.186), channel_id=1, source_target_pairs={{0,62},{1,3},{2,0},{3,5},{4,2},{5,7},{6,4},{7,9},{8,6},{9,11},{10,... | collective-permute-start | bytes 98312 | tf_op jit(solution)/shard_map/ppermute | solution.py:80
  70.4 7.6 %collective-permute-start.7 = (bf16[8,32,64]{2,1,0:T(8,128)(2,1)S(1)}, bf16[8,32,64]{2,1,0:T(8,128)(2,1)}, u32[]{:S(2)}, u32[]{:S(2)}) collective-permute-start(bf16[8,32,64]{2,1,0:T(8,128)(2,1)S(1)} %reshape.186), channel_id=1, source_target_pairs={{0,2},{1,63},{2,4},{3,1},{4,6},{5,3},{6,8},{7,5},{8,10},{9,7},{10,... | collective-permute-start | bytes 98312 | tf_op jit(solution)/shard_map/ppermute | solution.py:81
  78.2 2.3 %collective-permute-start.9 = (bf16[8,64,64]{2,1,0:T(8,128)(2,1)S(1)}, bf16[8,64,64]{2,1,0:T(8,128)(2,1)S(1)}, u32[]{:S(2)}, u32[]{:S(2)}) collective-permute-start(bf16[8,64,64]{2,1,0:T(8,128)(2,1)S(1)} %pad_maximum_fusion.14), channel_id=1, source_target_pairs={{0,1},{1,0},{2,3},{3,2},{4,5},{5,4},{6,7},{7,6},{8,9},{9,8},{10,11... | collective-permute-start | bytes 196616 | tf_op jit(solution)/shard_map/ppermute | solution.py:21
  80.8 0.7 collective-permute-done.9
  82.3 1.1 %fusion.10 = bf16[8,64,64]{1,2,0:T(8,128)(2,1)S(1)} fusion(bf16[8,32,64]{2,1,0:T(8,128)(2,1)} %collective-permute-done.7, s32[64]{0:T(128)S(1)} %eq.184, s32[32]{0:T(128)S(1)} %copy-done.12), kind=kOutput, calls=%fused_computation.24 | convolution fusion | flops 2131968 | bytes 98688 | tf_op jit(solution)/shard_map/qb,fbj->fqj/dot_general | solution.py:72
  84.0 1.6 %fusion.4 = f32[72,8,128]{0,2,1:T(8,128)S(1)} fusion(f32[72,8,128]{0,2,1:T(8,128)} %copy-done.3, f32[8,8,128]{2,1,0:T(8,128)S(1)} %reshape.189, f32[72,8]{0,1:T(8,128)S(1)} %copy-done.9), kind=kOutput, calls=%fused_computation.12 | convolution fusion | flops 3612672 | bytes 624896 | tf_op jit(solution)/shard_map/ml,l...->m.../dot_general | solution.py:49
  85.7 0.9 %copy.50 = f32[72,8,128]{2,1,0:T(8,128)} copy(f32[72,8,128]{0,2,1:T(8,128)S(1)} %fusion.4) | data formatting | bytes 589824
  (88 shorter events, 7.6 us)
Async XLA Ops:
  0.6 60.1 %copy-start = (bf16[32,4,64,64]{3,2,1,0:T(8,128)(2,1)S(1)}, bf16[32,4,64,64]{3,2,1,0:T(8,128)(2,1)}, u32[]{:S(2)}) copy-start(bf16[32,4,64,64]{3,2,1,0:T(8,128)(2,1)} %param.18) | copy-start | bytes 3145732
  0.6 21.3 %copy-start.10 = (s32[32,4]{0,1:T(4,128)S(1)}, s32[32,4]{0,1:T(4,128)}, u32[]{:S(2)}) copy-start(s32[32,4]{0,1:T(4,128)} %param.19) | copy-start | bytes 1540
  0.7 22.0 %copy-start.7 = (s32[2048]{0:T(1024)S(1)}, s32[2048]{0:T(1024)}, u32[]{:S(2)}) copy-start(s32[2048]{0:T(1024)} %param.23) | copy-start | bytes 24580
  0.7 22.0 %copy-start.11 = (s32[16,4]{0,1:T(4,128)S(1)}, s32[16,4]{0,1:T(4,128)}, u32[]{:S(2)}) copy-start(s32[16,4]{0,1:T(4,128)} %param.26) | copy-start | bytes 772
  0.7 22.2 %copy-start.4 = (f32[80,80]{1,0:T(8,128)S(1)}, f32[80,80]{1,0:T(8,128)}, u32[]{:S(2)}) copy-start(f32[80,80]{1,0:T(8,128)} %param.21) | copy-start | bytes 76804
  3.5 22.3 %collective-permute-start.1 = (f32[1168]{0:T(1024)S(1)}, f32[1168]{0:T(1024)S(1)}, u32[]{:S(2)}, u32[]{:S(2)}) collective-permute-start(f32[1168]{0:T(1024)S(1)} %select_n.186), channel_id=1, source_target_pairs={{0,1},{1,0},{2,3},{3,2},{4,5},{5,4},{6,7},{7,6},{8,9},{9,8},{10,11... | collective-permute-start | bytes 14024 | tf_op jit(solution)/shard_map/ppermute | solution.py:21
  19.9 5.8 %collective-permute-start = (f32[1168]{0:T(1024)S(1)}, f32[1168]{0:T(1024)S(1)}, u32[]{:S(2)}, u32[]{:S(2)}) collective-permute-start(f32[1168]{0:T(1024)S(1)} %select_n.184), channel_id=1, source_target_pairs={{0,63},{1,2},{2,1},{3,4},{4,3},{5,6},{6,5},{7,8},{8,7},{9,10},{10,... | collective-permute-start | bytes 14024 | tf_op jit(solution)/shard_map/ppermute | solution.py:21
  26.8 12.2 %copy-start.14 = (f32[72,72]{1,0:T(8,128)S(1)}, f32[72,72]{1,0:T(8,128)}, u32[]{:S(2)}) copy-start(f32[72,72]{1,0:T(8,128)} %param.16) | copy-start | bytes 62212
  26.9 9.1 %collective-permute-start.3 = (f32[73,2,132]{0,2,1:T(8,128)S(1)}, f32[73,2,132]{0,2,1:T(8,128)S(1)}, u32[]{:S(2)}, u32[]{:S(2)}) collective-permute-start(f32[73,2,132]{0,2,1:T(8,128)S(1)} %broadcast_select_fusion.2), channel_id=1, source_target_pairs={{0,64},{64,0},{128,192},{192,128},{256,320},{320,256},{384,448},{4... | collective-permute-start | bytes 231272 | tf_op jit(solution)/shard_map/ppermute | solution.py:21
  28.8 9.1 %collective-permute-start.2 = (f32[73,2,132]{0,2,1:T(8,128)S(1)}, f32[73,2,132]{0,2,1:T(8,128)S(1)}, u32[]{:S(2)}, u32[]{:S(2)}) collective-permute-start(f32[73,2,132]{0,2,1:T(8,128)S(1)} %get-tuple-element.14), channel_id=1, source_target_pairs={{0,960},{64,128},{128,64},{192,256},{256,192},{320,384},{384,320},... | collective-permute-start | bytes 231272 | tf_op jit(solution)/shard_map/ppermute | solution.py:21
  39.0 2.2 %copy-start.6 = (f32[24,72]{1,0:T(8,128)S(1)}, f32[24,72]{1,0:T(8,128)}, u32[]{:S(2)}) copy-start(f32[24,72]{1,0:T(8,128)} %param.17) | copy-start | bytes 20740
  40.4 0.8 copy-start.3
  41.7 14.9 %collective-permute-start.5 = (bf16[24,16,64]{2,1,0:T(8,128)(2,1)S(1)}, bf16[24,16,64]{2,1,0:T(8,128)(2,1)S(1)}, u32[]{:S(2)}, u32[]{:S(2)}) collective-permute-start(bf16[24,16,64]{2,1,0:T(8,128)(2,1)S(1)} %reshape.182), channel_id=1, source_target_pairs={{0,62},{1,3},{2,0},{3,5},{4,2},{5,7},{6,4},{7,9},{8,6},{9,11},{10,... | collective-permute-start | bytes 147464 | tf_op jit(solution)/shard_map/ppermute | solution.py:80
  47.6 13.8 %collective-permute-start.4 = (bf16[24,16,64]{2,1,0:T(8,128)(2,1)S(1)}, bf16[24,16,64]{2,1,0:T(8,128)(2,1)S(1)}, u32[]{:S(2)}, u32[]{:S(2)}) collective-permute-start(bf16[24,16,64]{2,1,0:T(8,128)(2,1)S(1)} %reshape.182), channel_id=1, source_target_pairs={{0,2},{1,63},{2,4},{3,1},{4,6},{5,3},{6,8},{7,5},{8,10},{9,7},{10,... | collective-permute-start | bytes 147464 | tf_op jit(solution)/shard_map/ppermute | solution.py:81
  56.7 3.3 %collective-permute-start.6 = (bf16[24,32,64]{2,1,0:T(8,128)(2,1)S(1)}, bf16[24,32,64]{2,1,0:T(8,128)(2,1)S(1)}, u32[]{:S(2)}, u32[]{:S(2)}) collective-permute-start(bf16[24,32,64]{2,1,0:T(8,128)(2,1)S(1)} %pad_maximum_fusion.9), channel_id=1, source_target_pairs={{0,1},{1,0},{2,3},{3,2},{4,5},{5,4},{6,7},{7,6},{8,9},{9,8},{10,11... | collective-permute-start | bytes 294920 | tf_op jit(solution)/shard_map/ppermute | solution.py:21
  60.3 1.1 %copy-start.13 = (s32[16]{0:T(128)S(1)}, s32[16]{0:T(128)}, u32[]{:S(2)}) copy-start(s32[16]{0:T(128)} %iota_add_fusion.3) | copy-start | bytes 196
  64.6 0.7 copy-start.5
  64.6 3.4 %copy-start.8 = (f32[8,80]{1,0:T(8,128)S(1)}, f32[8,80]{1,0:T(8,128)}, u32[]{:S(2)}) copy-start(f32[8,80]{1,0:T(8,128)} %param.24) | copy-start | bytes 7684
  65.3 16.6 %copy-start.1 = (bf16[16,4,64,64]{3,2,1,0:T(8,128)(2,1)S(1)}, bf16[16,4,64,64]{3,2,1,0:T(8,128)(2,1)}, u32[]{:S(2)}) copy-start(bf16[16,4,64,64]{3,2,1,0:T(8,128)(2,1)} %param.25) | copy-start | bytes 1572868
  67.2 0.8 copy-start.2
  68.0 14.3 %copy-start.12 = (s32[32]{0:T(128)S(1)}, s32[32]{0:T(128)}, u32[]{:S(2)}) copy-start(s32[32]{0:T(128)} %iota_add_fusion) | copy-start | bytes 388
  68.4 9.8 %collective-permute-start.8 = (bf16[8,32,64]{2,1,0:T(8,128)(2,1)S(1)}, bf16[8,32,64]{2,1,0:T(8,128)(2,1)S(1)}, u32[]{:S(2)}, u32[]{:S(2)}) collective-permute-start(bf16[8,32,64]{2,1,0:T(8,128)(2,1)S(1)} %reshape.186), channel_id=1, source_target_pairs={{0,62},{1,3},{2,0},{3,5},{4,2},{5,7},{6,4},{7,9},{8,6},{9,11},{10,... | collective-permute-start | bytes 98312 | tf_op jit(solution)/shard_map/ppermute | solution.py:80
  70.4 11.9 %collective-permute-start.7 = (bf16[8,32,64]{2,1,0:T(8,128)(2,1)S(1)}, bf16[8,32,64]{2,1,0:T(8,128)(2,1)}, u32[]{:S(2)}, u32[]{:S(2)}) collective-permute-start(bf16[8,32,64]{2,1,0:T(8,128)(2,1)S(1)} %reshape.186), channel_id=1, source_target_pairs={{0,2},{1,63},{2,4},{3,1},{4,6},{5,3},{6,8},{7,5},{8,10},{9,7},{10,... | collective-permute-start | bytes 98312 | tf_op jit(solution)/shard_map/ppermute | solution.py:81
  78.2 3.3 %collective-permute-start.9 = (bf16[8,64,64]{2,1,0:T(8,128)(2,1)S(1)}, bf16[8,64,64]{2,1,0:T(8,128)(2,1)S(1)}, u32[]{:S(2)}, u32[]{:S(2)}) collective-permute-start(bf16[8,64,64]{2,1,0:T(8,128)(2,1)S(1)} %pad_maximum_fusion.14), channel_id=1, source_target_pairs={{0,1},{1,0},{2,3},{3,2},{4,5},{5,4},{6,7},{7,6},{8,9},{9,8},{10,11... | collective-permute-start | bytes 196616 | tf_op jit(solution)/shard_map/ppermute | solution.py:21
  80.8 3.2 %copy-start.9 = (f32[72,8]{0,1:T(8,128)S(1)}, f32[72,8]{0,1:T(8,128)}, u32[]{:S(2)}) copy-start(f32[72,8]{0,1:T(8,128)} %param.27) | copy-start | bytes 6916
